TPU v7x, 256 devices: a whole 4x4x8 slice. The times are simulated.
256 devices in a mesh: dp: 4 (over x_lo, core), expert: 64 (over z, y, x_hi).
Axes of the slice: x: 4 (x_hi: 2, x_lo: 2; x = x_hi * 2 + x_lo), y: 4, z: 8, core: 2. Of those that a mesh axis runs over, the one named last changes fastest.
Arguments:
- tokens: bfloat16 [65536, 3584], P(('dp', 'expert')), may hold values from -6 to 6
- cotangent: bfloat16 [65536, 3584], P(('dp', 'expert')), may hold values from -0.59765625 to 0.59765625
- expert_ids: int32 [65536, 1], P(('dp', 'expert')), may hold values from 0 to 63; in each aligned block of 256 rows (0 to 255, 256 to 511, ...) at most 6 rows name the same one
- gates: float32 [65536, 1], P(('dp', 'expert')), may hold values from 0.2 to 1
- pair_flags: int32 [64], replicated, may hold values from 0 to 1, as said below
- w_in: bfloat16 [64, 3584, 1024], P('expert', None, 'dp'), may hold values from -0.09375 to 0.09375
- w_out: bfloat16 [64, 1024, 3584], P('expert', 'dp'), may hold values from -0.1875 to 0.1875
Outputs:
- mixed: bfloat16 [65536, 3584], P(('dp', 'expert'))
- grad_in: bfloat16 [64, 3584, 1024], P('expert', None, 'dp')
- grad_out: bfloat16 [64, 1024, 3584], P('expert', 'dp')
Inputs may be any that keep to these rules, and one draw needn't show every extreme that they name: `expert_ids`: among the 256 tokens of one device, no expert is named by more than 6 routes; some expert is named exactly 6 times. pair_flags[j] equals pair_flags[j XOR (32)].
All inputs are finite; a program needn't handle non-finite values.
Results may differ from a plain program's by a relative error of at most 0.015.
Values may be sent and summed in bfloat16 or wider, within the bound.
No kernel may reach another device: no remote copies, remote signals or barrier semaphores. Data moves between devices by JAX's collectives and lax.ppermute only.
A program may use at most 192 MiB of HBM per device.

v0:
```python
import jax
import jax.numpy as jnp
from jax import lax
from jax.sharding import PartitionSpec as P


def partner_2(block, axis, distance):
    count = lax.axis_size(axis)
    route = []
    for low in range(count):
        high = low | 1 << distance
        if high != low and high < count:
            route += [(low, high), (high, low)]
    return lax.ppermute(block, axis, route)


def body(tokens, cotangent, expert_ids, gates, pair_flags, w_in, w_out):
    expert_count = lax.axis_size("expert")
    own_index = lax.axis_index("expert")
    half_axis = expert_count // 2
    pair_bit = half_axis.bit_length() - 1
    local_tokens, top_count = expert_ids.shape
    width = tokens.shape[1]
    capacity = max(2, 3 * local_tokens * top_count // (2 * expert_count))
    route_count = local_tokens * top_count
    lanes = jnp.arange(expert_count, dtype=jnp.int32)
    partner = jnp.bitwise_xor(lanes, half_axis * pair_flags)
    flagged = pair_flags[own_index] == 1
    quarter_in = w_in[0]
    quarter_out = w_out[0]
    their_in, their_out = partner_2((quarter_in, quarter_out), "expert", pair_bit)
    quarter_in = jnp.where(flagged, their_in, quarter_in)
    quarter_out = jnp.where(flagged, their_out, quarter_out)
    flat_ids = expert_ids.reshape(-1)
    target_of = partner[flat_ids]
    onehot = (target_of[:, None] == lanes[None, :]).astype(jnp.int32)
    position = jnp.sum(jnp.cumsum(onehot, axis=0) * onehot, axis=1) - 1
    slot_of = target_of * capacity + position
    route_index = jnp.arange(route_count, dtype=jnp.int32)
    slot_source = (
        jnp.full((expert_count * capacity,), route_count, jnp.int32).at[slot_of].set(route_index)
    )
    filled = slot_source < route_count
    token_row = jnp.minimum(slot_source // top_count, local_tokens - 1)
    slot_gate = gates.reshape(-1)[jnp.minimum(slot_source, route_count - 1)]
    send_rows = jnp.where(filled[:, None], tokens[token_row], jnp.zeros((), jnp.bfloat16))
    send_rows = send_rows.reshape(expert_count, capacity, width)
    send_grads = jnp.where(
        filled[:, None], slot_gate[:, None] * cotangent[token_row].astype(jnp.float32), 0.0
    )
    send_grads = send_grads.astype(jnp.bfloat16).reshape(expert_count, capacity, width)
    recv_rows, recv_grads = (
        lax.all_to_all(send_rows, "expert", split_axis=0, concat_axis=0, tiled=True),
        lax.all_to_all(send_grads, "expert", split_axis=0, concat_axis=0, tiled=True),
    )
    contract_last = (((1,), (1,)), ((), ()))
    contract_first = (((0,), (0,)), ((), ()))
    whole_in, whole_out = (
        lax.all_gather(quarter_in, "dp", axis=1, tiled=True),
        lax.all_gather(quarter_out, "dp", axis=0, tiled=True),
    )
    row_block = recv_rows.reshape(-1, width)
    grad_block = recv_grads.reshape(-1, width)
    pre = jnp.dot(row_block, whole_in, preferred_element_type=jnp.float32)
    sig = jax.nn.sigmoid(pre)
    hidden = (pre * sig).astype(jnp.bfloat16)
    expert_out = jnp.dot(hidden, whole_out, preferred_element_type=jnp.float32).astype(jnp.bfloat16)
    dhid = lax.dot_general(grad_block, whole_out, contract_last, preferred_element_type=jnp.float32)
    dpre = (dhid * sig * (1.0 + pre * (1.0 - sig))).astype(jnp.bfloat16)
    term_in = lax.dot_general(row_block, dpre, contract_first, preferred_element_type=jnp.float32)
    term_out = lax.dot_general(
        hidden, grad_block, contract_first, preferred_element_type=jnp.float32
    )
    share_in, share_out = (
        lax.psum_scatter(
            term_in.astype(jnp.bfloat16), "dp", scatter_dimension=1, tiled=True
        ).astype(jnp.float32),
        lax.psum_scatter(
            term_out.astype(jnp.bfloat16), "dp", scatter_dimension=0, tiled=True
        ).astype(jnp.float32),
    )
    grad_quarter_in = share_in.astype(jnp.bfloat16)
    grad_quarter_out = share_out.astype(jnp.bfloat16)
    expert_out = expert_out.reshape(expert_count, capacity, width)
    returned = lax.all_to_all(expert_out, "expert", split_axis=0, concat_axis=0, tiled=True)
    route_out = returned.reshape(-1, width)[slot_of]
    weighted = gates.reshape(local_tokens, top_count, 1) * route_out.reshape(
        local_tokens, top_count, width
    ).astype(jnp.float32)
    mixed = jnp.sum(weighted, axis=1).astype(jnp.bfloat16)
    return (mixed, grad_quarter_in[None], grad_quarter_out[None])


def solution(mesh):
    placed = (
        P(("dp", "expert"), None),
        P(("dp", "expert"), None),
        P(("dp", "expert"), None),
        P(("dp", "expert"), None),
        P(),
        P("expert", None, "dp"),
        P("expert", "dp", None),
    )
    return jax.shard_map(
        body,
        mesh=mesh,
        in_specs=placed,
        out_specs=(P(("dp", "expert"), None), P("expert", None, "dp"), P("expert", "dp", None)),
        check_vma=False,
    )
```

profile of v0, /device:TPU:192, one launch (start us, length us, event | category | flops | bytes accessed | tf_op | source)
XLA Modules:
  0.0 568.0 jit_solution(1413525591571189585)
XLA Ops:
  7.2 0.0 copy-start
  7.2 0.0 all-gather.3.cloned.1.call-start
  7.2 0.6 collective-permute-start
  7.9 1.2 dynamic_slice.3
  9.7 82.6 %collective-permute-done = bf16[3584,256]{1,0:T(8,128)(2,1)} collective-permute-done((bf16[3584,256]{1,0:T(8,128)(2,1)}, bf16[3584,256]{1,0:T(8,128)(2,1)}, u32[]{:S(2)}, u32[]{:S(2)}) %collective-permute-start) | collective-permute-done | bytes 1835040 | tf_op jit(solution)/shard_map/ppermute | solution.py:14
  92.3 0.0 copy-start.5
  92.3 0.0 copy-start.6
  92.3 2.9 broadcast_select_fusion.2
  95.3 0.0 copy-start.2
  95.3 0.0 all-gather.3.cloned.1.call-update
  95.3 1.2 collective-permute-start.1
  96.5 0.0 copy-done.5
  96.5 0.0 copy-done.6
  96.5 1.9 gather_fusion
  98.4 0.6 reduce-window.6
  99.0 0.2 slice_reduce_fusion
  99.3 0.1 fusion.1
  99.4 1.4 scatter_custom_fusion
  100.8 0.0 copy-done.2
  100.9 2.8 gather_fusion.3
  103.7 0.1 mul.68
  103.8 0.0 copy-done
  103.8 3.9 gather_fusion.4
  107.7 6.0 %reshape.111 = f32[64,6,3584]{2,1,0:T(8,128)} reshape(bf16[384,3584]{1,0:T(8,128)(2,1)} %gather_fusion.4) | data formatting | bytes 8257536 | tf_op jit(solution)/shard_map/convert_element_type | solution.py:49
  113.7 0.1 broadcast_in_dim.43
  113.8 6.5 %select_convert_fusion = bf16[64,6,3584]{2,1,0:T(8,128)(2,1)} fusion(f32[64,6,3584]{2,1,0:T(8,128)} %reshape.111, f32[64,6]{1,0:T(8,128)S(1)} %mul.68, pred[64,6]{1,0:T(8,128)(4,1)S(1)} %broadcast_in_dim.43), kind=kLoop, calls=%fused_computation.8 | loop fusion | flops 4128768 | bytes 8259456 | tf_op jit(solution)/shard_map/convert_element_type | solution.py:51
  120.3 13.0 %all-to-all-start.2 = ((bf16[64,6,3584]{2,1,0:T(8,128)(2,1)}), bf16[64,6,3584]{2,1,0:T(8,128)(2,1)}, u32[]{:S(2)}, u32[]{:S(2)}) async-start(bf16[64,6,3584]{2,1,0:T(8,128)(2,1)} %select_convert_fusion), calls=%async_computation.2 | async-start | bytes 7340032 | tf_op jit(solution)/shard_map/all_to_all | solution.py:54
  133.4 0.0 copy-start.3
  133.4 0.0 all-gather.5.cloned.1.call-start
  133.4 40.1 %collective-permute-done.1 = bf16[256,3584]{1,0:T(8,128)(2,1)} collective-permute-done((bf16[256,3584]{1,0:T(8,128)(2,1)}, bf16[256,3584]{1,0:T(8,128)(2,1)}, u32[]{:S(2)}, u32[]{:S(2)}) %collective-permute-start.1) | collective-permute-done | bytes 1835040 | tf_op jit(solution)/shard_map/ppermute | solution.py:14
  173.5 2.9 broadcast_select_fusion.1
  176.4 0.0 all-gather.5.cloned.1.call-update
  176.4 0.0 copy-done.3
  176.4 3.9 gather_fusion.1
  180.3 5.4 gather.19
  185.7 4.3 broadcast_select_fusion
  190.0 62.6 %all-to-all-done.2 = bf16[64,6,3584]{2,1,0:T(8,128)(2,1)} async-done(((bf16[64,6,3584]{2,1,0:T(8,128)(2,1)}), bf16[64,6,3584]{2,1,0:T(8,128)(2,1)}, u32[]{:S(2)}, u32[]{:S(2)}) %all-to-all-start.2) | async-done | bytes 2752544 | tf_op jit(solution)/shard_map/all_to_all | solution.py:54
  252.7 12.2 %all-to-all-start = ((bf16[64,6,3584]{2,1,0:T(8,128)(2,1)}), bf16[64,6,3584]{2,1,0:T(8,128)(2,1)}, u32[]{:S(2)}, u32[]{:S(2)}) async-start(bf16[64,6,3584]{2,1,0:T(8,128)(2,1)} %broadcast_select_fusion), calls=%async_computation | async-start | bytes 7340032 | tf_op jit(solution)/shard_map/all_to_all | solution.py:53
  264.9 0.2 reduce-scatter.3.cloned.1.call-start
  265.1 5.5 reshape.110
  270.5 80.1 %all-to-all-done = bf16[64,6,3584]{2,1,0:T(8,128)(2,1)} async-done(((bf16[64,6,3584]{2,1,0:T(8,128)(2,1)}), bf16[64,6,3584]{2,1,0:T(8,128)(2,1)}, u32[]{:S(2)}, u32[]{:S(2)}) %all-to-all-start) | async-done | bytes 2752544 | tf_op jit(solution)/shard_map/all_to_all | solution.py:53
  350.6 5.4 reshape.107
  356.1 0.0 all-gather.3.cloned.1.call-done
  356.1 6.1 %fusion.5 = f32[384,1024]{1,0:T(8,128)S(1)} fusion(bf16[384,3584]{1,0:T(8,128)(2,1)} %reshape.107, bf16[3584,1024]{1,0:T(8,128)(2,1)} %all-gather.3.cloned.1.call-done), kind=kOutput, calls=%fused_computation.36 | convolution fusion | flops 2818572288 | bytes 11665408 | tf_op jit(solution)/shard_map/dot_general | solution.py:64
  362.2 0.0 all-gather.5.cloned.1.call-done
  362.2 0.0 copy-start.4
  362.2 7.3 %multiply_convert_fusion.1 = bf16[384,1024]{1,0:T(8,128)(2,1)S(1)} fusion(f32[384,1024]{1,0:T(8,128)S(1)} %fusion.5, bf16[384,3584]{1,0:T(8,128)(2,1)} %reshape.110, bf16[1024,3584]{1,0:T(8,128)(2,1)} %all-gather.5.cloned.1.call-done), kind=kOutput, calls=%fused_computation.14 | convolution fusion | flops 2822111232 | bytes 12451840 | tf_op jit(solution)/shard_map/dot_general | solution.py:68
  369.5 0.0 copy-done.4
  369.5 6.1 %convolution_convert_fusion.1 = bf16[3584,1024]{1,0:T(8,128)(2,1)} fusion(bf16[384,3584]{1,0:T(8,128)(2,1)S(1)} %copy-done.4, bf16[384,1024]{1,0:T(8,128)(2,1)S(1)} %multiply_convert_fusion.1), kind=kOutput, calls=%fused_computation.7 | convolution fusion | flops 2822242304 | bytes 10878976 | tf_op jit(solution)/shard_map/dot_general | solution.py:70
  375.6 0.0 reduce-scatter.3.cloned.1.call-update
  375.6 0.0 reduce-scatter.5.cloned.1.call-start
  375.6 8.5 %convolution_convert_fusion = bf16[1024,3584]{1,0:T(8,128)(2,1)} fusion(bf16[384,3584]{1,0:T(8,128)(2,1)} %reshape.110, f32[384,1024]{1,0:T(8,128)S(1)} %fusion.5), kind=kOutput, calls=%fused_computation.6 | convolution fusion | flops 2824208384 | bytes 11665408 | tf_op jit(solution)/shard_map/dot_general | solution.py:71
  384.2 0.0 reduce-scatter.5.cloned.1.call-update
  384.2 7.5 %convolution_convert_fusion.2 = bf16[384,3584]{1,0:T(8,128)(2,1)} fusion(bf16[1024,3584]{1,0:T(8,128)(2,1)} %all-gather.5.cloned.1.call-done, f32[384,1024]{1,0:T(8,128)S(1)} %fusion.5), kind=kOutput, calls=%fused_computation.9 | convolution fusion | flops 2821914624 | bytes 11665408 | tf_op jit(solution)/shard_map/dot_general | solution.py:67
  391.7 5.4 reshape.108
  397.1 7.7 %all-to-all-start.1 = ((bf16[64,6,3584]{2,1,0:T(8,128)(2,1)}), bf16[64,6,3584]{2,1,0:T(8,128)(2,1)}, u32[]{:S(2)}, u32[]{:S(2)}) async-start(bf16[64,6,3584]{2,1,0:T(8,128)(2,1)} %reshape.108), calls=%async_computation.1 | async-start | bytes 7340032 | tf_op jit(solution)/shard_map/all_to_all | solution.py:85
  404.8 83.8 %all-to-all-done.1 = bf16[64,6,3584]{2,1,0:T(8,128)(2,1)} async-done(((bf16[64,6,3584]{2,1,0:T(8,128)(2,1)}), bf16[64,6,3584]{2,1,0:T(8,128)(2,1)}, u32[]{:S(2)}, u32[]{:S(2)}) %all-to-all-start.1) | async-done | bytes 2752544 | tf_op jit(solution)/shard_map/all_to_all | solution.py:85
  488.6 5.5 reshape.109
  494.1 0.0 copy-start.1
  494.1 7.0 %gather_fusion.2 = bf16[256,3584]{1,0:T(8,128)(2,1)} fusion(bf16[384,3584]{1,0:T(8,128)(2,1)} %reshape.109, s32[1024]{0:T(1024)S(1)} %pad_clamp_fusion), kind=kCustom, calls=%fused_computation.2 | custom fusion | bytes 3671040 | tf_op jit(solution)/shard_map/gather | solution.py:86
  501.1 3.2 multiply_convert_fusion
  504.3 0.0 reduce-scatter.3.cloned.1.call-done
  504.3 57.1 %reduce-scatter.5.cloned.1.call-done = bf16[256,3584]{1,0:T(8,128)(2,1)} async-done(((bf16[1024,3584]{1,0:T(8,128)(2,1)}), bf16[256,3584]{1,0:T(8,128)(2,1)}) %reduce-scatter.5.cloned.1.call-update) | async-done | bytes 1835024 | tf_op jit(solution)/shard_map/reduce_scatter | solution.py:78
  561.4 0.0 copy-done.1
  (13 shorter events, 0.1 us)
Async XLA Ops:
  7.2 96.7 %copy-start = (bf16[256,3584]{1,0:T(8,128)(2,1)S(1)}, bf16[256,3584]{1,0:T(8,128)(2,1)}, u32[]{:S(2)}) copy-start(bf16[256,3584]{1,0:T(8,128)(2,1)} %param.8) | copy-start | bytes 5505028
  7.2 348.9 %all-gather.3.cloned.1.call-start = ((), (), s32[]{:S(2)}) async-start(), calls=%async_computation.5 | async-start | bytes 9175040 | tf_op jit(solution)/shard_map/all_gather | solution.py:59
  7.2 85.1 %collective-permute-start = (bf16[3584,256]{1,0:T(8,128)(2,1)}, bf16[3584,256]{1,0:T(8,128)(2,1)}, u32[]{:S(2)}, u32[]{:S(2)}) collective-permute-start(bf16[3584,256]{1,0:T(8,128)(2,1)} %bitcast.37), channel_id=1, source_target_pairs={{0,32},{32,0},{1,33},{33,1},{2,34},{34,2},{3,35},{35,3},{4,36},{36... | collective-permute-start | bytes 5505032 | tf_op jit(solution)/shard_map/ppermute | solution.py:14
  92.3 4.2 copy-start.5
  92.3 4.2 copy-start.6
  95.3 5.6 copy-start.2
  95.3 78.2 %collective-permute-start.1 = (bf16[256,3584]{1,0:T(8,128)(2,1)}, bf16[256,3584]{1,0:T(8,128)(2,1)}, u32[]{:S(2)}, u32[]{:S(2)}) collective-permute-start(bf16[256,3584]{1,0:T(8,128)(2,1)} %bitcast.38), channel_id=1, source_target_pairs={{0,32},{32,0},{1,33},{33,1},{2,34},{34,2},{3,35},{35,3},{4,36},{36... | collective-permute-start | bytes 5505032 | tf_op jit(solution)/shard_map/ppermute | solution.py:14
  120.3 132.4 %all-to-all-start.2 = ((bf16[64,6,3584]{2,1,0:T(8,128)(2,1)}), bf16[64,6,3584]{2,1,0:T(8,128)(2,1)}, u32[]{:S(2)}, u32[]{:S(2)}) async-start(bf16[64,6,3584]{2,1,0:T(8,128)(2,1)} %select_convert_fusion), calls=%async_computation.2 | async-start | bytes 7340032 | tf_op jit(solution)/shard_map/all_to_all | solution.py:54
  133.4 43.1 %copy-start.3 = (bf16[256,3584]{1,0:T(8,128)(2,1)S(1)}, bf16[256,3584]{1,0:T(8,128)(2,1)}, u32[]{:S(2)}) copy-start(bf16[256,3584]{1,0:T(8,128)(2,1)} %param.7) | copy-start | bytes 5505028
  133.4 228.8 %all-gather.5.cloned.1.call-start = ((), (), s32[]{:S(2)}) async-start(), calls=%async_computation.6 | async-start | bytes 9175040 | tf_op jit(solution)/shard_map/all_gather | solution.py:60
  252.7 97.9 %all-to-all-start = ((bf16[64,6,3584]{2,1,0:T(8,128)(2,1)}), bf16[64,6,3584]{2,1,0:T(8,128)(2,1)}, u32[]{:S(2)}, u32[]{:S(2)}) async-start(bf16[64,6,3584]{2,1,0:T(8,128)(2,1)} %broadcast_select_fusion), calls=%async_computation | async-start | bytes 7340032 | tf_op jit(solution)/shard_map/all_to_all | solution.py:53
  264.9 239.4 %reduce-scatter.3.cloned.1.call-start = ((), (), s32[]{:S(2)}) async-start(), calls=%async_computation.7 | async-start | bytes 9175040 | tf_op jit(solution)/shard_map/reduce_scatter | solution.py:75
  362.2 7.3 %copy-start.4 = (bf16[384,3584]{1,0:T(8,128)(2,1)S(1)}, bf16[384,3584]{1,0:T(8,128)(2,1)}, u32[]{:S(2)}) copy-start(bf16[384,3584]{1,0:T(8,128)(2,1)} %reshape.107) | copy-start | bytes 8257540
  375.6 185.8 %reduce-scatter.5.cloned.1.call-start = ((), (), s32[]{:S(2)}) async-start(), calls=%async_computation.8 | async-start | bytes 9175040 | tf_op jit(solution)/shard_map/reduce_scatter | solution.py:78
  397.1 91.5 %all-to-all-start.1 = ((bf16[64,6,3584]{2,1,0:T(8,128)(2,1)}), bf16[64,6,3584]{2,1,0:T(8,128)(2,1)}, u32[]{:S(2)}, u32[]{:S(2)}) async-start(bf16[64,6,3584]{2,1,0:T(8,128)(2,1)} %reshape.108), calls=%async_computation.1 | async-start | bytes 7340032 | tf_op jit(solution)/shard_map/all_to_all | solution.py:85
  494.1 67.4 %copy-start.1 = (bf16[256,3584]{1,0:T(8,128)(2,1)S(1)}, bf16[256,3584]{1,0:T(8,128)(2,1)}, u32[]{:S(2)}) copy-start(bf16[256,3584]{1,0:T(8,128)(2,1)} %param.8) | copy-start | bytes 5505028
Sparse Core Ops, SparseCore 0:
  95.4 84.4 all-gather.2
  182.3 125.1 all-gather.4
  375.7 108.3 reduce-scatter.2
  487.1 74.3 reduce-scatter.4
where the time goes:
time: 573 us; the launch traced here: 568 us
  waiting for transfers between devices  406 us (71%)
  local copies, waits for them, and re-layouts  55.8 us (10%)
  matrix products  35.4 us (6%)
  starting transfers between devices  35.1 us (6%)
  other arithmetic  20.7 us (4%)
  between operations  14.6 us (3%)
    ppermute x2, waiting for transfers between devices, partner_2(): return lax.ppermute(block, axis, route)  123 us
    all_to_all x1, waiting for transfers between devices, body(): lax.all_to_all(expert_out, 'expert', split_axis=0, concat_axis=0, tiled=T...  83.8 us
    all_to_all x1, waiting for transfers between devices, body(): lax.all_to_all(send_rows, 'expert', split_axis=0, concat_axis=0, tiled=True)  80.1 us
    all_to_all x1, waiting for transfers between devices, body(): lax.all_to_all(send_grads, 'expert', split_axis=0, concat_axis=0, tiled=T...  62.6 us
    reduce_scatter x1, waiting for transfers between devices, body(): lax.psum_scatter(term_out.astype(jnp.bfloat16), 'dp', scatter_dimension=0...  57.1 us
    all_to_all x1, starting transfers between devices, body(): lax.all_to_all(send_grads, 'expert', split_axis=0, concat_axis=0, tiled=T...  13 us
    all_to_all x1, starting transfers between devices, body(): lax.all_to_all(send_rows, 'expert', split_axis=0, concat_axis=0, tiled=True)  12.2 us
  transfers between devices with their start and end apart: 9, of which 6 were waited for; matrix products, arithmetic and copies ran while one was open for 17% of the time, Pallas kernels for 0%

commit v1 on v0

v1 whole, which is shorter than its diff:
```python
import jax
import jax.numpy as jnp
from jax import lax
from jax.sharding import Mesh, PartitionSpec as P


def partner_2(block, axis, distance):
    count = lax.axis_size(axis)
    route = []
    for low in range(count):
        high = low | 1 << distance
        if high != low and high < count:
            route += [(low, high), (high, low)]
    return lax.ppermute(block, axis, route)


def swap_core(block):
    return lax.ppermute(block, "dc", [(0, 1), (1, 0)])


def body(tokens, cotangent, expert_ids, gates, pair_flags, w_in, w_out):
    expert_count = lax.axis_size("expert")
    own_index = lax.axis_index("expert")
    half_axis = expert_count // 2
    pair_bit = half_axis.bit_length() - 1
    local_tokens, top_count = expert_ids.shape
    width = tokens.shape[1]
    capacity = max(2, 3 * local_tokens * top_count // (2 * expert_count))
    route_count = local_tokens * top_count
    slots = expert_count * capacity
    lanes = jnp.arange(expert_count, dtype=jnp.int32)
    partner = jnp.bitwise_xor(lanes, half_axis * pair_flags)
    flagged = pair_flags[own_index] == 1

    quarter_in = w_in[0]
    quarter_out = w_out[0]
    their_in, their_out = partner_2((quarter_in, quarter_out), "expert", pair_bit)
    quarter_in = jnp.where(flagged, their_in, quarter_in)
    quarter_out = jnp.where(flagged, their_out, quarter_out)
    half_in = lax.all_gather(quarter_in, "dx", axis=1, tiled=True)
    half_out = lax.all_gather(quarter_out, "dx", axis=0, tiled=True)

    flat_ids = expert_ids.reshape(-1)
    target_of = partner[flat_ids]
    onehot = (target_of[:, None] == lanes[None, :]).astype(jnp.int32)
    position = jnp.sum(jnp.cumsum(onehot, axis=0) * onehot, axis=1) - 1
    slot_of = target_of * capacity + position
    select = (slot_of[None, :] == jnp.arange(slots, dtype=jnp.int32)[:, None]).astype(
        jnp.bfloat16
    )
    token_of = jnp.arange(route_count, dtype=jnp.int32) // top_count
    route_rows = tokens[token_of] if top_count > 1 else tokens
    route_cot = cotangent[token_of] if top_count > 1 else cotangent
    scaled = (gates.reshape(-1)[:, None] * route_cot.astype(jnp.float32)).astype(jnp.bfloat16)
    send_rows = jnp.dot(select, route_rows, preferred_element_type=jnp.float32).astype(
        jnp.bfloat16
    )
    send_grads = jnp.dot(select, scaled, preferred_element_type=jnp.float32).astype(
        jnp.bfloat16
    )
    send = jnp.stack(
        [send_rows.reshape(expert_count, capacity, width),
         send_grads.reshape(expert_count, capacity, width)],
        axis=1,
    )
    recv = lax.all_to_all(send, "expert", split_axis=0, concat_axis=0, tiled=True)
    other = swap_core(recv)

    contract_last = (((1,), (1,)), ((), ()))
    contract_first = (((0,), (0,)), ((), ()))

    def expert_pass(block):
        rows = block[:, 0].reshape(slots, width)
        grads = block[:, 1].reshape(slots, width)
        pre = jnp.dot(rows, half_in, preferred_element_type=jnp.float32)
        sig = jax.nn.sigmoid(pre)
        hidden = (pre * sig).astype(jnp.bfloat16)
        out = jnp.dot(hidden, half_out, preferred_element_type=jnp.float32)
        dhid = lax.dot_general(grads, half_out, contract_last, preferred_element_type=jnp.float32)
        dpre = (dhid * sig * (1.0 + pre * (1.0 - sig))).astype(jnp.bfloat16)
        term_in = lax.dot_general(rows, dpre, contract_first, preferred_element_type=jnp.float32)
        term_out = lax.dot_general(hidden, grads, contract_first, preferred_element_type=jnp.float32)
        return out, term_in, term_out

    out_other, in_other, outg_other = expert_pass(other)
    back = swap_core(out_other.astype(jnp.bfloat16))
    out_own, in_own, outg_own = expert_pass(recv)
    expert_out = (out_own + back.astype(jnp.float32)).astype(jnp.bfloat16)

    term_in = (in_own + in_other).astype(jnp.bfloat16)
    term_out = (outg_own + outg_other).astype(jnp.bfloat16)
    grad_quarter_in = lax.psum_scatter(term_in, "dx", scatter_dimension=1, tiled=True)
    grad_quarter_out = lax.psum_scatter(term_out, "dx", scatter_dimension=0, tiled=True)

    returned = lax.all_to_all(
        expert_out.reshape(expert_count, capacity, width), "expert",
        split_axis=0, concat_axis=0, tiled=True,
    ).reshape(slots, width)
    route_out = lax.dot_general(
        select, returned, contract_first, preferred_element_type=jnp.float32
    )
    weighted = gates.reshape(local_tokens, top_count, 1) * route_out.astype(
        jnp.bfloat16
    ).astype(jnp.float32).reshape(local_tokens, top_count, width)
    mixed = jnp.sum(weighted, axis=1).astype(jnp.bfloat16)
    return (mixed, grad_quarter_in[None], grad_quarter_out[None])


def solution(mesh):
    devices = mesh.devices
    dp_count = devices.shape[0]
    split = Mesh(
        devices.reshape(dp_count // 2, 2, devices.shape[1]), ("dx", "dc", "expert")
    )
    rows = P(("dx", "dc", "expert"), None)
    placed = (
        rows,
        rows,
        rows,
        rows,
        P(),
        P("expert", None, ("dx", "dc")),
        P("expert", ("dx", "dc"), None),
    )
    return jax.shard_map(
        body,
        mesh=split,
        in_specs=placed,
        out_specs=(rows, P("expert", None, ("dx", "dc")), P("expert", ("dx", "dc"), None)),
        check_vma=False,
    )
```

time: 573 us -> 585 us (1.021); the launches traced: 568 us -> 574 us
  waiting for transfers between devices: 406 us -> 266 us
  blocking collectives: 0 us -> 99.1 us
  local copies, waits for them, and re-layouts: 55.8 us -> 104 us
  matrix products: 35.4 us -> 60.7 us
  starting transfers between devices: 35.1 us -> 18.7 us
  other arithmetic: 20.7 us -> 10.2 us
    all_to_all x3 -> x1, waiting for transfers between devices: 227 us -> 0.01 us  [body(): lax.all_to_all(send, 'expert', split_axis=0, concat_axis=0, tiled=True)]
    ppermute x2, waiting for transfers between devices: 123 us -> 266 us  [partner_2(): return lax.ppermute(block, axis, route)]
    all_to_all x0 -> x1, blocking collectives: none -> 99.1 us  [body(): lax.all_to_all(expert_out.reshape(expert_count, capacity, width), 'expert...]
    reduce_scatter x2, waiting for transfers between devices: 57.1 us -> 0.01 us  [the longest x1 0.01 us: body(): lax.psum_scatter(term_out, 'dx', scatter_dimension=0, tiled=True)]
    slice x1 -> x5, local copies, waits for them, and re-layouts: 0.18 us -> 47 us  [the longest x3 43.5 us: expert_pass(): grads = block[:, 1].reshape(slots, width)]
    another operation x1 -> x8, local copies, waits for them, and re-layouts: 0.01 us -> 37 us  [the longest x3 16.3 us: body(): jnp.stack([send_rows.reshape(expert_count, capacity, width), send_grads.r...]
    dot_general x5 -> x11, matrix products: 35.4 us -> 60.7 us  [the longest x2 21.2 us: expert_pass(): lax.dot_general(rows, dpre, contract_first, preferred_element_type=jnp.fl...]
    gather x5 -> x0, local copies, waits for them, and re-layouts: 23 us -> none  [the longest x2 9.29 us: body(): tokens[token_row]]
  transfers between devices with their start and end apart: 9 -> 9, of which waited for: 6 -> 2; matrix products, arithmetic and copies ran while one was open for 17% -> 24% of each run, Pallas kernels for 0% -> 0%
where the time goes in v1:
time: 585 us; the launch traced here: 574 us
  waiting for transfers between devices  266 us (45%)
  local copies, waits for them, and re-layouts  104 us (18%)
  blocking collectives  99.1 us (17%)
  matrix products  60.7 us (10%)
  starting transfers between devices  18.7 us (3%)
  between operations  15.1 us (3%)
  other arithmetic  10.2 us (2%)
    ppermute x2, waiting for transfers between devices, partner_2(): return lax.ppermute(block, axis, route)  266 us
    all_to_all x1, blocking collectives, body(): lax.all_to_all(expert_out.reshape(expert_count, capacity, width), 'expert...  99.1 us
    slice x3, local copies, waits for them, and re-layouts, expert_pass(): grads = block[:, 1].reshape(slots, width)  43.5 us
    dot_general x2, matrix products, expert_pass(): lax.dot_general(rows, dpre, contract_first, preferred_element_type=jnp.fl...  21.2 us
    another operation x3, local copies, waits for them, and re-layouts, body(): jnp.stack([send_rows.reshape(expert_count, capacity, width), send_grads.r...  16.3 us
    all_to_all x1, starting transfers between devices, body(): lax.all_to_all(send, 'expert', split_axis=0, concat_axis=0, tiled=True)  12.5 us
  transfers between devices with their start and end apart: 9, of which 2 were waited for; matrix products, arithmetic and copies ran while one was open for 24% of the time, Pallas kernels for 0%

profile of v1, /device:TPU:192, one launch (start us, length us, event | category | flops | bytes accessed | tf_op | source)
XLA Modules:
  0.0 573.8 jit_solution(5537738117449763609)
XLA Ops:
  7.2 0.0 copy-start
  7.2 0.8 compare_select_fusion
  8.0 0.7 multiply_xor_fusion
  8.7 1.9 gather_fusion
  10.6 0.6 reduce-window.6
  11.2 0.2 slice_reduce_fusion.2
  11.4 0.1 fusion.19
  11.5 4.0 convolution_convert_fusion.1
  15.5 5.4 stack_reshape.7
  20.9 2.5 convolution_convert_fusion.2
  23.4 5.4 stack_reshape.6
  28.8 5.1 pad_maximum_fusion
  33.9 5.5 copy.12
  39.4 12.5 %all-to-all-start = ((bf16[64,2,6,3584]{3,1,2,0:T(2,128)(2,1)}), bf16[64,2,6,3584]{3,1,2,0:T(2,128)(2,1)}, u32[]{:S(2)}, u32[]{:S(2)}) async-start(bf16[64,2,6,3584]{3,1,2,0:T(2,128)(2,1)} %copy.12), calls=%async_computation | async-start | bytes 11010048 | tf_op jit(solution)/shard_map/all_to_all | solution.py:66
  51.9 0.0 all-gather.3.cloned.1.call-start
  51.9 2.2 collective-permute-start
  54.2 0.6 dynamic_slice.3
  55.4 195.2 %collective-permute-done = bf16[3584,256]{1,0:T(8,128)(2,1)} collective-permute-done((bf16[3584,256]{1,0:T(8,128)(2,1)S(1)}, bf16[3584,256]{1,0:T(8,128)(2,1)}, u32[]{:S(2)}, u32[]{:S(2)}) %collective-permute-start) | collective-permute-done | bytes 1835040 | tf_op jit(solution)/shard_map/ppermute | solution.py:14
  250.6 1.4 broadcast_select_fusion.1
  252.0 0.0 all-gather.3.cloned.1.call-update
  252.1 0.0 all-gather.5.cloned.1.call-start
  252.1 0.0 copy-start.8
  252.1 3.8 collective-permute-start.1
  255.9 0.0 all-to-all-done
  255.9 6.0 %copy.13 = bf16[64,2,6,3584]{3,0,2,1:T(8,128)(2,1)} copy(bf16[64,2,6,3584]{3,1,2,0:T(2,128)(2,1)} %all-to-all-done) | data formatting | bytes 11010048 | tf_op jit(solution)/shard_map/all_to_all | solution.py:66
  261.9 0.0 collective-permute-start.2
  261.9 70.5 %collective-permute-done.1 = bf16[256,3584]{1,0:T(8,128)(2,1)} collective-permute-done((bf16[256,3584]{1,0:T(8,128)(2,1)}, bf16[256,3584]{1,0:T(8,128)(2,1)}, u32[]{:S(2)}, u32[]{:S(2)}) %collective-permute-start.1) | collective-permute-done | bytes 1835040 | tf_op jit(solution)/shard_map/ppermute | solution.py:14
  332.4 1.4 broadcast_select_fusion
  333.9 0.0 all-gather.5.cloned.1.call-update
  333.9 0.0 reduce-scatter.5.cloned.1.call-start
  333.9 37.2 %slice_reduce_fusion = (bf16[64,6,3584]{2,1,0:T(8,128)(2,1)}, bf16[64,6,3584]{2,1,0:T(8,128)(2,1)}) fusion(bf16[64,2,6,3584]{3,1,2,0:T(2,128)(2,1)} %all-to-all-done), kind=kLoop, calls=%fused_computation.9 | loop fusion | bytes 11010048 | tf_op jit(solution)/shard_map/slice | solution.py:74
  371.1 5.4 reshape_squeeze.12
  376.5 4.0 reshape_squeeze.14
  380.5 0.0 all-gather.3.cloned.1.call-done
  380.5 5.4 fusion.25
  386.0 0.0 copy-done.4
  386.0 5.1 fusion.23
  391.1 0.0 collective-permute-done.2
  391.1 3.0 fusion.24
  394.2 3.3 copy.14
  397.5 5.4 reshape_squeeze.13
  402.9 3.3 copy.15
  406.3 5.8 %reshape_squeeze.15 = bf16[384,3584]{1,0:T(8,128)(2,1)} reshape(bf16[64,1,6,3584]{3,2,0,1:T(8,128)(2,1)} %copy.15) | data formatting | bytes 5505024 | tf_op jit(solution)/shard_map/reshape;squeeze | solution.py:74
  412.1 0.0 slice-start.1
  412.1 4.6 fusion.26
  416.7 0.0 copy-start.5
  416.7 0.9 copy-done.5
  417.6 4.0 add_convert_fusion
  421.6 0.0 reduce-scatter.5.cloned.1.call-update
  421.6 0.0 reduce-scatter.3.cloned.1.call-start
  421.7 0.0 all-gather.5.cloned.1.call-done
  421.7 1.0 copy-done.6
  422.7 5.2 convolution_convert_fusion
  427.9 0.0 collective-permute-start.3
  427.9 10.6 %fusion.9 = f32[3584,512]{1,0:T(8,128)} fusion(bf16[384,3584]{1,0:T(8,128)(2,1)} %reshape_squeeze.12, bf16[384,3584]{1,0:T(8,128)(2,1)} %copy-done.4, bf16[512,3584]{1,0:T(8,128)(2,1)} %all-gather.5.cloned.1.call-done, f32[384,512]{1,0:T(8,128)} %copy-done.9), kind=kOutput, calls=%fused_computation.25 | convolution fusion | flops 2820341760 | bytes 17301504 | tf_op jit(solution)/shard_map/dot_general | solution.py:81
  438.6 10.5 %add_convert_fusion.1 = bf16[3584,512]{1,0:T(8,128)(2,1)} fusion(f32[3584,512]{1,0:T(8,128)} %fusion.9, bf16[384,3584]{1,0:T(8,128)(2,1)} %reshape_squeeze.13, bf16[384,3584]{1,0:T(8,128)(2,1)S(1)} %copy-done.3, bf16[512,3584]{1,0:T(8,128)(2,1)} %all-gather.5.cloned.1.call-done, f32[384,512]{1,0:T(8,128)S(1)} %copy-done.6), kind=kOutput, calls=%fused_computation.3 | convolution fusion | flops 2824011776 | bytes 20971520 | tf_op jit(solution)/shard_map/dot_general | solution.py:81
  449.1 0.0 reduce-scatter.3.cloned.1.call-update
  449.1 0.0 collective-permute-done.3
  449.2 1.1 copy-done.10
  450.2 4.5 fusion
  454.8 3.0 reshape.47
  457.8 99.1 %all_to_all.10 = bf16[64,6,3584]{2,1,0:T(8,128)(2,1)} all-to-all(bf16[64,6,3584]{2,1,0:T(8,128)(2,1)} %reshape.47), channel_id=1, replica_groups=mesh['dx'=2,'dc'=2,'expert'=64] {'expert'}, dimensions={0} | all-to-all | bytes 5505024 | tf_op jit(solution)/shard_map/all_to_all | solution.py:95
  556.9 5.6 reshape.48
  562.5 4.2 fusion.3
  (30 shorter events, 0.1 us)
Async XLA Ops:
  7.2 13.8 %copy-start = (bf16[256,3584]{1,0:T(8,128)(2,1)S(1)}, bf16[256,3584]{1,0:T(8,128)(2,1)}, u32[]{:S(2)}) copy-start(bf16[256,3584]{1,0:T(8,128)(2,1)} %param.7) | copy-start | bytes 5505028
  39.4 12.5 %copy-start.7 = (bf16[1,3584,256]{2,1,0:T(8,128)(2,1)S(1)}, bf16[1,3584,256]{2,1,0:T(8,128)(2,1)}, u32[]{:S(2)}) copy-start(bf16[1,3584,256]{2,1,0:T(8,128)(2,1)} %param.12) | copy-start | bytes 5505028
  39.4 14.8 %copy-start.12 = (s32[64]{0:T(128)S(1)}, s32[64]{0:T(128)}, u32[]{:S(2)}) copy-start(s32[64]{0:T(128)} %param.11) | copy-start | bytes 772
  39.4 216.5 %all-to-all-start = ((bf16[64,2,6,3584]{3,1,2,0:T(2,128)(2,1)}), bf16[64,2,6,3584]{3,1,2,0:T(2,128)(2,1)}, u32[]{:S(2)}, u32[]{:S(2)}) async-start(bf16[64,2,6,3584]{3,1,2,0:T(2,128)(2,1)} %copy.12), calls=%async_computation | async-start | bytes 11010048 | tf_op jit(solution)/shard_map/all_to_all | solution.py:66
  51.9 328.6 %all-gather.3.cloned.1.call-start = ((), (), s32[]{:S(2)}) async-start(), calls=%async_computation.4 | async-start | bytes 5505024 | tf_op jit(solution)/shard_map/all_gather | solution.py:40
  51.9 198.7 %collective-permute-start = (bf16[3584,256]{1,0:T(8,128)(2,1)S(1)}, bf16[3584,256]{1,0:T(8,128)(2,1)}, u32[]{:S(2)}, u32[]{:S(2)}) collective-permute-start(bf16[3584,256]{1,0:T(8,128)(2,1)S(1)} %bitcast.47), channel_id=1, source_target_pairs={{0,32},{32,0},{1,33},{33,1},{2,34},{34,2},{3,35},{35,3},{4,36},{36... | collective-permute-start | bytes 5505032 | tf_op jit(solution)/shard_map/ppermute | solution.py:14
  252.1 169.6 %all-gather.5.cloned.1.call-start = ((), (), s32[]{:S(2)}) async-start(), calls=%async_computation.5 | async-start | bytes 5505024 | tf_op jit(solution)/shard_map/all_gather | solution.py:41
  252.1 80.3 %copy-start.8 = (bf16[1,256,3584]{2,1,0:T(8,128)(2,1)S(1)}, bf16[1,256,3584]{2,1,0:T(8,128)(2,1)}, u32[]{:S(2)}) copy-start(bf16[1,256,3584]{2,1,0:T(8,128)(2,1)} %param.13) | copy-start | bytes 5505028
  252.1 80.3 %collective-permute-start.1 = (bf16[256,3584]{1,0:T(8,128)(2,1)}, bf16[256,3584]{1,0:T(8,128)(2,1)}, u32[]{:S(2)}, u32[]{:S(2)}) collective-permute-start(bf16[256,3584]{1,0:T(8,128)(2,1)} %bitcast.48), channel_id=1, source_target_pairs={{0,32},{32,0},{1,33},{33,1},{2,34},{34,2},{3,35},{35,3},{4,36},{36... | collective-permute-start | bytes 5505032 | tf_op jit(solution)/shard_map/ppermute | solution.py:14
  261.9 129.2 %collective-permute-start.2 = (bf16[64,2,6,3584]{3,0,2,1:T(8,128)(2,1)}, bf16[64,2,6,3584]{3,0,2,1:T(8,128)(2,1)}, u32[]{:S(2)}, u32[]{:S(2)}) collective-permute-start(bf16[64,2,6,3584]{3,0,2,1:T(8,128)(2,1)} %copy.13), channel_id=1, source_target_pairs={{0,64},{64,0},{1,65},{65,1},{2,66},{66,2},{3,67},{67,3},{4,68},{68... | collective-permute-start | bytes 16515080 | tf_op jit(solution)/shard_map/ppermute | solution.py:18
  333.9 232.9 %reduce-scatter.5.cloned.1.call-start = ((), (), s32[]{:S(2)}) async-start(), calls=%async_computation.7 | async-start | bytes 5505024 | tf_op jit(solution)/shard_map/reduce_scatter | solution.py:93
  380.5 5.5 copy-start.4
  386.0 5.2 copy-start.9
  406.3 11.3 %slice-start = ((s8[7340032]{0:T(1024)(128)(4,1)}), s8[3145728]{0:T(1024)(128)(4,1)S(1)}, s32[]{:S(2)}) async-start(s8[7340032]{0:T(1024)(128)(4,1)} %bitcast.45), calls=%async_computation.8 | async-start | bytes 6291456
  412.1 5.5 slice-start.1
  412.1 5.5 copy-start.2
  416.7 0.9 copy-start.5
  421.6 1.1 copy-start.6
  421.6 145.2 %reduce-scatter.3.cloned.1.call-start = ((), (), s32[]{:S(2)}) async-start(), calls=%async_computation.6 | async-start | bytes 5505024 | tf_op jit(solution)/shard_map/reduce_scatter | solution.py:92
  427.9 10.6 %copy-start.3 = (bf16[384,3584]{1,0:T(8,128)(2,1)S(1)}, bf16[384,3584]{1,0:T(8,128)(2,1)}, u32[]{:S(2)}) copy-start(bf16[384,3584]{1,0:T(8,128)(2,1)} %reshape_squeeze.15) | copy-start | bytes 8257540
  427.9 21.2 %collective-permute-start.3 = (bf16[384,3584]{1,0:T(8,128)(2,1)}, bf16[384,3584]{1,0:T(8,128)(2,1)}, u32[]{:S(2)}, u32[]{:S(2)}) collective-permute-start(bf16[384,3584]{1,0:T(8,128)(2,1)} %convolution_convert_fusion), channel_id=1, source_target_pairs={{0,64},{64,0},{1,65},{65,1},{2,66},{66,2},{3,67},{67,3},{4,68},{68... | collective-permute-start | bytes 8257544 | tf_op jit(solution)/shard_map/ppermute | solution.py:18
  449.1 1.1 copy-start.10
  556.9 5.7 copy-start.11
  556.9 9.9 %copy-start.1 = (bf16[256,3584]{1,0:T(8,128)(2,1)S(1)}, bf16[256,3584]{1,0:T(8,128)(2,1)}, u32[]{:S(2)}) copy-start(bf16[256,3584]{1,0:T(8,128)(2,1)} %param.7) | copy-start | bytes 5505028
Sparse Core Ops, SparseCore 0:
  252.2 57.2 all-gather.2
  334.0 57.0 all-gather.4
  421.8 64.9 reduce-scatter.4
  489.8 74.3 reduce-scatter.2

commit v2 on v1

--- a/solution.py
+++ b/solution.py
@@ -34,9 +34,11 @@
 
     quarter_in = w_in[0]
     quarter_out = w_out[0]
-    their_in, their_out = partner_2((quarter_in, quarter_out), "expert", pair_bit)
-    quarter_in = jnp.where(flagged, their_in, quarter_in)
-    quarter_out = jnp.where(flagged, their_out, quarter_out)
+    size_in = quarter_in.size
+    both = jnp.concatenate([quarter_in.reshape(-1), quarter_out.reshape(-1)])
+    both = jnp.where(flagged, partner_2(both, "expert", pair_bit), both)
+    quarter_in = both[:size_in].reshape(quarter_in.shape)
+    quarter_out = both[size_in:].reshape(quarter_out.shape)
     half_in = lax.all_gather(quarter_in, "dx", axis=1, tiled=True)
     half_out = lax.all_gather(quarter_out, "dx", axis=0, tiled=True)
 
@@ -52,26 +54,20 @@
     route_rows = tokens[token_of] if top_count > 1 else tokens
     route_cot = cotangent[token_of] if top_count > 1 else cotangent
     scaled = (gates.reshape(-1)[:, None] * route_cot.astype(jnp.float32)).astype(jnp.bfloat16)
-    send_rows = jnp.dot(select, route_rows, preferred_element_type=jnp.float32).astype(
-        jnp.bfloat16
-    )
-    send_grads = jnp.dot(select, scaled, preferred_element_type=jnp.float32).astype(
-        jnp.bfloat16
-    )
-    send = jnp.stack(
-        [send_rows.reshape(expert_count, capacity, width),
-         send_grads.reshape(expert_count, capacity, width)],
-        axis=1,
-    )
-    recv = lax.all_to_all(send, "expert", split_axis=0, concat_axis=0, tiled=True)
+    payload = jnp.concatenate([route_rows, scaled], axis=1)
+    send = jnp.dot(select, payload, preferred_element_type=jnp.float32).astype(jnp.bfloat16)
+    recv = lax.all_to_all(
+        send.reshape(expert_count, capacity, 2 * width), "expert",
+        split_axis=0, concat_axis=0, tiled=True,
+    ).reshape(slots, 2 * width)
     other = swap_core(recv)
 
     contract_last = (((1,), (1,)), ((), ()))
     contract_first = (((0,), (0,)), ((), ()))
 
     def expert_pass(block):
-        rows = block[:, 0].reshape(slots, width)
-        grads = block[:, 1].reshape(slots, width)
+        rows = block[:, :width]
+        grads = block[:, width:]
         pre = jnp.dot(rows, half_in, preferred_element_type=jnp.float32)
         sig = jax.nn.sigmoid(pre)
         hidden = (pre * sig).astype(jnp.bfloat16)

time: 585 us -> 567 us (0.969); the launches traced: 574 us -> 562 us
  waiting for transfers between devices: 266 us -> 329 us
  local copies, waits for them, and re-layouts: 104 us -> 44.3 us
    all_to_all x1, waiting for transfers between devices: 0.01 us -> 151 us  [body(): lax.all_to_all(send.reshape(expert_count, capacity, 2 * width), 'expert',...]
    ppermute x2 -> x1, waiting for transfers between devices: 266 us -> 132 us  [partner_2(): return lax.ppermute(block, axis, route)]
    slice x5 -> x4, local copies, waits for them, and re-layouts: 47 us -> 8.37 us  [the longest x2 5.26 us: body(): quarter_in = both[:size_in].reshape(quarter_in.shape)]
    all_gather x1, waiting for transfers between devices: 0.02 us -> 37.9 us  [body(): half_out = lax.all_gather(quarter_out, 'dx', axis=0, tiled=True)]
    another operation x8 -> x2, local copies, waits for them, and re-layouts: 37 us -> 3.83 us  [the longest x1 3.83 us: body(): both = jnp.concatenate([quarter_in.reshape(-1), quarter_out.reshape(-1)])]
    reshape x0 -> x2, local copies, waits for them, and re-layouts: none -> 16.9 us  [the longest x1 8.56 us: body(): recv = lax.all_to_all(send.reshape(expert_count, capacity, 2 * width), 'e...]
    reduce_scatter x1, waiting for transfers between devices: 0.01 us -> 7.93 us  [body(): lax.psum_scatter(term_in, 'dx', scatter_dimension=1, tiled=True)]
    all_to_all x1 -> x0, local copies, waits for them, and re-layouts: 5.96 us -> none  [body(): lax.all_to_all(send, 'expert', split_axis=0, concat_axis=0, tiled=True)]
  transfers between devices with their start and end apart: 9 -> 8, of which waited for: 2 -> 4; matrix products, arithmetic and copies ran while one was open for 24% -> 17% of each run, Pallas kernels for 0% -> 0%
where the time goes in v2:
time: 567 us; the launch traced here: 562 us
  waiting for transfers between devices  329 us (58%)
  blocking collectives  98.8 us (17%)
  matrix products  56.5 us (10%)
  local copies, waits for them, and re-layouts  44.3 us (8%)
  starting transfers between devices  14.6 us (3%)
  between operations  14.6 us (3%)
    all_to_all x1, waiting for transfers between devices, body(): lax.all_to_all(send.reshape(expert_count, capacity, 2 * width), 'expert',...  151 us
    ppermute x1, waiting for transfers between devices, partner_2(): return lax.ppermute(block, axis, route)  132 us
    all_to_all x1, blocking collectives, body(): lax.all_to_all(expert_out.reshape(expert_count, capacity, width), 'expert...  98.8 us
    all_gather x1, waiting for transfers between devices, body(): half_out = lax.all_gather(quarter_out, 'dx', axis=0, tiled=True)  37.9 us
    dot_general x2, matrix products, expert_pass(): lax.dot_general(rows, dpre, contract_first, preferred_element_type=jnp.fl...  22.4 us
    all_to_all x1, starting transfers between devices, body(): lax.all_to_all(send.reshape(expert_count, capacity, 2 * width), 'expert',...  13.7 us
  transfers between devices with their start and end apart: 8, of which 4 were waited for; matrix products, arithmetic and copies ran while one was open for 17% of the time, Pallas kernels for 0%

profile of v2, /device:TPU:192, one launch (start us, length us, event | category | flops | bytes accessed | tf_op | source)
XLA Modules:
  0.0 562.5 jit_solution(17764545580967884704)
XLA Ops:
  7.2 3.4 copy.12
  10.6 1.3 constant_dynamic-update-slice_fusion.1
  11.9 0.0 copy-start.1
  11.9 0.0 copy-start.4
  11.9 0.0 copy-start
  11.9 3.8 reshape_squeeze.7
  15.7 1.4 constant_dynamic-update-slice_fusion
  17.1 0.5 collective-permute-start
  17.6 0.0 copy-done.1
  17.7 0.0 copy-start.3
  17.7 0.0 copy-done.4
  17.7 1.9 gather_fusion
  19.6 0.6 reduce-window.6
  20.2 0.2 slice_reduce_fusion
  20.4 0.1 fusion.54
  20.5 0.0 copy-done
  20.6 2.0 multiply_convert_fusion
  22.5 0.0 copy-done.3
  22.5 3.7 convolution_convert_fusion
  26.2 8.3 %reshape.71 = bf16[64,6,7168]{2,1,0:T(8,128)(2,1)} reshape(bf16[384,7168]{1,0:T(8,128)(2,1)} %convolution_convert_fusion) | data formatting | bytes 11010048 | tf_op jit(solution)/shard_map/reshape | solution.py:60
  34.5 13.7 %all-to-all-start = ((bf16[64,6,7168]{2,1,0:T(8,128)(2,1)}), bf16[64,6,7168]{2,1,0:T(8,128)(2,1)}, u32[]{:S(2)}, u32[]{:S(2)}) async-start(bf16[64,6,7168]{2,1,0:T(8,128)(2,1)} %reshape.71), calls=%async_computation | async-start | bytes 14680064 | tf_op jit(solution)/shard_map/all_to_all | solution.py:59
  48.2 0.0 all-gather.3.cloned.1.call-start
  48.3 0.6 dynamic_slice.3
  49.5 132.3 %collective-permute-done = bf16[1835008]{0:T(1024)(128)(2,1)} collective-permute-done((bf16[1835008]{0:T(1024)(128)(2,1)}, bf16[1835008]{0:T(1024)(128)(2,1)}, u32[]{:S(2)}, u32[]{:S(2)}) %collective-permute-start) | collective-permute-done | bytes 3670048 | tf_op jit(solution)/shard_map/ppermute | solution.py:14
  181.8 2.3 broadcast_select_fusion
  184.1 1.5 fusion.59
  185.6 3.8 slice.48
  189.3 0.0 all-gather.3.cloned.1.call-update
  189.4 0.0 all-gather.5.cloned.1.call-start
  189.4 150.5 %all-to-all-done = bf16[64,6,7168]{2,1,0:T(8,128)(2,1)} async-done(((bf16[64,6,7168]{2,1,0:T(8,128)(2,1)}), bf16[64,6,7168]{2,1,0:T(8,128)(2,1)}, u32[]{:S(2)}, u32[]{:S(2)}) %all-to-all-start) | async-done | bytes 5505056 | tf_op jit(solution)/shard_map/all_to_all | solution.py:59
  339.9 8.6 %reshape.72 = bf16[384,7168]{1,0:T(8,128)(2,1)} reshape(bf16[64,6,7168]{2,1,0:T(8,128)(2,1)} %all-to-all-done) | data formatting | bytes 11010048 | tf_op jit(solution)/shard_map/reshape | solution.py:62
  348.5 0.0 collective-permute-start.1
  348.5 2.9 slice.50
  351.4 0.0 all-gather.5.cloned.1.call-update
  351.4 0.2 reduce-scatter.5.cloned.1.call-start
  351.7 0.0 all-gather.3.cloned.1.call-done
  351.7 4.4 fusion.19
  356.2 0.0 copy-start.2
  356.2 4.1 fusion.10
  360.2 0.0 collective-permute-done.1
  360.2 0.0 copy-done.2
  360.3 3.4 fusion.15
  363.6 6.2 %add_convert_fusion = bf16[512,3584]{1,0:T(8,128)(2,1)} fusion(f32[512,3584]{1,0:T(8,128)S(1)} %fusion.10, bf16[384,7168]{1,0:T(8,128)(2,1)} %collective-permute-done.1, f32[384,512]{1,0:T(8,128)S(1)} %fusion.15), kind=kOutput, calls=%fused_computation.2 | convolution fusion | flops 1413939200 | bytes 14548992 | tf_op jit(solution)/shard_map/dot_general | solution.py:78
  369.8 0.0 reduce-scatter.5.cloned.1.call-update
  369.9 0.0 reduce-scatter.3.cloned.1.call-start
  369.9 37.9 %all-gather.5.cloned.1.call-done = bf16[512,3584]{1,0:T(8,128)(2,1)} async-done(((bf16[256,3584]{1,0:T(8,128)(2,1)}), bf16[512,3584]{1,0:T(8,128)(2,1)}) %all-gather.5.cloned.1.call-update) | async-done | bytes 3670032 | tf_op jit(solution)/shard_map/all_gather | solution.py:43
  407.8 5.3 convolution_convert_fusion.1
  413.1 0.0 collective-permute-start.2
  413.1 10.4 %fusion.17 = f32[3584,512]{1,0:T(8,128)} fusion(bf16[384,7168]{1,0:T(8,128)(2,1)} %reshape.72, bf16[512,3584]{1,0:T(8,128)(2,1)} %all-gather.5.cloned.1.call-done, f32[384,512]{1,0:T(8,128)S(1)} %fusion.19), kind=kOutput, calls=%fused_computation.26 | convolution fusion | flops 2820341760 | bytes 17301504 | tf_op jit(solution)/shard_map/dot_general | solution.py:77
  423.5 11.9 %add_convert_fusion.1 = bf16[3584,512]{1,0:T(8,128)(2,1)} fusion(f32[3584,512]{1,0:T(8,128)} %fusion.17, bf16[384,7168]{1,0:T(8,128)(2,1)} %collective-permute-done.1, bf16[512,3584]{1,0:T(8,128)(2,1)} %all-gather.5.cloned.1.call-done, f32[384,512]{1,0:T(8,128)S(1)} %fusion.15), kind=kOutput, calls=%fused_computation.3 | convolution fusion | flops 2824011776 | bytes 20971520 | tf_op jit(solution)/shard_map/dot_general | solution.py:77
  435.5 0.0 reduce-scatter.3.cloned.1.call-update
  435.5 0.0 collective-permute-done.2
  435.5 4.7 fusion
  440.2 2.7 reshape.73
  442.9 98.8 %all_to_all.10 = bf16[64,6,3584]{2,1,0:T(8,128)(2,1)} all-to-all(bf16[64,6,3584]{2,1,0:T(8,128)(2,1)} %reshape.73), channel_id=1, replica_groups=mesh['dx'=2,'dc'=2,'expert'=64] {'expert'}, dimensions={0} | all-to-all | bytes 5505024 | tf_op jit(solution)/shard_map/all_to_all | solution.py:91
  541.6 4.0 reshape.74
  545.6 2.4 fusion.3
  548.0 0.0 reduce-scatter.5.cloned.1.call-done
  548.0 7.9 %reduce-scatter.3.cloned.1.call-done = bf16[3584,256]{1,0:T(8,128)(2,1)} async-done(((bf16[3584,512]{1,0:T(8,128)(2,1)}), bf16[3584,256]{1,0:T(8,128)(2,1)}) %reduce-scatter.3.cloned.1.call-update) | async-done | bytes 1835024 | tf_op jit(solution)/shard_map/reduce_scatter | solution.py:88
  (7 shorter events, 0.1 us)
Async XLA Ops:
  11.9 5.8 %copy-start.1 = (s32[256,1]{0,1:T(1,128)S(1)}, s32[256,1]{0,1:T(1,128)}, u32[]{:S(2)}) copy-start(s32[256,1]{0,1:T(1,128)} %param.9) | copy-start | bytes 3076
  11.9 5.8 %copy-start.4 = (s32[64]{0:T(128)S(1)}, s32[64]{0:T(128)}, u32[]{:S(2)}) copy-start(s32[64]{0:T(128)} %param.11) | copy-start | bytes 772
  11.9 8.7 %copy-start = (f32[256,1]{0,1:T(1,128)S(1)}, f32[256,1]{0,1:T(1,128)}, u32[]{:S(2)}) copy-start(f32[256,1]{0,1:T(1,128)} %param.10) | copy-start | bytes 3076
  17.1 164.7 %collective-permute-start = (bf16[1835008]{0:T(1024)(128)(2,1)}, bf16[1835008]{0:T(1024)(128)(2,1)}, u32[]{:S(2)}, u32[]{:S(2)}) collective-permute-start(bf16[1835008]{0:T(1024)(128)(2,1)} %constant_dynamic-update-slice_fusion), channel_id=1, source_target_pairs={{0,32},{32,0},{1,33},{33,1},{2,34},{34,2},{3,35},{35,3},{4,36},{36... | collective-permute-start | bytes 11010056 | tf_op jit(solution)/shard_map/ppermute | solution.py:14
  17.7 4.9 copy-start.3
  34.5 305.4 %all-to-all-start = ((bf16[64,6,7168]{2,1,0:T(8,128)(2,1)}), bf16[64,6,7168]{2,1,0:T(8,128)(2,1)}, u32[]{:S(2)}, u32[]{:S(2)}) async-start(bf16[64,6,7168]{2,1,0:T(8,128)(2,1)} %reshape.71), calls=%async_computation | async-start | bytes 14680064 | tf_op jit(solution)/shard_map/all_to_all | solution.py:59
  48.2 303.5 %all-gather.3.cloned.1.call-start = ((), (), s32[]{:S(2)}) async-start(), calls=%async_computation.4 | async-start | bytes 5505024 | tf_op jit(solution)/shard_map/all_gather | solution.py:42
  189.4 218.5 %all-gather.5.cloned.1.call-start = ((), (), s32[]{:S(2)}) async-start(), calls=%async_computation.5 | async-start | bytes 5505024 | tf_op jit(solution)/shard_map/all_gather | solution.py:43
  348.5 11.7 %collective-permute-start.1 = (bf16[384,7168]{1,0:T(8,128)(2,1)}, bf16[384,7168]{1,0:T(8,128)(2,1)}, u32[]{:S(2)}, u32[]{:S(2)}) collective-permute-start(bf16[384,7168]{1,0:T(8,128)(2,1)} %reshape.72), channel_id=1, source_target_pairs={{0,64},{64,0},{1,65},{65,1},{2,66},{66,2},{3,67},{67,3},{4,68},{68... | collective-permute-start | bytes 16515080 | tf_op jit(solution)/shard_map/ppermute | solution.py:18
  351.4 196.5 %reduce-scatter.5.cloned.1.call-start = ((), (), s32[]{:S(2)}) async-start(), calls=%async_computation.7 | async-start | bytes 5505024 | tf_op jit(solution)/shard_map/reduce_scatter | solution.py:89
  356.2 4.1 copy-start.2
  369.9 186.1 %reduce-scatter.3.cloned.1.call-start = ((), (), s32[]{:S(2)}) async-start(), calls=%async_computation.6 | async-start | bytes 5505024 | tf_op jit(solution)/shard_map/reduce_scatter | solution.py:88
  413.1 22.4 %collective-permute-start.2 = (bf16[384,3584]{1,0:T(8,128)(2,1)}, bf16[384,3584]{1,0:T(8,128)(2,1)}, u32[]{:S(2)}, u32[]{:S(2)}) collective-permute-start(bf16[384,3584]{1,0:T(8,128)(2,1)} %convolution_convert_fusion.1), channel_id=1, source_target_pairs={{0,64},{64,0},{1,65},{65,1},{2,66},{66,2},{3,67},{67,3},{4,68},{68... | collective-permute-start | bytes 8257544 | tf_op jit(solution)/shard_map/ppermute | solution.py:18
Sparse Core Ops, SparseCore 0:
  189.5 88.5 all-gather.2
  351.6 56.2 all-gather.4
  410.9 70.9 reduce-scatter.4
  485.0 70.8 reduce-scatter.2

commit v3 on v2

--- a/solution.py
+++ b/solution.py
@@ -29,21 +29,20 @@
     route_count = local_tokens * top_count
     slots = expert_count * capacity
     lanes = jnp.arange(expert_count, dtype=jnp.int32)
-    partner = jnp.bitwise_xor(lanes, half_axis * pair_flags)
     flagged = pair_flags[own_index] == 1
 
     quarter_in = w_in[0]
     quarter_out = w_out[0]
     size_in = quarter_in.size
     both = jnp.concatenate([quarter_in.reshape(-1), quarter_out.reshape(-1)])
-    both = jnp.where(flagged, partner_2(both, "expert", pair_bit), both)
-    quarter_in = both[:size_in].reshape(quarter_in.shape)
-    quarter_out = both[size_in:].reshape(quarter_out.shape)
-    half_in = lax.all_gather(quarter_in, "dx", axis=1, tiled=True)
-    half_out = lax.all_gather(quarter_out, "dx", axis=0, tiled=True)
+    both = lax.all_gather(both, "dx", axis=0, tiled=False)
+    pair_count = both.shape[0]
+    half_in = both[:, :size_in].reshape((pair_count,) + quarter_in.shape)
+    half_in = jnp.moveaxis(half_in, 0, 1).reshape(quarter_in.shape[0], -1)
+    half_out = both[:, size_in:].reshape(pair_count * quarter_out.shape[0], -1)
 
     flat_ids = expert_ids.reshape(-1)
-    target_of = partner[flat_ids]
+    target_of = flat_ids
     onehot = (target_of[:, None] == lanes[None, :]).astype(jnp.int32)
     position = jnp.sum(jnp.cumsum(onehot, axis=0) * onehot, axis=1) - 1
     slot_of = target_of * capacity + position
@@ -87,6 +86,9 @@
     term_out = (outg_own + outg_other).astype(jnp.bfloat16)
     grad_quarter_in = lax.psum_scatter(term_in, "dx", scatter_dimension=1, tiled=True)
     grad_quarter_out = lax.psum_scatter(term_out, "dx", scatter_dimension=0, tiled=True)
+    their_in, their_out = partner_2((grad_quarter_in, grad_quarter_out), "expert", pair_bit)
+    grad_quarter_in = jnp.where(flagged, their_in, grad_quarter_in)
+    grad_quarter_out = jnp.where(flagged, their_out, grad_quarter_out)
 
     returned = lax.all_to_all(
         expert_out.reshape(expert_count, capacity, width), "expert",

time: 567 us -> 577 us (1.018)
  blocking collectives: 98.8 us -> 0 us
  waiting for transfers between devices: 329 us -> 389 us
  local copies, waits for them, and re-layouts: 44.3 us -> 63.8 us
  starting transfers between devices: 14.6 us -> 30.5 us
  other arithmetic: 5 us -> 16.2 us
    all_to_all x0 -> x1, waiting for transfers between devices: none -> 154 us  [body(): lax.all_to_all(expert_out.reshape(expert_count, capacity, width), 'expert...]
    all_to_all x1, waiting for transfers between devices: 151 us -> 0.01 us  [body(): lax.all_to_all(send.reshape(expert_count, capacity, 2 * width), 'expert',...]
    ppermute x1 -> x2, waiting for transfers between devices: 132 us -> 0.01 us  [partner_2(): return lax.ppermute(block, axis, route)]
    all_gather x2 -> x1, waiting for transfers between devices: 37.9 us -> 151 us  [body(): both = lax.all_gather(both, 'dx', axis=0, tiled=False)]
    all_to_all x1 -> x0, blocking collectives: 98.8 us -> none  [body(): lax.all_to_all(expert_out.reshape(expert_count, capacity, width), 'expert...]
    reduce_scatter x1, waiting for transfers between devices: 7.93 us -> 83.1 us  [body(): lax.psum_scatter(term_in, 'dx', scatter_dimension=1, tiled=True)]
    all_to_all x0 -> x1, starting transfers between devices: none -> 12.2 us  [body(): lax.all_to_all(expert_out.reshape(expert_count, capacity, width), 'expert...]
    concatenate x0 -> x1, other arithmetic: none -> 8.35 us  [body(): both = jnp.concatenate([quarter_in.reshape(-1), quarter_out.reshape(-1)])]
  transfers between devices with their start and end apart: 8 -> 9, of which waited for: 4 -> 4; matrix products, arithmetic and copies ran while one was open for 17% -> 17% of each run, Pallas kernels for 0% -> 0%
where the time goes in v3:
time: 577 us; the launch traced here: 568 us
  waiting for transfers between devices  389 us (67%)
  local copies, waits for them, and re-layouts  63.8 us (11%)
  matrix products  53.5 us (9%)
  starting transfers between devices  30.5 us (5%)
  other arithmetic  16.2 us (3%)
  between operations  15 us (3%)
    all_to_all x1, waiting for transfers between devices, body(): lax.all_to_all(expert_out.reshape(expert_count, capacity, width), 'expert...  154 us
    all_gather x1, waiting for transfers between devices, body(): both = lax.all_gather(both, 'dx', axis=0, tiled=False)  151 us
    reduce_scatter x1, waiting for transfers between devices, body(): lax.psum_scatter(term_in, 'dx', scatter_dimension=1, tiled=True)  83.1 us
    dot_general x2, matrix products, expert_pass(): lax.dot_general(rows, dpre, contract_first, preferred_element_type=jnp.fl...  21.8 us
    all_to_all x1, starting transfers between devices, body(): lax.all_to_all(send.reshape(expert_count, capacity, 2 * width), 'expert',...  12.3 us
    all_to_all x1, starting transfers between devices, body(): lax.all_to_all(expert_out.reshape(expert_count, capacity, width), 'expert...  12.2 us
  transfers between devices with their start and end apart: 9, of which 4 were waited for; matrix products, arithmetic and copies ran while one was open for 17% of the time, Pallas kernels for 0%

profile of v3, /device:TPU:192, one launch (start us, length us, event | category | flops | bytes accessed | tf_op | source)
XLA Modules:
  0.0 567.7 jit_solution(16947864920074192768)
XLA Ops:
  7.2 0.0 copy-start.4
  7.2 0.8 fusion.54
  8.0 0.6 reduce-window.6
  8.6 0.2 slice_reduce_fusion
  8.8 0.8 fusion.53
  9.6 0.7 add_add_fusion
  10.3 1.9 multiply_convert_fusion
  12.3 0.0 copy-done.4
  12.3 3.7 convolution_convert_fusion
  15.9 8.2 %reshape.67 = bf16[64,6,7168]{2,1,0:T(8,128)(2,1)} reshape(bf16[384,7168]{1,0:T(8,128)(2,1)} %convolution_convert_fusion) | data formatting | bytes 11010048 | tf_op jit(solution)/shard_map/reshape | solution.py:59
  24.2 12.3 %all-to-all-start = ((bf16[64,6,7168]{2,1,0:T(8,128)(2,1)}), bf16[64,6,7168]{2,1,0:T(8,128)(2,1)}, u32[]{:S(2)}, u32[]{:S(2)}) async-start(bf16[64,6,7168]{2,1,0:T(8,128)(2,1)} %reshape.67), calls=%async_computation | async-start | bytes 14680064 | tf_op jit(solution)/shard_map/all_to_all | solution.py:58
  36.5 0.0 all-gather.3.cloned.1.call-start
  36.6 3.4 copy.16
  39.9 4.6 reshape_squeeze.7
  44.6 8.3 %pad_maximum_fusion = bf16[1835008]{0:T(1024)(128)(2,1)} fusion(bf16[917504]{0:T(1024)(128)(2,1)} %reshape_squeeze.7, bf16[917504]{0:T(1024)(128)(2,1)S(1)} %bitcast.44), kind=kLoop, calls=%fused_computation.13 | loop fusion | flops 7340032 | bytes 7340032 | tf_op jit(solution)/shard_map/concatenate | solution.py:37
  52.9 0.0 all-gather.3.cloned.1.call-update
  53.0 0.2 reduce-scatter.5.cloned.1.call-start
  53.2 151.4 %all-gather.3.cloned.1.call-done = bf16[3670016]{0:T(1024)(128)(2,1)} async-done(((bf16[1835008]{0:T(1024)(128)(2,1)}), bf16[3670016]{0:T(1024)(128)(2,1)}) %all-gather.3.cloned.1.call-update) | async-done | bytes 7340048 | tf_op jit(solution)/shard_map/all_gather | solution.py:38
  204.6 7.8 %reshape.74 = bf16[2,1835008]{1,0:T(2,128)(2,1)} reshape(bf16[3670016]{0:T(1024)(128)(2,1)} %all-gather.3.cloned.1.call-done) | data formatting | bytes 14680064 | tf_op jit(solution)/shard_map/all_gather | solution.py:38
  212.4 0.0 all-to-all-done
  212.4 8.6 %reshape.68 = bf16[384,7168]{1,0:T(8,128)(2,1)} reshape(bf16[64,6,7168]{2,1,0:T(8,128)(2,1)} %all-to-all-done) | data formatting | bytes 11010048 | tf_op jit(solution)/shard_map/reshape | solution.py:61
  221.0 0.1 collective-permute-start
  221.0 7.2 %fusion.59 = (bf16[2,917504]{1,0:T(2,128)(2,1)S(1)}, bf16[2,917504]{1,0:T(2,128)(2,1)}) fusion(bf16[2,1835008]{1,0:T(2,128)(2,1)} %reshape.74), kind=kLoop, calls=%fused_computation.65 | loop fusion | bytes 14680064 | tf_op jit(solution)/shard_map/slice | solution.py:40
  228.2 2.3 copy.20
  230.5 6.1 %copy.14 = bf16[3584,2,256]{0,2,1:T(8,128)(2,1)} copy(bf16[3584,2,256]{2,0,1:T(8,128)(2,1)} %bitcast.41) | data formatting | bytes 7340032 | tf_op jit(solution)/shard_map/transpose | solution.py:41
  236.6 4.6 fusion.18
  241.2 0.0 slice-done
  241.3 0.0 slice-done.1
  241.3 0.0 copy-start
  241.3 2.2 fusion.9
  243.4 0.0 collective-permute-done
  243.5 0.0 copy-done
  243.5 3.4 fusion.14
  246.9 5.8 %add_convert_fusion = bf16[512,3584]{1,0:T(8,128)(2,1)} fusion(f32[512,3584]{1,0:T(8,128)S(1)} %fusion.9, bf16[384,7168]{1,0:T(8,128)(2,1)} %collective-permute-done, f32[384,512]{1,0:T(8,128)S(1)} %fusion.14), kind=kOutput, calls=%fused_computation.1 | convolution fusion | flops 1413939200 | bytes 14548992 | tf_op jit(solution)/shard_map/dot_general | solution.py:77
  252.7 0.0 reduce-scatter.5.cloned.1.call-update
  252.7 0.3 reduce-scatter.3.cloned.1.call-start
  253.0 7.5 %reshape.71 = bf16[512,3584]{1,0:T(8,128)(2,1)} reshape(bf16[2,917504]{1,0:T(2,128)(2,1)} %get-tuple-element.4) | data formatting | bytes 7340032 | tf_op jit(solution)/shard_map/reshape | solution.py:42
  260.4 10.3 %fusion.16 = f32[3584,512]{1,0:T(8,128)} fusion(bf16[384,7168]{1,0:T(8,128)(2,1)} %reshape.68, bf16[512,3584]{1,0:T(8,128)(2,1)} %reshape.71, f32[384,512]{1,0:T(8,128)S(1)} %fusion.18), kind=kOutput, calls=%fused_computation.25 | convolution fusion | flops 2820341760 | bytes 17301504 | tf_op jit(solution)/shard_map/dot_general | solution.py:76
  270.7 5.2 convolution_convert_fusion.1
  275.9 0.7 collective-permute-start.1
  276.6 11.5 %add_convert_fusion.1 = bf16[3584,512]{1,0:T(8,128)(2,1)} fusion(f32[3584,512]{1,0:T(8,128)} %fusion.16, bf16[384,7168]{1,0:T(8,128)(2,1)} %collective-permute-done, bf16[512,3584]{1,0:T(8,128)(2,1)} %reshape.71, f32[384,512]{1,0:T(8,128)S(1)} %fusion.14), kind=kOutput, calls=%fused_computation.2 | convolution fusion | flops 2824011776 | bytes 20971520 | tf_op jit(solution)/shard_map/dot_general | solution.py:76
  288.1 0.0 reduce-scatter.3.cloned.1.call-update
  288.1 0.0 collective-permute-done.1
  288.1 4.5 add_convert_fusion.2
  292.7 2.7 reshape.72
  295.3 12.2 %all-to-all-start.1 = ((bf16[64,6,3584]{2,1,0:T(8,128)(2,1)}), bf16[64,6,3584]{2,1,0:T(8,128)(2,1)}, u32[]{:S(2)}, u32[]{:S(2)}) async-start(bf16[64,6,3584]{2,1,0:T(8,128)(2,1)} %reshape.72), calls=%async_computation.1 | async-start | bytes 7340032 | tf_op jit(solution)/shard_map/all_to_all | solution.py:93
  307.6 0.0 copy-start.3
  307.6 0.1 reduce-scatter.5.cloned.1.call-done
  307.7 2.2 collective-permute-start.3
  309.9 83.1 %reduce-scatter.3.cloned.1.call-done = bf16[3584,256]{1,0:T(8,128)(2,1)} async-done(((bf16[3584,512]{1,0:T(8,128)(2,1)}), bf16[3584,256]{1,0:T(8,128)(2,1)}) %reduce-scatter.3.cloned.1.call-update) | async-done | bytes 1835024 | tf_op jit(solution)/shard_map/reduce_scatter | solution.py:87
  392.9 2.5 collective-permute-start.2
  395.5 0.0 copy-done.5
  395.5 0.6 dynamic_slice.3
  396.7 154.0 %all-to-all-done.1 = bf16[64,6,3584]{2,1,0:T(8,128)(2,1)} async-done(((bf16[64,6,3584]{2,1,0:T(8,128)(2,1)}), bf16[64,6,3584]{2,1,0:T(8,128)(2,1)}, u32[]{:S(2)}, u32[]{:S(2)}) %all-to-all-start.1) | async-done | bytes 2752544 | tf_op jit(solution)/shard_map/all_to_all | solution.py:93
  550.7 4.0 reshape.73
  554.7 0.0 copy-done.3
  554.7 0.0 copy-start.1
  554.7 2.4 fusion.2
  557.1 0.0 collective-permute-done.3
  557.1 0.0 copy-done.1
  557.1 1.5 select_bitcast_fusion
  558.6 0.0 collective-permute-done.2
  558.6 0.7 copy-done.2
  559.3 1.5 select_bitcast_fusion.1
  (7 shorter events, 0.0 us)
Async XLA Ops:
  7.2 5.1 copy-start.4
  24.2 188.2 %all-to-all-start = ((bf16[64,6,7168]{2,1,0:T(8,128)(2,1)}), bf16[64,6,7168]{2,1,0:T(8,128)(2,1)}, u32[]{:S(2)}, u32[]{:S(2)}) async-start(bf16[64,6,7168]{2,1,0:T(8,128)(2,1)} %reshape.67), calls=%async_computation | async-start | bytes 14680064 | tf_op jit(solution)/shard_map/all_to_all | solution.py:58
  36.5 168.1 %all-gather.3.cloned.1.call-start = ((), (), s32[]{:S(2)}) async-start(), calls=%async_computation.6 | async-start | bytes 11010048 | tf_op jit(solution)/shard_map/all_gather | solution.py:38
  53.0 254.7 %reduce-scatter.5.cloned.1.call-start = ((), (), s32[]{:S(2)}) async-start(), calls=%async_computation.5 | async-start | bytes 5505024 | tf_op jit(solution)/shard_map/reduce_scatter | solution.py:88
  221.0 22.5 %collective-permute-start = (bf16[384,7168]{1,0:T(8,128)(2,1)}, bf16[384,7168]{1,0:T(8,128)(2,1)}, u32[]{:S(2)}, u32[]{:S(2)}) collective-permute-start(bf16[384,7168]{1,0:T(8,128)(2,1)} %reshape.68), channel_id=1, source_target_pairs={{0,64},{64,0},{1,65},{65,1},{2,66},{66,2},{3,67},{67,3},{4,68},{68... | collective-permute-start | bytes 16515080 | tf_op jit(solution)/shard_map/ppermute | solution.py:18
  230.5 10.7 %slice-start = ((s8[5505024]{0:T(1024)(128)(4,1)}), s8[1310720]{0:T(1024)(128)(4,1)S(1)}, s32[]{:S(2)}) async-start(s8[5505024]{0:T(1024)(128)(4,1)} %bitcast.42), calls=%async_computation.7 | async-start | bytes 2621440
  236.6 4.6 slice-start.1
  241.3 2.2 copy-start
  252.7 140.2 %reduce-scatter.3.cloned.1.call-start = ((), (), s32[]{:S(2)}) async-start(), calls=%async_computation.4 | async-start | bytes 5505024 | tf_op jit(solution)/shard_map/reduce_scatter | solution.py:87
  275.9 12.2 %collective-permute-start.1 = (bf16[384,3584]{1,0:T(8,128)(2,1)}, bf16[384,3584]{1,0:T(8,128)(2,1)}, u32[]{:S(2)}, u32[]{:S(2)}) collective-permute-start(bf16[384,3584]{1,0:T(8,128)(2,1)} %convolution_convert_fusion.1), channel_id=1, source_target_pairs={{0,64},{64,0},{1,65},{65,1},{2,66},{66,2},{3,67},{67,3},{4,68},{68... | collective-permute-start | bytes 8257544 | tf_op jit(solution)/shard_map/ppermute | solution.py:18
  295.3 100.1 %copy-start.5 = (s32[64]{0:T(128)S(1)}, s32[64]{0:T(128)}, u32[]{:S(2)}) copy-start(s32[64]{0:T(128)} %param.11) | copy-start | bytes 772
  295.3 255.4 %all-to-all-start.1 = ((bf16[64,6,3584]{2,1,0:T(8,128)(2,1)}), bf16[64,6,3584]{2,1,0:T(8,128)(2,1)}, u32[]{:S(2)}, u32[]{:S(2)}) async-start(bf16[64,6,3584]{2,1,0:T(8,128)(2,1)} %reshape.72), calls=%async_computation.1 | async-start | bytes 7340032 | tf_op jit(solution)/shard_map/all_to_all | solution.py:93
  307.6 247.1 %copy-start.3 = (f32[256,1]{0,1:T(1,128)S(1)}, f32[256,1]{0,1:T(1,128)}, u32[]{:S(2)}) copy-start(f32[256,1]{0,1:T(1,128)} %param.10) | copy-start | bytes 3076
  307.7 249.4 %collective-permute-start.3 = (bf16[256,3584]{1,0:T(8,128)(2,1)}, bf16[256,3584]{1,0:T(8,128)(2,1)}, u32[]{:S(2)}, u32[]{:S(2)}) collective-permute-start(bf16[256,3584]{1,0:T(8,128)(2,1)} %reduce-scatter.5.cloned.1.call-done), channel_id=1, source_target_pairs={{0,32},{32,0},{1,33},{33,1},{2,34},{34,2},{3,35},{35,3},{4,36},{36... | collective-permute-start | bytes 5505032 | tf_op jit(solution)/shard_map/ppermute | solution.py:14
  392.9 165.7 %collective-permute-start.2 = (bf16[3584,256]{1,0:T(8,128)(2,1)}, bf16[3584,256]{1,0:T(8,128)(2,1)}, u32[]{:S(2)}, u32[]{:S(2)}) collective-permute-start(bf16[3584,256]{1,0:T(8,128)(2,1)} %reduce-scatter.3.cloned.1.call-done), channel_id=1, source_target_pairs={{0,32},{32,0},{1,33},{33,1},{2,34},{34,2},{3,35},{35,3},{4,36},{36... | collective-permute-start | bytes 5505032 | tf_op jit(solution)/shard_map/ppermute | solution.py:14
  554.7 2.4 copy-start.1
  557.1 2.2 copy-start.2
Sparse Core Ops, SparseCore 0:
  53.1 151.4 all-gather.2
  252.8 54.8 reduce-scatter.4
  310.3 82.5 reduce-scatter.2

commit v4 on v2

--- a/solution.py
+++ b/solution.py
@@ -32,15 +32,14 @@
     partner = jnp.bitwise_xor(lanes, half_axis * pair_flags)
     flagged = pair_flags[own_index] == 1
 
-    quarter_in = w_in[0]
+    quarter_in = w_in[0].T
     quarter_out = w_out[0]
-    size_in = quarter_in.size
-    both = jnp.concatenate([quarter_in.reshape(-1), quarter_out.reshape(-1)])
-    both = jnp.where(flagged, partner_2(both, "expert", pair_bit), both)
-    quarter_in = both[:size_in].reshape(quarter_in.shape)
-    quarter_out = both[size_in:].reshape(quarter_out.shape)
-    half_in = lax.all_gather(quarter_in, "dx", axis=1, tiled=True)
-    half_out = lax.all_gather(quarter_out, "dx", axis=0, tiled=True)
+    their_in, their_out = partner_2((quarter_in, quarter_out), "expert", pair_bit)
+    quarter_in = jnp.where(flagged, their_in, quarter_in)
+    quarter_out = jnp.where(flagged, their_out, quarter_out)
+    halves = lax.all_gather(jnp.stack([quarter_in, quarter_out]), "dx", axis=1, tiled=True)
+    half_in = halves[0]
+    half_out = halves[1]
 
     flat_ids = expert_ids.reshape(-1)
     target_of = partner[flat_ids]
@@ -68,13 +67,13 @@
     def expert_pass(block):
         rows = block[:, :width]
         grads = block[:, width:]
-        pre = jnp.dot(rows, half_in, preferred_element_type=jnp.float32)
+        pre = lax.dot_general(rows, half_in, contract_last, preferred_element_type=jnp.float32)
         sig = jax.nn.sigmoid(pre)
         hidden = (pre * sig).astype(jnp.bfloat16)
         out = jnp.dot(hidden, half_out, preferred_element_type=jnp.float32)
         dhid = lax.dot_general(grads, half_out, contract_last, preferred_element_type=jnp.float32)
         dpre = (dhid * sig * (1.0 + pre * (1.0 - sig))).astype(jnp.bfloat16)
-        term_in = lax.dot_general(rows, dpre, contract_first, preferred_element_type=jnp.float32)
+        term_in = lax.dot_general(dpre, rows, contract_first, preferred_element_type=jnp.float32)
         term_out = lax.dot_general(hidden, grads, contract_first, preferred_element_type=jnp.float32)
         return out, term_in, term_out
 
@@ -83,10 +82,10 @@
     out_own, in_own, outg_own = expert_pass(recv)
     expert_out = (out_own + back.astype(jnp.float32)).astype(jnp.bfloat16)
 
-    term_in = (in_own + in_other).astype(jnp.bfloat16)
-    term_out = (outg_own + outg_other).astype(jnp.bfloat16)
-    grad_quarter_in = lax.psum_scatter(term_in, "dx", scatter_dimension=1, tiled=True)
-    grad_quarter_out = lax.psum_scatter(term_out, "dx", scatter_dimension=0, tiled=True)
+    terms = jnp.stack([in_own + in_other, outg_own + outg_other]).astype(jnp.bfloat16)
+    grad_quarters = lax.psum_scatter(terms, "dx", scatter_dimension=1, tiled=True)
+    grad_quarter_in = grad_quarters[0].T
+    grad_quarter_out = grad_quarters[1]
 
     returned = lax.all_to_all(
         expert_out.reshape(expert_count, capacity, width), "expert",

time: 567 us -> 652 us (1.15)
  waiting for transfers between devices: 329 us -> 413 us
  local copies, waits for them, and re-layouts: 44.3 us -> 34.8 us
  other arithmetic: 5 us -> 13.6 us
    ppermute x1 -> x2, waiting for transfers between devices: 132 us -> 294 us  [partner_2(): return lax.ppermute(block, axis, route)]
    all_to_all x1, waiting for transfers between devices: 151 us -> 12 us  [body(): lax.all_to_all(send.reshape(expert_count, capacity, 2 * width), 'expert',...]
    all_gather x2 -> x1, waiting for transfers between devices: 37.9 us -> 87.8 us  [body(): lax.all_gather(jnp.stack([quarter_in, quarter_out]), 'dx', axis=1, tiled=...]
    another operation x2 -> x6, other arithmetic: 0.65 us -> 10 us  [the longest x3 5.49 us: body(): jnp.stack([quarter_in, quarter_out])]
    reduce_scatter x2 -> x1, waiting for transfers between devices: 7.93 us -> 13.8 us  [body(): lax.psum_scatter(terms, 'dx', scatter_dimension=1, tiled=True)]
  transfers between devices with their start and end apart: 8 -> 7, of which waited for: 4 -> 6; matrix products, arithmetic and copies ran while one was open for 17% -> 8% of each run, Pallas kernels for 0% -> 0%
where the time goes in v4:
time: 652 us; the launch traced here: 648 us
  waiting for transfers between devices  413 us (63%)
  blocking collectives  98.5 us (15%)
  matrix products  55.5 us (9%)
  local copies, waits for them, and re-layouts  34.8 us (5%)
  starting transfers between devices  18.5 us (3%)
  between operations  14.9 us (2%)
  other arithmetic  13.6 us (2%)
    ppermute x2, waiting for transfers between devices, partner_2(): return lax.ppermute(block, axis, route)  294 us
    all_to_all x1, blocking collectives, body(): lax.all_to_all(expert_out.reshape(expert_count, capacity, width), 'expert...  98.5 us
    all_gather x1, waiting for transfers between devices, body(): lax.all_gather(jnp.stack([quarter_in, quarter_out]), 'dx', axis=1, tiled=...  87.8 us
    dot_general x2, matrix products, expert_pass(): lax.dot_general(dpre, rows, contract_first, preferred_element_type=jnp.fl...  21.7 us
    reduce_scatter x1, waiting for transfers between devices, body(): lax.psum_scatter(terms, 'dx', scatter_dimension=1, tiled=True)  13.8 us
  transfers between devices with their start and end apart: 7, of which 6 were waited for; matrix products, arithmetic and copies ran while one was open for 8% of the time, Pallas kernels for 0%

profile of v4, /device:TPU:192, one launch (start us, length us, event | category | flops | bytes accessed | tf_op | source)
XLA Modules:
  0.0 648.3 jit_solution(10825068240103264271)
XLA Ops:
  7.2 0.0 copy-start.4
  7.2 0.8 compare_select_fusion
  8.0 0.7 multiply_xor_fusion
  8.7 1.9 gather_fusion
  10.5 0.6 reduce-window.6
  11.2 0.2 slice_reduce_fusion
  11.4 0.1 fusion.56
  11.5 2.0 multiply_convert_fusion
  13.5 0.0 copy-done.4
  13.5 3.7 convolution_convert_fusion
  17.2 8.3 %reshape.53 = bf16[64,6,7168]{2,1,0:T(8,128)(2,1)} reshape(bf16[384,7168]{1,0:T(8,128)(2,1)} %convolution_convert_fusion) | data formatting | bytes 11010048 | tf_op jit(solution)/shard_map/reshape | solution.py:59
  25.5 12.3 %all-to-all-start = ((bf16[64,6,7168]{2,1,0:T(8,128)(2,1)}), bf16[64,6,7168]{2,1,0:T(8,128)(2,1)}, u32[]{:S(2)}, u32[]{:S(2)}) async-start(bf16[64,6,7168]{2,1,0:T(8,128)(2,1)} %reshape.53), calls=%async_computation | async-start | bytes 14680064 | tf_op jit(solution)/shard_map/all_to_all | solution.py:58
  37.8 0.0 copy-start.5
  37.8 0.0 all-gather.2.cloned.1.call-start
  37.9 2.8 copy.13
  40.6 2.2 collective-permute-start
  42.9 3.8 collective-permute-start.1
  46.7 0.0 copy-done.5
  46.7 0.0 copy-start.2
  46.7 0.6 dynamic_slice.3
  47.9 224.4 %collective-permute-done = bf16[256,3584]{1,0:T(8,128)(2,1)} collective-permute-done((bf16[256,3584]{1,0:T(8,128)(2,1)S(1)}, bf16[256,3584]{1,0:T(8,128)(2,1)}, u32[]{:S(2)}, u32[]{:S(2)}) %collective-permute-start) | collective-permute-done | bytes 1835040 | tf_op jit(solution)/shard_map/ppermute | solution.py:14
  272.3 1.7 select_bitcast_fusion.1
  274.0 69.4 %collective-permute-done.1 = bf16[256,3584]{1,0:T(8,128)(2,1)} collective-permute-done((bf16[256,3584]{1,0:T(8,128)(2,1)}, bf16[256,3584]{1,0:T(8,128)(2,1)}, u32[]{:S(2)}, u32[]{:S(2)}) %collective-permute-start.1) | collective-permute-done | bytes 1835040 | tf_op jit(solution)/shard_map/ppermute | solution.py:14
  343.5 0.0 copy-done.2
  343.5 1.7 select_bitcast_fusion
  345.2 2.1 pad_maximum_fusion.1
  347.3 0.0 all-gather.2.cloned.1.call-update
  347.3 0.0 reduce-scatter.2.cloned.1.call-start
  347.3 12.0 %all-to-all-done = bf16[64,6,7168]{2,1,0:T(8,128)(2,1)} async-done(((bf16[64,6,7168]{2,1,0:T(8,128)(2,1)}), bf16[64,6,7168]{2,1,0:T(8,128)(2,1)}, u32[]{:S(2)}, u32[]{:S(2)}) %all-to-all-start) | async-done | bytes 5505056 | tf_op jit(solution)/shard_map/all_to_all | solution.py:58
  359.4 8.6 %reshape.54 = bf16[384,7168]{1,0:T(8,128)(2,1)} reshape(bf16[64,6,7168]{2,1,0:T(8,128)(2,1)} %all-to-all-done) | data formatting | bytes 11010048 | tf_op jit(solution)/shard_map/reshape | solution.py:61
  367.9 0.0 collective-permute-start.2
  368.0 87.8 %all-gather.2.cloned.1.call-done = bf16[2,512,3584]{2,1,0:T(8,128)(2,1)} async-done(((bf16[2,256,3584]{2,1,0:T(8,128)(2,1)}), bf16[2,512,3584]{2,1,0:T(8,128)(2,1)}) %all-gather.2.cloned.1.call-update) | async-done | bytes 7340048 | tf_op jit(solution)/shard_map/all_gather | solution.py:40
  455.7 0.0 copy-start
  455.7 4.6 fusion.9
  460.3 0.0 copy-done
  460.4 5.1 fusion.13
  465.4 10.4 %fusion.19 = f32[512,3584]{1,0:T(8,128)} fusion(bf16[384,7168]{1,0:T(8,128)(2,1)} %reshape.54, bf16[2,512,3584]{2,1,0:T(8,128)(2,1)} %all-gather.2.cloned.1.call-done, f32[384,512]{1,0:T(8,128)S(1)} %fusion.9), kind=kOutput, calls=%fused_computation.31 | convolution fusion | flops 2820341760 | bytes 17301504 | tf_op jit(solution)/shard_map/dot_general | solution.py:76
  475.8 0.0 collective-permute-done.2
  475.8 4.5 fusion.8
  480.2 11.4 %fusion = bf16[1,512,3584]{2,1,0:T(8,128)(2,1)} fusion(f32[512,3584]{1,0:T(8,128)} %fusion.19, bf16[384,7168]{1,0:T(8,128)(2,1)} %collective-permute-done.2, bf16[2,512,3584]{2,1,0:T(8,128)(2,1)} %all-gather.2.cloned.1.call-done, f32[384,512]{1,0:T(8,128)S(1)} %fusion.8), kind=kOutput, calls=%fused_computation.7 | convolution fusion | flops 2824011776 | bytes 20971520 | tf_op jit(solution)/shard_map/dot_general | solution.py:76
  491.6 0.0 copy-start.1
  491.6 6.2 fusion.1
  497.8 0.0 copy-done.1
  497.8 3.9 pad_maximum_fusion
  501.7 0.0 reduce-scatter.2.cloned.1.call-update
  501.7 3.7 convolution_convert_fusion.1
  505.4 0.1 collective-permute-start.3
  505.5 5.1 collective-permute-done.3
  510.6 3.7 add_convert_fusion.2
  514.3 2.7 reshape.55
  516.9 98.5 %all_to_all.10 = bf16[64,6,3584]{2,1,0:T(8,128)(2,1)} all-to-all(bf16[64,6,3584]{2,1,0:T(8,128)(2,1)} %reshape.55), channel_id=1, replica_groups=mesh['dx'=2,'dc'=2,'expert'=64] {'expert'}, dimensions={0} | all-to-all | bytes 5505024 | tf_op jit(solution)/shard_map/all_to_all | solution.py:90
  615.4 0.0 copy-start.3
  615.5 4.0 reshape.56
  619.5 0.0 copy-done.3
  619.5 2.4 fusion.4
  621.9 13.8 %reduce-scatter.2.cloned.1.call-done = bf16[2,256,3584]{2,1,0:T(8,128)(2,1)} async-done(((bf16[2,512,3584]{2,1,0:T(8,128)(2,1)}), bf16[2,256,3584]{2,1,0:T(8,128)(2,1)}) %reduce-scatter.2.cloned.1.call-update) | async-done | bytes 3670032 | tf_op jit(solution)/shard_map/reduce_scatter | solution.py:86
  635.7 3.5 fusion.61
  639.2 2.2 copy.14
  (5 shorter events, 0.1 us)
Async XLA Ops:
  7.2 6.3 copy-start.4
  25.5 333.9 %all-to-all-start = ((bf16[64,6,7168]{2,1,0:T(8,128)(2,1)}), bf16[64,6,7168]{2,1,0:T(8,128)(2,1)}, u32[]{:S(2)}, u32[]{:S(2)}) async-start(bf16[64,6,7168]{2,1,0:T(8,128)(2,1)} %reshape.53), calls=%async_computation | async-start | bytes 14680064 | tf_op jit(solution)/shard_map/all_to_all | solution.py:58
  37.8 8.9 %copy-start.5 = (s32[64]{0:T(128)S(1)}, s32[64]{0:T(128)}, u32[]{:S(2)}) copy-start(s32[64]{0:T(128)} %param.11) | copy-start | bytes 772
  37.8 417.9 %all-gather.2.cloned.1.call-start = ((), (), s32[]{:S(2)}) async-start(), calls=%async_computation.3 | async-start | bytes 11010048 | tf_op jit(solution)/shard_map/all_gather | solution.py:40
  40.6 231.7 %collective-permute-start = (bf16[256,3584]{1,0:T(8,128)(2,1)S(1)}, bf16[256,3584]{1,0:T(8,128)(2,1)}, u32[]{:S(2)}, u32[]{:S(2)}) collective-permute-start(bf16[256,3584]{1,0:T(8,128)(2,1)S(1)} %bitcast.68), channel_id=1, source_target_pairs={{0,32},{32,0},{1,33},{33,1},{2,34},{34,2},{3,35},{35,3},{4,36},{36... | collective-permute-start | bytes 5505032 | tf_op jit(solution)/shard_map/ppermute | solution.py:14
  42.9 300.6 %collective-permute-start.1 = (bf16[256,3584]{1,0:T(8,128)(2,1)}, bf16[256,3584]{1,0:T(8,128)(2,1)}, u32[]{:S(2)}, u32[]{:S(2)}) collective-permute-start(bf16[256,3584]{1,0:T(8,128)(2,1)} %bitcast.69), channel_id=1, source_target_pairs={{0,32},{32,0},{1,33},{33,1},{2,34},{34,2},{3,35},{35,3},{4,36},{36... | collective-permute-start | bytes 5505032 | tf_op jit(solution)/shard_map/ppermute | solution.py:14
  46.7 296.8 %copy-start.2 = (bf16[1,256,3584]{2,1,0:T(8,128)(2,1)S(1)}, bf16[1,256,3584]{2,1,0:T(8,128)(2,1)}, u32[]{:S(2)}) copy-start(bf16[1,256,3584]{2,1,0:T(8,128)(2,1)} %param.13) | copy-start | bytes 5505028
  347.3 288.4 %reduce-scatter.2.cloned.1.call-start = ((), (), s32[]{:S(2)}) async-start(), calls=%async_computation.4 | async-start | bytes 11010048 | tf_op jit(solution)/shard_map/reduce_scatter | solution.py:86
  367.9 107.8 %collective-permute-start.2 = (bf16[384,7168]{1,0:T(8,128)(2,1)}, bf16[384,7168]{1,0:T(8,128)(2,1)}, u32[]{:S(2)}, u32[]{:S(2)}) collective-permute-start(bf16[384,7168]{1,0:T(8,128)(2,1)} %reshape.54), channel_id=1, source_target_pairs={{0,64},{64,0},{1,65},{65,1},{2,66},{66,2},{3,67},{67,3},{4,68},{68... | collective-permute-start | bytes 16515080 | tf_op jit(solution)/shard_map/ppermute | solution.py:18
  455.7 4.6 copy-start
  491.6 6.2 copy-start.1
  505.4 5.2 collective-permute-start.3
  615.4 4.1 copy-start.3
Sparse Core Ops, SparseCore 0:
  347.4 108.2 all-gather.1
  501.8 133.8 reduce-scatter.1

commit v5 on v4

--- a/solution.py
+++ b/solution.py
@@ -29,20 +29,14 @@
     route_count = local_tokens * top_count
     slots = expert_count * capacity
     lanes = jnp.arange(expert_count, dtype=jnp.int32)
-    partner = jnp.bitwise_xor(lanes, half_axis * pair_flags)
     flagged = pair_flags[own_index] == 1
 
-    quarter_in = w_in[0].T
-    quarter_out = w_out[0]
-    their_in, their_out = partner_2((quarter_in, quarter_out), "expert", pair_bit)
-    quarter_in = jnp.where(flagged, their_in, quarter_in)
-    quarter_out = jnp.where(flagged, their_out, quarter_out)
-    halves = lax.all_gather(jnp.stack([quarter_in, quarter_out]), "dx", axis=1, tiled=True)
+    halves = lax.all_gather(jnp.stack([w_in[0].T, w_out[0]]), "dx", axis=1, tiled=True)
     half_in = halves[0]
     half_out = halves[1]
 
     flat_ids = expert_ids.reshape(-1)
-    target_of = partner[flat_ids]
+    target_of = flat_ids
     onehot = (target_of[:, None] == lanes[None, :]).astype(jnp.int32)
     position = jnp.sum(jnp.cumsum(onehot, axis=0) * onehot, axis=1) - 1
     slot_of = target_of * capacity + position
@@ -82,10 +76,10 @@
     out_own, in_own, outg_own = expert_pass(recv)
     expert_out = (out_own + back.astype(jnp.float32)).astype(jnp.bfloat16)
 
-    terms = jnp.stack([in_own + in_other, outg_own + outg_other]).astype(jnp.bfloat16)
-    grad_quarters = lax.psum_scatter(terms, "dx", scatter_dimension=1, tiled=True)
-    grad_quarter_in = grad_quarters[0].T
-    grad_quarter_out = grad_quarters[1]
+    term_out = (outg_own + outg_other).astype(jnp.bfloat16)
+    term_in = (in_own + in_other).astype(jnp.bfloat16)
+    quarter_out = lax.psum_scatter(term_out, "dx", scatter_dimension=0, tiled=True)
+    quarter_in = lax.psum_scatter(term_in, "dx", scatter_dimension=0, tiled=True)
 
     returned = lax.all_to_all(
         expert_out.reshape(expert_count, capacity, width), "expert",
@@ -98,7 +92,10 @@
         jnp.bfloat16
     ).astype(jnp.float32).reshape(local_tokens, top_count, width)
     mixed = jnp.sum(weighted, axis=1).astype(jnp.bfloat16)
-    return (mixed, grad_quarter_in[None], grad_quarter_out[None])
+
+    quarters, _ = lax.optimization_barrier((jnp.stack([quarter_in, quarter_out]), returned))
+    quarters = jnp.where(flagged, partner_2(quarters, "expert", pair_bit), quarters)
+    return (mixed, quarters[0].T[None], quarters[1][None])
 
 
 def solution(mesh):

time: 652 us -> 568 us (0.87)
  blocking collectives: 98.5 us -> 0 us
  waiting for transfers between devices: 413 us -> 425 us
    all_to_all x1, waiting for transfers between devices: 12 us -> 158 us  [body(): lax.all_to_all(send.reshape(expert_count, capacity, 2 * width), 'expert',...]
    ppermute x2 -> x1, waiting for transfers between devices: 294 us -> 158 us  [partner_2(): return lax.ppermute(block, axis, route)]
    all_to_all x1 -> x0, blocking collectives: 98.5 us -> none  [body(): lax.all_to_all(expert_out.reshape(expert_count, capacity, width), 'expert...]
    reduce_scatter x1 -> x2, waiting for transfers between devices: 13.8 us -> 109 us  [the longest x1 65.3 us: body(): lax.psum_scatter(term_out, 'dx', scatter_dimension=0, tiled=True)]
    all_gather x1, waiting for transfers between devices: 87.8 us -> 0.01 us  [body(): lax.all_gather(jnp.stack([w_in[0].T, w_out[0]]), 'dx', axis=1, tiled=True)]
    all_to_all x0 -> x1, starting transfers between devices: none -> 7.01 us  [body(): lax.all_to_all(expert_out.reshape(expert_count, capacity, width), 'expert...]
  transfers between devices with their start and end apart: 7 -> 8, of which waited for: 6 -> 4; matrix products, arithmetic and copies ran while one was open for 8% -> 11% of each run, Pallas kernels for 0% -> 0%
where the time goes in v5:
time: 568 us; the launch traced here: 563 us
  waiting for transfers between devices  425 us (75%)
  matrix products  56.7 us (10%)
  local copies, waits for them, and re-layouts  30.6 us (5%)
  starting transfers between devices  22.4 us (4%)
  between operations  14.8 us (3%)
  other arithmetic  13.2 us (2%)
    ppermute x1, waiting for transfers between devices, partner_2(): return lax.ppermute(block, axis, route)  158 us
    all_to_all x1, waiting for transfers between devices, body(): lax.all_to_all(send.reshape(expert_count, capacity, 2 * width), 'expert',...  158 us
    reduce_scatter x1, waiting for transfers between devices, body(): lax.psum_scatter(term_out, 'dx', scatter_dimension=0, tiled=True)  65.3 us
    reduce_scatter x1, waiting for transfers between devices, body(): lax.psum_scatter(term_in, 'dx', scatter_dimension=0, tiled=True)  43.5 us
    dot_general x2, matrix products, expert_pass(): lax.dot_general(dpre, rows, contract_first, preferred_element_type=jnp.fl...  21.8 us
    all_to_all x1, starting transfers between devices, body(): lax.all_to_all(send.reshape(expert_count, capacity, 2 * width), 'expert',...  12.3 us
  transfers between devices with their start and end apart: 8, of which 4 were waited for; matrix products, arithmetic and copies ran while one was open for 11% of the time, Pallas kernels for 0%

profile of v5, /device:TPU:192, one launch (start us, length us, event | category | flops | bytes accessed | tf_op | source)
XLA Modules:
  0.0 562.6 jit_solution(7014250691714789447)
XLA Ops:
  7.2 0.0 copy-start.2
  7.2 0.8 fusion.55
  8.0 0.6 reduce-window.6
  8.6 0.2 slice_reduce_fusion
  8.8 0.8 fusion.54
  9.6 0.7 add_add_fusion
  10.3 1.9 multiply_convert_fusion
  12.3 0.0 copy-done.2
  12.3 3.7 convolution_convert_fusion
  15.9 8.3 %reshape.58 = bf16[64,6,7168]{2,1,0:T(8,128)(2,1)} reshape(bf16[384,7168]{1,0:T(8,128)(2,1)} %convolution_convert_fusion) | data formatting | bytes 11010048 | tf_op jit(solution)/shard_map/reshape | solution.py:53
  24.3 12.3 %all-to-all-start = ((bf16[64,6,7168]{2,1,0:T(8,128)(2,1)}), bf16[64,6,7168]{2,1,0:T(8,128)(2,1)}, u32[]{:S(2)}, u32[]{:S(2)}) async-start(bf16[64,6,7168]{2,1,0:T(8,128)(2,1)} %reshape.58), calls=%async_computation | async-start | bytes 14680064 | tf_op jit(solution)/shard_map/all_to_all | solution.py:52
  36.6 0.0 all-gather.2.cloned.1.call-start
  36.6 2.8 copy.13
  39.4 3.7 pad_maximum_fusion
  43.2 0.0 all-gather.2.cloned.1.call-update
  43.2 0.0 reduce-scatter.3.cloned.1.call-start
  43.2 157.7 %all-to-all-done = bf16[64,6,7168]{2,1,0:T(8,128)(2,1)} async-done(((bf16[64,6,7168]{2,1,0:T(8,128)(2,1)}), bf16[64,6,7168]{2,1,0:T(8,128)(2,1)}, u32[]{:S(2)}, u32[]{:S(2)}) %all-to-all-start) | async-done | bytes 5505056 | tf_op jit(solution)/shard_map/all_to_all | solution.py:52
  200.9 8.4 %reshape.59 = bf16[384,7168]{1,0:T(8,128)(2,1)} reshape(bf16[64,6,7168]{2,1,0:T(8,128)(2,1)} %all-to-all-done) | data formatting | bytes 11010048 | tf_op jit(solution)/shard_map/reshape | solution.py:55
  209.3 0.0 collective-permute-start
  209.3 0.0 all-gather.2.cloned.1.call-done
  209.3 4.5 fusion.7
  213.8 10.4 %fusion.17 = f32[512,3584]{1,0:T(8,128)} fusion(bf16[384,7168]{1,0:T(8,128)(2,1)} %reshape.59, bf16[2,512,3584]{2,1,0:T(8,128)(2,1)} %all-gather.2.cloned.1.call-done, f32[384,512]{1,0:T(8,128)S(1)} %fusion.7), kind=kOutput, calls=%fused_computation.29 | convolution fusion | flops 2820341760 | bytes 17301504 | tf_op jit(solution)/shard_map/dot_general | solution.py:70
  224.3 0.0 collective-permute-done
  224.3 4.5 fusion.6
  228.8 11.3 %add_convert_fusion.1 = bf16[512,3584]{1,0:T(8,128)(2,1)} fusion(f32[512,3584]{1,0:T(8,128)} %fusion.17, bf16[384,7168]{1,0:T(8,128)(2,1)} %collective-permute-done, bf16[2,512,3584]{2,1,0:T(8,128)(2,1)} %all-gather.2.cloned.1.call-done, f32[384,512]{1,0:T(8,128)S(1)} %fusion.6), kind=kOutput, calls=%fused_computation.2 | convolution fusion | flops 2824011776 | bytes 20971520 | tf_op jit(solution)/shard_map/dot_general | solution.py:70
  240.1 0.0 reduce-scatter.3.cloned.1.call-update
  240.1 0.0 reduce-scatter.5.cloned.1.call-start
  240.1 5.2 convolution_convert_fusion.1
  245.3 0.5 collective-permute-start.1
  245.8 4.4 fusion.11
  250.2 5.8 %add_convert_fusion = bf16[512,3584]{1,0:T(8,128)(2,1)} fusion(f32[512,3584]{1,0:T(8,128)S(1)} %fusion.11, bf16[384,7168]{1,0:T(8,128)(2,1)} %collective-permute-done, f32[384,512]{1,0:T(8,128)S(1)} %fusion.6), kind=kOutput, calls=%fused_computation.1 | convolution fusion | flops 1413939200 | bytes 14548992 | tf_op jit(solution)/shard_map/dot_general | solution.py:71
  256.0 0.0 reduce-scatter.5.cloned.1.call-update
  256.0 0.0 collective-permute-done.1
  256.0 4.5 add_convert_fusion.2
  260.6 2.7 reshape.60
  263.2 7.0 %all-to-all-start.1 = ((bf16[64,6,3584]{2,1,0:T(8,128)(2,1)}), bf16[64,6,3584]{2,1,0:T(8,128)(2,1)}, u32[]{:S(2)}, u32[]{:S(2)}) async-start(bf16[64,6,3584]{2,1,0:T(8,128)(2,1)} %reshape.60), calls=%async_computation.1 | async-start | bytes 7340032 | tf_op jit(solution)/shard_map/all_to_all | solution.py:84
  270.3 43.5 %reduce-scatter.3.cloned.1.call-done = bf16[256,3584]{1,0:T(8,128)(2,1)} async-done(((bf16[512,3584]{1,0:T(8,128)(2,1)}), bf16[256,3584]{1,0:T(8,128)(2,1)}) %reduce-scatter.3.cloned.1.call-update) | async-done | bytes 1835024 | tf_op jit(solution)/shard_map/reduce_scatter | solution.py:82
  313.8 65.3 %reduce-scatter.5.cloned.1.call-done = bf16[256,3584]{1,0:T(8,128)(2,1)} async-done(((bf16[512,3584]{1,0:T(8,128)(2,1)}), bf16[256,3584]{1,0:T(8,128)(2,1)}) %reduce-scatter.5.cloned.1.call-update) | async-done | bytes 1835024 | tf_op jit(solution)/shard_map/reduce_scatter | solution.py:81
  379.1 4.2 pad_maximum_fusion.1
  383.3 0.0 copy-start.3
  383.3 0.0 copy-start.1
  383.3 0.0 all-to-all-done.1
  383.3 4.0 reshape.61
  387.3 2.5 collective-permute-start.2
  389.8 0.0 copy-done.3
  389.8 0.0 copy-start
  389.8 0.6 dynamic_slice.3
  391.3 0.0 copy-done.1
  391.3 2.4 fusion.2
  393.7 158.2 %collective-permute-done.2 = bf16[2,256,3584]{2,1,0:T(8,128)(2,1)} collective-permute-done((bf16[2,256,3584]{2,1,0:T(8,128)(2,1)}, bf16[2,256,3584]{2,1,0:T(8,128)(2,1)}, u32[]{:S(2)}, u32[]{:S(2)}) %collective-permute-start.2) | collective-permute-done | bytes 3670048 | tf_op jit(solution)/shard_map/ppermute | solution.py:14
  552.0 0.0 copy-done
  552.0 0.4 broadcast_select_fusion
  552.4 1.5 fusion.59
  553.8 2.2 copy.14
  (2 shorter events, 0.0 us)
Async XLA Ops:
  7.2 5.1 copy-start.2
  24.3 176.7 %all-to-all-start = ((bf16[64,6,7168]{2,1,0:T(8,128)(2,1)}), bf16[64,6,7168]{2,1,0:T(8,128)(2,1)}, u32[]{:S(2)}, u32[]{:S(2)}) async-start(bf16[64,6,7168]{2,1,0:T(8,128)(2,1)} %reshape.58), calls=%async_computation | async-start | bytes 14680064 | tf_op jit(solution)/shard_map/all_to_all | solution.py:52
  36.6 172.7 %all-gather.2.cloned.1.call-start = ((), (), s32[]{:S(2)}) async-start(), calls=%async_computation.4 | async-start | bytes 11010048 | tf_op jit(solution)/shard_map/all_gather | solution.py:34
  43.2 270.6 %reduce-scatter.3.cloned.1.call-start = ((), (), s32[]{:S(2)}) async-start(), calls=%async_computation.5 | async-start | bytes 5505024 | tf_op jit(solution)/shard_map/reduce_scatter | solution.py:82
  209.3 14.9 %collective-permute-start = (bf16[384,7168]{1,0:T(8,128)(2,1)}, bf16[384,7168]{1,0:T(8,128)(2,1)}, u32[]{:S(2)}, u32[]{:S(2)}) collective-permute-start(bf16[384,7168]{1,0:T(8,128)(2,1)} %reshape.59), channel_id=1, source_target_pairs={{0,64},{64,0},{1,65},{65,1},{2,66},{66,2},{3,67},{67,3},{4,68},{68... | collective-permute-start | bytes 16515080 | tf_op jit(solution)/shard_map/ppermute | solution.py:18
  240.1 139.0 %reduce-scatter.5.cloned.1.call-start = ((), (), s32[]{:S(2)}) async-start(), calls=%async_computation.6 | async-start | bytes 5505024 | tf_op jit(solution)/shard_map/reduce_scatter | solution.py:81
  245.3 10.7 %collective-permute-start.1 = (bf16[384,3584]{1,0:T(8,128)(2,1)}, bf16[384,3584]{1,0:T(8,128)(2,1)}, u32[]{:S(2)}, u32[]{:S(2)}) collective-permute-start(bf16[384,3584]{1,0:T(8,128)(2,1)} %convolution_convert_fusion.1), channel_id=1, source_target_pairs={{0,64},{64,0},{1,65},{65,1},{2,66},{66,2},{3,67},{67,3},{4,68},{68... | collective-permute-start | bytes 8257544 | tf_op jit(solution)/shard_map/ppermute | solution.py:18
  263.2 120.1 %all-to-all-start.1 = ((bf16[64,6,3584]{2,1,0:T(8,128)(2,1)}), bf16[64,6,3584]{2,1,0:T(8,128)(2,1)}, u32[]{:S(2)}, u32[]{:S(2)}) async-start(bf16[64,6,3584]{2,1,0:T(8,128)(2,1)} %reshape.60), calls=%async_computation.1 | async-start | bytes 7340032 | tf_op jit(solution)/shard_map/all_to_all | solution.py:84
  383.3 6.5 %copy-start.3 = (s32[64]{0:T(128)S(1)}, s32[64]{0:T(128)}, u32[]{:S(2)}) copy-start(s32[64]{0:T(128)} %param.11) | copy-start | bytes 772
  383.3 8.0 %copy-start.1 = (f32[256,1]{0,1:T(1,128)S(1)}, f32[256,1]{0,1:T(1,128)}, u32[]{:S(2)}) copy-start(f32[256,1]{0,1:T(1,128)} %param.10) | copy-start | bytes 3076
  387.3 164.7 %collective-permute-start.2 = (bf16[2,256,3584]{2,1,0:T(8,128)(2,1)}, bf16[2,256,3584]{2,1,0:T(8,128)(2,1)}, u32[]{:S(2)}, u32[]{:S(2)}) collective-permute-start(bf16[2,256,3584]{2,1,0:T(8,128)(2,1)} %pad_maximum_fusion.1), channel_id=1, source_target_pairs={{0,32},{32,0},{1,33},{33,1},{2,34},{34,2},{3,35},{35,3},{4,36},{36... | collective-permute-start | bytes 11010056 | tf_op jit(solution)/shard_map/ppermute | solution.py:14
  389.8 162.2 %copy-start = (bf16[2,256,3584]{2,1,0:T(8,128)(2,1)S(1)}, bf16[2,256,3584]{2,1,0:T(8,128)(2,1)}, u32[]{:S(2)}) copy-start(bf16[2,256,3584]{2,1,0:T(8,128)(2,1)} %pad_maximum_fusion.1) | copy-start | bytes 11010052
Sparse Core Ops, SparseCore 0:
  43.3 155.6 all-gather.1
  240.2 73.5 reduce-scatter.2
  316.4 62.6 reduce-scatter.4

commit v6 on v2

--- a/solution.py
+++ b/solution.py
@@ -34,13 +34,6 @@
 
     quarter_in = w_in[0]
     quarter_out = w_out[0]
-    size_in = quarter_in.size
-    both = jnp.concatenate([quarter_in.reshape(-1), quarter_out.reshape(-1)])
-    both = jnp.where(flagged, partner_2(both, "expert", pair_bit), both)
-    quarter_in = both[:size_in].reshape(quarter_in.shape)
-    quarter_out = both[size_in:].reshape(quarter_out.shape)
-    half_in = lax.all_gather(quarter_in, "dx", axis=1, tiled=True)
-    half_out = lax.all_gather(quarter_out, "dx", axis=0, tiled=True)
 
     flat_ids = expert_ids.reshape(-1)
     target_of = partner[flat_ids]
@@ -56,10 +49,16 @@
     scaled = (gates.reshape(-1)[:, None] * route_cot.astype(jnp.float32)).astype(jnp.bfloat16)
     payload = jnp.concatenate([route_rows, scaled], axis=1)
     send = jnp.dot(select, payload, preferred_element_type=jnp.float32).astype(jnp.bfloat16)
+    their_in, send_kept = lax.optimization_barrier((quarter_in, send))
+    quarter_in = jnp.where(flagged, partner_2(their_in, "expert", pair_bit), quarter_in)
+    half_in = lax.all_gather(quarter_in, "dx", axis=1, tiled=True)
     recv = lax.all_to_all(
-        send.reshape(expert_count, capacity, 2 * width), "expert",
+        send_kept.reshape(expert_count, capacity, 2 * width), "expert",
         split_axis=0, concat_axis=0, tiled=True,
     ).reshape(slots, 2 * width)
+    their_out, recv = lax.optimization_barrier((quarter_out, recv))
+    quarter_out = jnp.where(flagged, partner_2(their_out, "expert", pair_bit), quarter_out)
+    half_out = lax.all_gather(quarter_out, "dx", axis=0, tiled=True)
     other = swap_core(recv)
 
     contract_last = (((1,), (1,)), ((), ()))

time: 567 us -> 590 us (1.041)
  waiting for transfers between devices: 329 us -> 367 us
  local copies, waits for them, and re-layouts: 44.3 us -> 26.2 us
    ppermute x1 -> x2, waiting for transfers between devices: 132 us -> 315 us  [partner_2(): return lax.ppermute(block, axis, route)]
    all_to_all x1, waiting for transfers between devices: 151 us -> 8.57 us  [body(): lax.all_to_all(send_kept.reshape(expert_count, capacity, 2 * width), 'exp...]
    slice x4 -> x1, local copies, waits for them, and re-layouts: 8.37 us -> 0.18 us  [the longest x2 5.26 us: body(): quarter_in = both[:size_in].reshape(quarter_in.shape)]
  transfers between devices with their start and end apart: 8 -> 9, of which waited for: 4 -> 5; matrix products, arithmetic and copies ran while one was open for 17% -> 12% of each run, Pallas kernels for 0% -> 0%
where the time goes in v6:
time: 590 us; the launch traced here: 585 us
  waiting for transfers between devices  367 us (62%)
  blocking collectives  98.7 us (17%)
  matrix products  56.6 us (10%)
  local copies, waits for them, and re-layouts  26.2 us (4%)
  starting transfers between devices  15.1 us (3%)
  between operations  14.6 us (2%)
  other arithmetic  7.09 us (1%)
    ppermute x2, waiting for transfers between devices, partner_2(): return lax.ppermute(block, axis, route)  315 us
    all_to_all x1, blocking collectives, body(): lax.all_to_all(expert_out.reshape(expert_count, capacity, width), 'expert...  98.7 us
    all_gather x1, waiting for transfers between devices, body(): half_out = lax.all_gather(quarter_out, 'dx', axis=0, tiled=True)  35.6 us
    dot_general x2, matrix products, expert_pass(): lax.dot_general(rows, dpre, contract_first, preferred_element_type=jnp.fl...  22.4 us
    all_to_all x1, starting transfers between devices, body(): lax.all_to_all(send_kept.reshape(expert_count, capacity, 2 * width), 'exp...  12.5 us
  transfers between devices with their start and end apart: 9, of which 5 were waited for; matrix products, arithmetic and copies ran while one was open for 12% of the time, Pallas kernels for 0%

profile of v6, /device:TPU:192, one launch (start us, length us, event | category | flops | bytes accessed | tf_op | source)
XLA Modules:
  0.0 585.3 jit_solution(351179379281001602)
XLA Ops:
  7.2 0.0 copy-start.4
  7.2 0.8 compare_select_fusion
  8.0 0.7 multiply_xor_fusion
  8.7 1.9 gather_fusion
  10.5 0.6 reduce-window.6
  11.2 0.2 slice_reduce_fusion
  11.4 0.1 fusion.54
  11.5 2.0 multiply_convert_fusion
  13.5 0.0 copy-done.4
  13.5 3.7 convolution_convert_fusion
  17.2 8.3 %reshape.53 = bf16[64,6,7168]{2,1,0:T(8,128)(2,1)} reshape(bf16[384,7168]{1,0:T(8,128)(2,1)} %convolution_convert_fusion) | data formatting | bytes 11010048 | tf_op jit(solution)/shard_map/reshape | solution.py:56
  25.5 0.0 copy-start
  25.5 0.0 copy-start.5
  25.5 12.5 %all-to-all-start = ((bf16[64,6,7168]{2,1,0:T(8,128)(2,1)}), bf16[64,6,7168]{2,1,0:T(8,128)(2,1)}, u32[]{:S(2)}, u32[]{:S(2)}) async-start(bf16[64,6,7168]{2,1,0:T(8,128)(2,1)} %reshape.53), calls=%async_computation | async-start | bytes 14680064 | tf_op jit(solution)/shard_map/all_to_all | solution.py:55
  38.0 0.0 all-gather.3.cloned.1.call-start
  38.0 0.0 copy-done
  38.0 2.2 collective-permute-start
  40.3 0.0 copy-done.5
  40.3 0.6 dynamic_slice.3
  41.5 229.3 %collective-permute-done = bf16[3584,256]{1,0:T(8,128)(2,1)} collective-permute-done((bf16[3584,256]{1,0:T(8,128)(2,1)S(1)}, bf16[3584,256]{1,0:T(8,128)(2,1)}, u32[]{:S(2)}, u32[]{:S(2)}) %collective-permute-start) | collective-permute-done | bytes 1835040 | tf_op jit(solution)/shard_map/ppermute | solution.py:14
  270.8 1.4 broadcast_select_fusion.1
  272.2 0.0 all-gather.3.cloned.1.call-update
  272.2 0.0 copy-start.1
  272.2 0.0 all-gather.5.cloned.1.call-start
  272.3 8.6 %all-to-all-done = bf16[64,6,7168]{2,1,0:T(8,128)(2,1)} async-done(((bf16[64,6,7168]{2,1,0:T(8,128)(2,1)}), bf16[64,6,7168]{2,1,0:T(8,128)(2,1)}, u32[]{:S(2)}, u32[]{:S(2)}) %all-to-all-start) | async-done | bytes 5505056 | tf_op jit(solution)/shard_map/all_to_all | solution.py:55
  280.8 8.6 %reshape.54 = bf16[384,7168]{1,0:T(8,128)(2,1)} reshape(bf16[64,6,7168]{2,1,0:T(8,128)(2,1)} %all-to-all-done) | data formatting | bytes 11010048 | tf_op jit(solution)/shard_map/reshape | solution.py:58
  289.4 0.0 collective-permute-start.2
  289.4 0.0 copy-done.1
  289.4 0.0 collective-permute-start.1
  289.4 85.6 %collective-permute-done.1 = bf16[256,3584]{1,0:T(8,128)(2,1)S(1)} collective-permute-done((bf16[256,3584]{1,0:T(8,128)(2,1)S(1)}, bf16[256,3584]{1,0:T(8,128)(2,1)S(1)}, u32[]{:S(2)}, u32[]{:S(2)}) %collective-permute-start.1) | collective-permute-done | bytes 1835040 | tf_op jit(solution)/shard_map/ppermute | solution.py:14
  375.0 1.5 broadcast_select_fusion
  376.5 0.0 all-gather.5.cloned.1.call-update
  376.5 0.0 reduce-scatter.5.cloned.1.call-start
  376.5 0.0 all-gather.3.cloned.1.call-done
  376.6 4.4 fusion.19
  381.0 0.0 copy-start.3
  381.0 4.1 fusion.13
  385.1 0.0 collective-permute-done.2
  385.1 0.0 copy-done.3
  385.1 3.7 fusion.11
  388.8 6.0 %add_convert_fusion = bf16[512,3584]{1,0:T(8,128)(2,1)} fusion(f32[512,3584]{1,0:T(8,128)S(1)} %fusion.13, bf16[384,7168]{1,0:T(8,128)(2,1)} %collective-permute-done.2, f32[384,512]{1,0:T(8,128)S(1)} %fusion.11), kind=kOutput, calls=%fused_computation.2 | convolution fusion | flops 1413939200 | bytes 14548992 | tf_op jit(solution)/shard_map/dot_general | solution.py:77
  394.8 0.0 reduce-scatter.5.cloned.1.call-update
  394.8 0.2 reduce-scatter.3.cloned.1.call-start
  395.1 35.6 %all-gather.5.cloned.1.call-done = bf16[512,3584]{1,0:T(8,128)(2,1)} async-done(((bf16[256,3584]{1,0:T(8,128)(2,1)}), bf16[512,3584]{1,0:T(8,128)(2,1)}) %all-gather.5.cloned.1.call-update) | async-done | bytes 3670032 | tf_op jit(solution)/shard_map/all_gather | solution.py:61
  430.7 5.3 convolution_convert_fusion.1
  436.0 0.0 collective-permute-start.3
  436.0 10.4 %fusion.17 = f32[3584,512]{1,0:T(8,128)} fusion(bf16[384,7168]{1,0:T(8,128)(2,1)} %reshape.54, bf16[512,3584]{1,0:T(8,128)(2,1)} %all-gather.5.cloned.1.call-done, f32[384,512]{1,0:T(8,128)S(1)} %fusion.19), kind=kOutput, calls=%fused_computation.25 | convolution fusion | flops 2820341760 | bytes 17301504 | tf_op jit(solution)/shard_map/dot_general | solution.py:76
  446.4 11.9 %add_convert_fusion.1 = bf16[3584,512]{1,0:T(8,128)(2,1)} fusion(f32[3584,512]{1,0:T(8,128)} %fusion.17, bf16[384,7168]{1,0:T(8,128)(2,1)} %collective-permute-done.2, bf16[512,3584]{1,0:T(8,128)(2,1)} %all-gather.5.cloned.1.call-done, f32[384,512]{1,0:T(8,128)S(1)} %fusion.11), kind=kOutput, calls=%fused_computation.3 | convolution fusion | flops 2824011776 | bytes 20971520 | tf_op jit(solution)/shard_map/dot_general | solution.py:76
  458.4 0.0 reduce-scatter.3.cloned.1.call-update
  458.4 0.0 collective-permute-done.3
  458.4 4.7 fusion
  463.1 2.7 reshape.55
  465.7 98.7 %all_to_all.10 = bf16[64,6,3584]{2,1,0:T(8,128)(2,1)} all-to-all(bf16[64,6,3584]{2,1,0:T(8,128)(2,1)} %reshape.55), channel_id=1, replica_groups=mesh['dx'=2,'dc'=2,'expert'=64] {'expert'}, dimensions={0} | all-to-all | bytes 5505024 | tf_op jit(solution)/shard_map/all_to_all | solution.py:90
  564.5 0.0 copy-start.2
  564.5 4.0 reshape.56
  568.5 0.0 copy-done.2
  568.5 2.4 fusion.3
  570.9 0.0 reduce-scatter.5.cloned.1.call-done
  570.9 7.9 %reduce-scatter.3.cloned.1.call-done = bf16[3584,256]{1,0:T(8,128)(2,1)} async-done(((bf16[3584,512]{1,0:T(8,128)(2,1)}), bf16[3584,256]{1,0:T(8,128)(2,1)}) %reduce-scatter.3.cloned.1.call-update) | async-done | bytes 1835024 | tf_op jit(solution)/shard_map/reduce_scatter | solution.py:87
  (5 shorter events, 0.1 us)
Async XLA Ops:
  7.2 6.3 %copy-start.4 = (bf16[256,3584]{1,0:T(8,128)(2,1)S(1)}, bf16[256,3584]{1,0:T(8,128)(2,1)}, u32[]{:S(2)}) copy-start(bf16[256,3584]{1,0:T(8,128)(2,1)} %param.7) | copy-start | bytes 5505028
  25.5 12.5 %copy-start = (bf16[1,3584,256]{2,1,0:T(8,128)(2,1)S(1)}, bf16[1,3584,256]{2,1,0:T(8,128)(2,1)}, u32[]{:S(2)}) copy-start(bf16[1,3584,256]{2,1,0:T(8,128)(2,1)} %param.12) | copy-start | bytes 5505028
  25.5 14.8 %copy-start.5 = (s32[64]{0:T(128)S(1)}, s32[64]{0:T(128)}, u32[]{:S(2)}) copy-start(s32[64]{0:T(128)} %param.11) | copy-start | bytes 772
  25.5 255.3 %all-to-all-start = ((bf16[64,6,7168]{2,1,0:T(8,128)(2,1)}), bf16[64,6,7168]{2,1,0:T(8,128)(2,1)}, u32[]{:S(2)}, u32[]{:S(2)}) async-start(bf16[64,6,7168]{2,1,0:T(8,128)(2,1)} %reshape.53), calls=%async_computation | async-start | bytes 14680064 | tf_op jit(solution)/shard_map/all_to_all | solution.py:55
  38.0 338.6 %all-gather.3.cloned.1.call-start = ((), (), s32[]{:S(2)}) async-start(), calls=%async_computation.4 | async-start | bytes 5505024 | tf_op jit(solution)/shard_map/all_gather | solution.py:54
  38.0 232.7 %collective-permute-start = (bf16[3584,256]{1,0:T(8,128)(2,1)S(1)}, bf16[3584,256]{1,0:T(8,128)(2,1)}, u32[]{:S(2)}, u32[]{:S(2)}) collective-permute-start(bf16[3584,256]{1,0:T(8,128)(2,1)S(1)} %bitcast.32), channel_id=1, source_target_pairs={{0,32},{32,0},{1,33},{33,1},{2,34},{34,2},{3,35},{35,3},{4,36},{36... | collective-permute-start | bytes 5505032 | tf_op jit(solution)/shard_map/ppermute | solution.py:14
  272.2 17.2 %copy-start.1 = (bf16[1,256,3584]{2,1,0:T(8,128)(2,1)S(1)}, bf16[1,256,3584]{2,1,0:T(8,128)(2,1)}, u32[]{:S(2)}) copy-start(bf16[1,256,3584]{2,1,0:T(8,128)(2,1)} %param.13) | copy-start | bytes 5505028
  272.2 158.5 %all-gather.5.cloned.1.call-start = ((), (), s32[]{:S(2)}) async-start(), calls=%async_computation.5 | async-start | bytes 5505024 | tf_op jit(solution)/shard_map/all_gather | solution.py:61
  289.4 95.7 %collective-permute-start.2 = (bf16[384,7168]{1,0:T(8,128)(2,1)}, bf16[384,7168]{1,0:T(8,128)(2,1)}, u32[]{:S(2)}, u32[]{:S(2)}) collective-permute-start(bf16[384,7168]{1,0:T(8,128)(2,1)} %reshape.54), channel_id=1, source_target_pairs={{0,64},{64,0},{1,65},{65,1},{2,66},{66,2},{3,67},{67,3},{4,68},{68... | collective-permute-start | bytes 16515080 | tf_op jit(solution)/shard_map/ppermute | solution.py:18
  289.4 85.6 %collective-permute-start.1 = (bf16[256,3584]{1,0:T(8,128)(2,1)S(1)}, bf16[256,3584]{1,0:T(8,128)(2,1)S(1)}, u32[]{:S(2)}, u32[]{:S(2)}) collective-permute-start(bf16[256,3584]{1,0:T(8,128)(2,1)S(1)} %bitcast.33), channel_id=1, source_target_pairs={{0,32},{32,0},{1,33},{33,1},{2,34},{34,2},{3,35},{35,3},{4,36},{36... | collective-permute-start | bytes 5505032 | tf_op jit(solution)/shard_map/ppermute | solution.py:14
  376.5 194.4 %reduce-scatter.5.cloned.1.call-start = ((), (), s32[]{:S(2)}) async-start(), calls=%async_computation.7 | async-start | bytes 5505024 | tf_op jit(solution)/shard_map/reduce_scatter | solution.py:88
  381.0 4.1 copy-start.3
  394.8 183.9 %reduce-scatter.3.cloned.1.call-start = ((), (), s32[]{:S(2)}) async-start(), calls=%async_computation.6 | async-start | bytes 5505024 | tf_op jit(solution)/shard_map/reduce_scatter | solution.py:87
  436.0 22.4 %collective-permute-start.3 = (bf16[384,3584]{1,0:T(8,128)(2,1)}, bf16[384,3584]{1,0:T(8,128)(2,1)}, u32[]{:S(2)}, u32[]{:S(2)}) collective-permute-start(bf16[384,3584]{1,0:T(8,128)(2,1)} %convolution_convert_fusion.1), channel_id=1, source_target_pairs={{0,64},{64,0},{1,65},{65,1},{2,66},{66,2},{3,67},{67,3},{4,68},{68... | collective-permute-start | bytes 8257544 | tf_op jit(solution)/shard_map/ppermute | solution.py:18
  564.5 4.0 copy-start.2
Sparse Core Ops, SparseCore 0:
  272.3 62.4 all-gather.2
  376.6 54.0 all-gather.4
  433.8 70.9 reduce-scatter.4
  507.8 70.8 reduce-scatter.2

commit v7 on v2

--- a/solution.py
+++ b/solution.py
@@ -4,25 +4,18 @@
 from jax.sharding import Mesh, PartitionSpec as P
 
 
-def partner_2(block, axis, distance):
-    count = lax.axis_size(axis)
-    route = []
-    for low in range(count):
-        high = low | 1 << distance
-        if high != low and high < count:
-            route += [(low, high), (high, low)]
-    return lax.ppermute(block, axis, route)
-
-
 def swap_core(block):
     return lax.ppermute(block, "dc", [(0, 1), (1, 0)])
 
 
+EXPERT = ("zh", "er")
+
+
 def body(tokens, cotangent, expert_ids, gates, pair_flags, w_in, w_out):
-    expert_count = lax.axis_size("expert")
-    own_index = lax.axis_index("expert")
-    half_axis = expert_count // 2
-    pair_bit = half_axis.bit_length() - 1
+    half_axis = lax.axis_size("er")
+    expert_count = 2 * half_axis
+    high = lax.axis_index("zh")
+    own_index = high * half_axis + lax.axis_index("er")
     local_tokens, top_count = expert_ids.shape
     width = tokens.shape[1]
     capacity = max(2, 3 * local_tokens * top_count // (2 * expert_count))
@@ -34,11 +27,10 @@
 
     quarter_in = w_in[0]
     quarter_out = w_out[0]
-    size_in = quarter_in.size
-    both = jnp.concatenate([quarter_in.reshape(-1), quarter_out.reshape(-1)])
-    both = jnp.where(flagged, partner_2(both, "expert", pair_bit), both)
-    quarter_in = both[:size_in].reshape(quarter_in.shape)
-    quarter_out = both[size_in:].reshape(quarter_out.shape)
+    pair_in, pair_out = lax.all_gather((quarter_in, quarter_out), "zh", axis=0, tiled=False)
+    pick = jnp.where(flagged, 1 - high, high)
+    quarter_in = jnp.where(pick == 0, pair_in[0], pair_in[1])
+    quarter_out = jnp.where(pick == 0, pair_out[0], pair_out[1])
     half_in = lax.all_gather(quarter_in, "dx", axis=1, tiled=True)
     half_out = lax.all_gather(quarter_out, "dx", axis=0, tiled=True)
 
@@ -57,7 +49,7 @@
     payload = jnp.concatenate([route_rows, scaled], axis=1)
     send = jnp.dot(select, payload, preferred_element_type=jnp.float32).astype(jnp.bfloat16)
     recv = lax.all_to_all(
-        send.reshape(expert_count, capacity, 2 * width), "expert",
+        send.reshape(expert_count, capacity, 2 * width), EXPERT,
         split_axis=0, concat_axis=0, tiled=True,
     ).reshape(slots, 2 * width)
     other = swap_core(recv)
@@ -89,7 +81,7 @@
     grad_quarter_out = lax.psum_scatter(term_out, "dx", scatter_dimension=0, tiled=True)
 
     returned = lax.all_to_all(
-        expert_out.reshape(expert_count, capacity, width), "expert",
+        expert_out.reshape(expert_count, capacity, width), EXPERT,
         split_axis=0, concat_axis=0, tiled=True,
     ).reshape(slots, width)
     route_out = lax.dot_general(
@@ -106,22 +98,22 @@
     devices = mesh.devices
     dp_count = devices.shape[0]
     split = Mesh(
-        devices.reshape(dp_count // 2, 2, devices.shape[1]), ("dx", "dc", "expert")
+        devices.reshape(dp_count // 2, 2, 2, devices.shape[1] // 2), ("dx", "dc") + EXPERT
     )
-    rows = P(("dx", "dc", "expert"), None)
+    rows = P(("dx", "dc") + EXPERT, None)
     placed = (
         rows,
         rows,
         rows,
         rows,
         P(),
-        P("expert", None, ("dx", "dc")),
-        P("expert", ("dx", "dc"), None),
+        P(EXPERT, None, ("dx", "dc")),
+        P(EXPERT, ("dx", "dc"), None),
     )
     return jax.shard_map(
         body,
         mesh=split,
         in_specs=placed,
-        out_specs=(rows, P("expert", None, ("dx", "dc")), P("expert", ("dx", "dc"), None)),
+        out_specs=(rows, P(EXPERT, None, ("dx", "dc")), P(EXPERT, ("dx", "dc"), None)),
         check_vma=False,
     )

time: 567 us -> 653 us (1.15)
  waiting for transfers between devices: 329 us -> 430 us
  local copies, waits for them, and re-layouts: 44.3 us -> 26.1 us
  other arithmetic: 5 us -> 11.6 us
    all_gather x0 -> x2, waiting for transfers between devices: none -> 170 us  [body(): lax.all_gather((quarter_in, quarter_out), 'zh', axis=0, tiled=False)]
    ppermute x1 -> x0, waiting for transfers between devices: 132 us -> none  [partner_2(): return lax.ppermute(block, axis, route)]
    all_gather x1, waiting for transfers between devices: 0.02 us -> 40.8 us  [body(): half_in = lax.all_gather(quarter_in, 'dx', axis=1, tiled=True)]
    reduce_scatter x1, waiting for transfers between devices: 0.01 us -> 17.4 us  [body(): lax.psum_scatter(term_out, 'dx', scatter_dimension=0, tiled=True)]
    all_gather x1, waiting for transfers between devices: 37.9 us -> 54.7 us  [body(): half_out = lax.all_gather(quarter_out, 'dx', axis=0, tiled=True)]
    slice x4 -> x1, local copies, waits for them, and re-layouts: 8.37 us -> 0.18 us  [the longest x2 5.26 us: body(): quarter_in = both[:size_in].reshape(quarter_in.shape)]
    reduce_scatter x1, waiting for transfers between devices: 7.93 us -> 0.01 us  [body(): lax.psum_scatter(term_in, 'dx', scatter_dimension=1, tiled=True)]
  transfers between devices with their start and end apart: 8 -> 9, of which waited for: 4 -> 5; matrix products, arithmetic and copies ran while one was open for 17% -> 9% of each run, Pallas kernels for 0% -> 0%
where the time goes in v7:
time: 653 us; the launch traced here: 648 us
  waiting for transfers between devices  430 us (66%)
  blocking collectives  98.9 us (15%)
  matrix products  54.4 us (8%)
  local copies, waits for them, and re-layouts  26.1 us (4%)
  between operations  15 us (2%)
  starting transfers between devices  12.7 us (2%)
  other arithmetic  11.6 us (2%)
    all_gather x2, waiting for transfers between devices, body(): lax.all_gather((quarter_in, quarter_out), 'zh', axis=0, tiled=False)  170 us
    all_to_all x1, waiting for transfers between devices, body(): lax.all_to_all(send.reshape(expert_count, capacity, 2 * width), EXPERT, s...  146 us
    all_to_all x1, blocking collectives, body(): lax.all_to_all(expert_out.reshape(expert_count, capacity, width), EXPERT,...  98.9 us
    all_gather x1, waiting for transfers between devices, body(): half_out = lax.all_gather(quarter_out, 'dx', axis=0, tiled=True)  54.7 us
    all_gather x1, waiting for transfers between devices, body(): half_in = lax.all_gather(quarter_in, 'dx', axis=1, tiled=True)  40.8 us
    reduce_scatter x1, waiting for transfers between devices, body(): lax.psum_scatter(term_out, 'dx', scatter_dimension=0, tiled=True)  17.4 us
    dot_general x2, matrix products, expert_pass(): lax.dot_general(rows, dpre, contract_first, preferred_element_type=jnp.fl...  16.1 us
  transfers between devices with their start and end apart: 9, of which 5 were waited for; matrix products, arithmetic and copies ran while one was open for 9% of the time, Pallas kernels for 0%

profile of v7, /device:TPU:192, one launch (start us, length us, event | category | flops | bytes accessed | tf_op | source)
XLA Modules:
  0.0 648.4 jit_solution(5515484065703007524)
XLA Ops:
  7.2 0.0 copy-start.2
  7.2 0.8 multiply_xor_fusion
  8.0 0.7 compare_select_fusion
  8.7 1.9 gather_fusion
  10.5 0.6 reduce-window.6
  11.2 0.2 slice_reduce_fusion
  11.4 0.1 fusion.62
  11.5 2.0 multiply_convert_fusion
  13.5 0.0 copy-done.2
  13.5 3.7 convolution_convert_fusion
  17.2 8.2 %reshape.57 = bf16[64,6,7168]{2,1,0:T(8,128)(2,1)} reshape(bf16[384,7168]{1,0:T(8,128)(2,1)} %convolution_convert_fusion) | data formatting | bytes 11010048 | tf_op jit(solution)/shard_map/reshape | solution.py:52
  25.4 12.3 %all-to-all-start = ((bf16[64,6,7168]{2,1,0:T(8,128)(2,1)}), bf16[64,6,7168]{2,1,0:T(8,128)(2,1)}, u32[]{:S(2)}, u32[]{:S(2)}) async-start(bf16[64,6,7168]{2,1,0:T(8,128)(2,1)} %reshape.57), calls=%async_computation | async-start | bytes 14680064 | tf_op jit(solution)/shard_map/all_to_all | solution.py:51
  37.7 0.0 copy-start.3
  37.7 0.0 all-gather.7.cloned.1.call-start
  37.8 0.7 all-gather.7.cloned.1.call-update
  38.5 0.0 all-gather.9.cloned.1.call-start
  38.5 0.7 all-gather.9.cloned.1.call-update
  39.2 0.0 all-gather.11.cloned.1.call-start
  39.3 0.0 copy-done.3
  39.3 0.6 dynamic_slice.3
  40.5 169.6 %all-gather.7.cloned.1.call-done = bf16[2,3584,256]{2,1,0:T(8,128)(2,1)} async-done(((bf16[1,3584,256]{2,1,0:T(8,128)(2,1)}), bf16[2,3584,256]{2,1,0:T(8,128)(2,1)}) %all-gather.7.cloned.1.call-update) | async-done | bytes 3670032 | tf_op jit(solution)/shard_map/all_gather | solution.py:30
  210.1 3.5 slice_select_fusion.1
  213.6 0.0 all-gather.11.cloned.1.call-update
  213.6 0.0 all-gather.13.cloned.1.call-start
  213.7 145.6 %all-to-all-done = bf16[64,6,7168]{2,1,0:T(8,128)(2,1)} async-done(((bf16[64,6,7168]{2,1,0:T(8,128)(2,1)}), bf16[64,6,7168]{2,1,0:T(8,128)(2,1)}, u32[]{:S(2)}, u32[]{:S(2)}) %all-to-all-start) | async-done | bytes 5505056 | tf_op jit(solution)/shard_map/all_to_all | solution.py:51
  359.3 8.6 %reshape.58 = bf16[384,7168]{1,0:T(8,128)(2,1)} reshape(bf16[64,6,7168]{2,1,0:T(8,128)(2,1)} %all-to-all-done) | data formatting | bytes 11010048 | tf_op jit(solution)/shard_map/reshape | solution.py:54
  367.8 0.0 collective-permute-start
  367.8 0.0 all-gather.9.cloned.1.call-done
  367.8 3.9 slice_select_fusion
  371.8 0.0 all-gather.13.cloned.1.call-update
  371.8 0.2 reduce-scatter.3.cloned.1.call-start
  372.0 40.8 %all-gather.11.cloned.1.call-done = bf16[1,3584,512]{2,1,0:T(8,128)(2,1)} async-done(((bf16[1,3584,256]{2,1,0:T(8,128)(2,1)}), bf16[1,3584,512]{2,1,0:T(8,128)(2,1)}) %all-gather.11.cloned.1.call-update) | async-done | bytes 3670032 | tf_op jit(solution)/shard_map/all_gather | solution.py:34
  412.8 4.4 fusion.17
  417.2 54.7 %all-gather.13.cloned.1.call-done = bf16[1,512,3584]{2,1,0:T(8,128)(2,1)} async-done(((bf16[1,256,3584]{2,1,0:T(8,128)(2,1)}), bf16[1,512,3584]{2,1,0:T(8,128)(2,1)}) %all-gather.13.cloned.1.call-update) | async-done | bytes 3670032 | tf_op jit(solution)/shard_map/all_gather | solution.py:35
  472.0 10.3 %fusion.26 = f32[3584,512]{1,0:T(8,128)} fusion(bf16[384,7168]{1,0:T(8,128)(2,1)} %reshape.58, bf16[1,512,3584]{2,1,0:T(8,128)(2,1)} %all-gather.13.cloned.1.call-done, f32[384,512]{1,0:T(8,128)S(1)} %fusion.17), kind=kOutput, calls=%fused_computation.32 | convolution fusion | flops 2820341760 | bytes 17301504 | tf_op jit(solution)/shard_map/dot_general | solution.py:69
  482.3 0.0 copy-start.1
  482.3 0.0 collective-permute-done
  482.3 0.0 slice-start
  482.3 4.6 fusion.15
  486.9 0.0 copy-done.1
  486.9 0.0 slice-start.1
  486.9 3.6 fusion.54
  490.6 0.0 slice-done
  490.6 0.0 slice-done.1
  490.6 5.8 add_convert_fusion.1
  496.4 0.0 reduce-scatter.3.cloned.1.call-update
  496.4 0.0 reduce-scatter.5.cloned.1.call-start
  496.5 5.3 convolution_convert_fusion.1
  501.7 0.0 collective-permute-start.1
  501.7 3.9 fusion.21
  505.6 5.9 add_convert_fusion
  511.5 0.0 reduce-scatter.5.cloned.1.call-update
  511.5 0.0 collective-permute-done.1
  511.5 4.5 add_convert_fusion.2
  516.1 2.7 reshape.59
  518.8 98.9 %all_to_all.10 = bf16[64,6,3584]{2,1,0:T(8,128)(2,1)} all-to-all(bf16[64,6,3584]{2,1,0:T(8,128)(2,1)} %reshape.59), channel_id=1, replica_groups=mesh['dx'=2,'dc'=2,'zh'=2,'er'=32] {'zh','er'}, dimensions={0} | all-to-all | bytes 5505024 | tf_op jit(solution)/shard_map/all_to_all | solution.py:83
  617.7 0.0 copy-start
  617.7 4.0 reshape.60
  621.7 0.0 copy-done
  621.7 2.4 fusion.2
  624.1 0.0 reduce-scatter.3.cloned.1.call-done
  624.1 17.4 %reduce-scatter.5.cloned.1.call-done = bf16[256,3584]{1,0:T(8,128)(2,1)} async-done(((bf16[512,3584]{1,0:T(8,128)(2,1)}), bf16[256,3584]{1,0:T(8,128)(2,1)}) %reduce-scatter.5.cloned.1.call-update) | async-done | bytes 1835024 | tf_op jit(solution)/shard_map/reduce_scatter | solution.py:81
  (6 shorter events, 0.1 us)
Async XLA Ops:
  7.2 6.3 copy-start.2
  25.4 333.9 %all-to-all-start = ((bf16[64,6,7168]{2,1,0:T(8,128)(2,1)}), bf16[64,6,7168]{2,1,0:T(8,128)(2,1)}, u32[]{:S(2)}, u32[]{:S(2)}) async-start(bf16[64,6,7168]{2,1,0:T(8,128)(2,1)} %reshape.57), calls=%async_computation | async-start | bytes 14680064 | tf_op jit(solution)/shard_map/all_to_all | solution.py:51
  37.7 1.6 copy-start.3
  37.7 172.4 %all-gather.7.cloned.1.call-start = ((), (), s32[]{:S(2)}) async-start(), calls=%async_computation.4 | async-start | bytes 5505024 | tf_op jit(solution)/shard_map/all_gather | solution.py:30
  38.5 329.3 %all-gather.9.cloned.1.call-start = ((), (), s32[]{:S(2)}) async-start(), calls=%async_computation.5 | async-start | bytes 5505024 | tf_op jit(solution)/shard_map/all_gather | solution.py:30
  39.2 373.6 %all-gather.11.cloned.1.call-start = ((), (), s32[]{:S(2)}) async-start(), calls=%async_computation.8 | async-start | bytes 5505024 | tf_op jit(solution)/shard_map/all_gather | solution.py:34
  213.6 258.3 %all-gather.13.cloned.1.call-start = ((), (), s32[]{:S(2)}) async-start(), calls=%async_computation.9 | async-start | bytes 5505024 | tf_op jit(solution)/shard_map/all_gather | solution.py:35
  367.8 114.5 %collective-permute-start = (bf16[384,7168]{1,0:T(8,128)(2,1)}, bf16[384,7168]{1,0:T(8,128)(2,1)}, u32[]{:S(2)}, u32[]{:S(2)}) collective-permute-start(bf16[384,7168]{1,0:T(8,128)(2,1)} %reshape.58), channel_id=1, source_target_pairs={{0,64},{64,0},{1,65},{65,1},{2,66},{66,2},{3,67},{67,3},{4,68},{68... | collective-permute-start | bytes 16515080 | tf_op jit(solution)/shard_map/ppermute | solution.py:8
  371.8 252.3 %reduce-scatter.3.cloned.1.call-start = ((), (), s32[]{:S(2)}) async-start(), calls=%async_computation.6 | async-start | bytes 5505024 | tf_op jit(solution)/shard_map/reduce_scatter | solution.py:80
  482.3 4.6 copy-start.1
  482.3 8.3 %slice-start = ((s8[7340032]{0:T(1024)(128)(4,1)}), s8[4194304]{0:T(1024)(128)(4,1)S(1)}, s32[]{:S(2)}) async-start(s8[7340032]{0:T(1024)(128)(4,1)} %bitcast.53), calls=%async_computation.10 | async-start | bytes 8388608
  486.9 3.7 slice-start.1
  496.4 145.1 %reduce-scatter.5.cloned.1.call-start = ((), (), s32[]{:S(2)}) async-start(), calls=%async_computation.7 | async-start | bytes 5505024 | tf_op jit(solution)/shard_map/reduce_scatter | solution.py:81
  501.7 9.8 %collective-permute-start.1 = (bf16[384,3584]{1,0:T(8,128)(2,1)}, bf16[384,3584]{1,0:T(8,128)(2,1)}, u32[]{:S(2)}, u32[]{:S(2)}) collective-permute-start(bf16[384,3584]{1,0:T(8,128)(2,1)} %convolution_convert_fusion.1), channel_id=1, source_target_pairs={{0,64},{64,0},{1,65},{65,1},{2,66},{66,2},{3,67},{67,3},{4,68},{68... | collective-permute-start | bytes 8257544 | tf_op jit(solution)/shard_map/ppermute | solution.py:8
  617.7 4.0 copy-start
Sparse Core Ops, SparseCore 0:
  40.4 169.7 all-gather.6
  211.9 142.5 all-gather.8
  356.9 55.8 all-gather.10
  415.0 56.8 all-gather.12
  496.5 77.2 reduce-scatter.2
  576.9 64.5 reduce-scatter.4

commit v8 on v4

--- a/solution.py
+++ b/solution.py
@@ -37,9 +37,6 @@
     their_in, their_out = partner_2((quarter_in, quarter_out), "expert", pair_bit)
     quarter_in = jnp.where(flagged, their_in, quarter_in)
     quarter_out = jnp.where(flagged, their_out, quarter_out)
-    halves = lax.all_gather(jnp.stack([quarter_in, quarter_out]), "dx", axis=1, tiled=True)
-    half_in = halves[0]
-    half_out = halves[1]
 
     flat_ids = expert_ids.reshape(-1)
     target_of = partner[flat_ids]
@@ -55,6 +52,10 @@
     scaled = (gates.reshape(-1)[:, None] * route_cot.astype(jnp.float32)).astype(jnp.bfloat16)
     payload = jnp.concatenate([route_rows, scaled], axis=1)
     send = jnp.dot(select, payload, preferred_element_type=jnp.float32).astype(jnp.bfloat16)
+    send, quarters = lax.optimization_barrier((send, jnp.stack([quarter_in, quarter_out])))
+    halves = lax.all_gather(quarters, "dx", axis=1, tiled=True)
+    half_in = halves[0]
+    half_out = halves[1]
     recv = lax.all_to_all(
         send.reshape(expert_count, capacity, 2 * width), "expert",
         split_axis=0, concat_axis=0, tiled=True,

time: 652 us -> 561 us (0.86)
  waiting for transfers between devices: 413 us -> 323 us
    ppermute x2, waiting for transfers between devices: 294 us -> 144 us  [partner_2(): return lax.ppermute(block, axis, route)]
    all_to_all x1, waiting for transfers between devices: 12 us -> 161 us  [body(): lax.all_to_all(send.reshape(expert_count, capacity, 2 * width), 'expert',...]
    all_gather x1, waiting for transfers between devices: 87.8 us -> 0.01 us  [body(): halves = lax.all_gather(quarters, 'dx', axis=1, tiled=True)]
  transfers between devices with their start and end apart: 7 -> 7, of which waited for: 6 -> 5; matrix products, arithmetic and copies ran while one was open for 8% -> 10% of each run, Pallas kernels for 0% -> 0%
where the time goes in v8:
time: 561 us; the launch traced here: 557 us
  waiting for transfers between devices  323 us (58%)
  blocking collectives  93.8 us (17%)
  matrix products  58 us (10%)
  local copies, waits for them, and re-layouts  34.6 us (6%)
  starting transfers between devices  21.7 us (4%)
  between operations  14.9 us (3%)
  other arithmetic  10.3 us (2%)
    all_to_all x1, waiting for transfers between devices, body(): lax.all_to_all(send.reshape(expert_count, capacity, 2 * width), 'expert',...  161 us
    ppermute x2, waiting for transfers between devices, partner_2(): return lax.ppermute(block, axis, route)  144 us
    all_to_all x1, blocking collectives, body(): lax.all_to_all(expert_out.reshape(expert_count, capacity, width), 'expert...  93.8 us
    dot_general x2, matrix products, expert_pass(): lax.dot_general(dpre, rows, contract_first, preferred_element_type=jnp.fl...  21.8 us
    all_to_all x1, starting transfers between devices, body(): lax.all_to_all(send.reshape(expert_count, capacity, 2 * width), 'expert',...  15.1 us
    reduce_scatter x1, waiting for transfers between devices, body(): lax.psum_scatter(terms, 'dx', scatter_dimension=1, tiled=True)  12.9 us
    dot_general x2, matrix products, expert_pass(): lax.dot_general(hidden, grads, contract_first, preferred_element_type=jnp...  11.4 us
  transfers between devices with their start and end apart: 7, of which 5 were waited for; matrix products, arithmetic and copies ran while one was open for 10% of the time, Pallas kernels for 0%

profile of v8, /device:TPU:192, one launch (start us, length us, event | category | flops | bytes accessed | tf_op | source)
XLA Modules:
  0.0 556.7 jit_solution(3997892410622889340)
XLA Ops:
  7.2 0.0 copy-start.4
  7.2 0.0 copy-start.5
  7.2 0.0 copy-start.3
  7.2 2.8 copy.13
  10.0 0.6 collective-permute-start
  10.6 5.4 collective-permute-start.1
  16.0 0.0 copy-done.4
  16.0 0.0 copy-done.5
  16.0 1.9 gather_fusion
  17.9 0.6 dynamic_slice.3
  18.5 0.6 reduce-window.6
  19.1 0.0 copy-done.3
  19.1 3.2 multiply_convert_fusion
  22.3 0.2 slice_reduce_fusion
  23.2 0.1 fusion.56
  23.3 6.1 %convolution_convert_fusion = bf16[384,7168]{1,0:T(8,128)(2,1)} fusion(bf16[256,3584]{1,0:T(8,128)(2,1)} %multiply_convert_fusion, bf16[256,3584]{1,0:T(8,128)(2,1)} %param.7, s32[256]{0:T(256)S(1)} %add_add_fusion), kind=kOutput, calls=%fused_computation.1 | convolution fusion | flops 1419476992 | bytes 9176064 | tf_op jit(solution)/shard_map/dot_general | solution.py:54
  29.3 0.0 copy-start.2
  29.3 99.0 %collective-permute-done = bf16[256,3584]{1,0:T(8,128)(2,1)} collective-permute-done((bf16[256,3584]{1,0:T(8,128)(2,1)S(1)}, bf16[256,3584]{1,0:T(8,128)(2,1)}, u32[]{:S(2)}, u32[]{:S(2)}) %collective-permute-start) | collective-permute-done | bytes 1835040 | tf_op jit(solution)/shard_map/ppermute | solution.py:14
  128.4 0.2 select_bitcast_fusion.1
  128.6 44.6 %collective-permute-done.1 = bf16[256,3584]{1,0:T(8,128)(2,1)} collective-permute-done((bf16[256,3584]{1,0:T(8,128)(2,1)}, bf16[256,3584]{1,0:T(8,128)(2,1)}, u32[]{:S(2)}, u32[]{:S(2)}) %collective-permute-start.1) | collective-permute-done | bytes 1835040 | tf_op jit(solution)/shard_map/ppermute | solution.py:14
  173.2 0.0 copy-done.2
  173.2 0.2 select_bitcast_fusion
  173.4 2.1 pad_maximum_fusion.1
  175.5 8.3 %reshape.53 = bf16[64,6,7168]{2,1,0:T(8,128)(2,1)} reshape(bf16[384,7168]{1,0:T(8,128)(2,1)} %convolution_convert_fusion) | data formatting | bytes 11010048 | tf_op jit(solution)/shard_map/reshape | solution.py:60
  183.8 15.1 %all-to-all-start = ((bf16[64,6,7168]{2,1,0:T(8,128)(2,1)}), bf16[64,6,7168]{2,1,0:T(8,128)(2,1)}, u32[]{:S(2)}, u32[]{:S(2)}) async-start(bf16[64,6,7168]{2,1,0:T(8,128)(2,1)} %reshape.53), calls=%async_computation | async-start | bytes 14680064 | tf_op jit(solution)/shard_map/all_to_all | solution.py:59
  198.9 0.0 all-gather.2.cloned.1.call-start
  198.9 0.7 all-gather.2.cloned.1.call-update
  199.6 0.0 reduce-scatter.2.cloned.1.call-start
  199.7 161.4 %all-to-all-done = bf16[64,6,7168]{2,1,0:T(8,128)(2,1)} async-done(((bf16[64,6,7168]{2,1,0:T(8,128)(2,1)}), bf16[64,6,7168]{2,1,0:T(8,128)(2,1)}, u32[]{:S(2)}, u32[]{:S(2)}) %all-to-all-start) | async-done | bytes 5505056 | tf_op jit(solution)/shard_map/all_to_all | solution.py:59
  361.1 8.5 %reshape.54 = bf16[384,7168]{1,0:T(8,128)(2,1)} reshape(bf16[64,6,7168]{2,1,0:T(8,128)(2,1)} %all-to-all-done) | data formatting | bytes 11010048 | tf_op jit(solution)/shard_map/reshape | solution.py:62
  369.6 0.0 collective-permute-start.2
  369.6 0.0 all-gather.2.cloned.1.call-done
  369.6 0.0 copy-start
  369.6 4.6 fusion.9
  374.2 0.0 copy-done
  374.2 5.2 fusion.13
  379.4 10.3 %fusion.19 = f32[512,3584]{1,0:T(8,128)} fusion(bf16[384,7168]{1,0:T(8,128)(2,1)} %reshape.54, bf16[2,512,3584]{2,1,0:T(8,128)(2,1)} %all-gather.2.cloned.1.call-done, f32[384,512]{1,0:T(8,128)S(1)} %fusion.9), kind=kOutput, calls=%fused_computation.31 | convolution fusion | flops 2820341760 | bytes 17301504 | tf_op jit(solution)/shard_map/dot_general | solution.py:77
  389.7 0.0 collective-permute-done.2
  389.7 4.5 fusion.8
  394.2 11.4 %fusion = bf16[1,512,3584]{2,1,0:T(8,128)(2,1)} fusion(f32[512,3584]{1,0:T(8,128)} %fusion.19, bf16[384,7168]{1,0:T(8,128)(2,1)} %collective-permute-done.2, bf16[2,512,3584]{2,1,0:T(8,128)(2,1)} %all-gather.2.cloned.1.call-done, f32[384,512]{1,0:T(8,128)S(1)} %fusion.8), kind=kOutput, calls=%fused_computation.7 | convolution fusion | flops 2824011776 | bytes 20971520 | tf_op jit(solution)/shard_map/dot_general | solution.py:77
  405.7 0.0 copy-start.1
  405.7 6.2 %fusion.1 = bf16[1,512,3584]{2,1,0:T(8,128)(2,1)S(1)} fusion(f32[512,3584]{1,0:T(8,128)} %fusion.13, bf16[384,7168]{1,0:T(8,128)(2,1)} %collective-permute-done.2, f32[384,512]{1,0:T(8,128)S(1)} %fusion.8), kind=kOutput, calls=%fused_computation.8 | convolution fusion | flops 1413939200 | bytes 14548992 | tf_op jit(solution)/shard_map/dot_general | solution.py:78
  411.9 0.0 copy-done.1
  411.9 3.9 pad_maximum_fusion
  415.7 0.0 reduce-scatter.2.cloned.1.call-update
  415.8 3.6 convolution_convert_fusion.1
  419.4 0.6 collective-permute-start.3
  420.0 4.7 collective-permute-done.3
  424.7 3.7 add_convert_fusion.2
  428.4 2.7 reshape.55
  431.1 93.8 %all_to_all.10 = bf16[64,6,3584]{2,1,0:T(8,128)(2,1)} all-to-all(bf16[64,6,3584]{2,1,0:T(8,128)(2,1)} %reshape.55), channel_id=1, replica_groups=mesh['dx'=2,'dc'=2,'expert'=64] {'expert'}, dimensions={0} | all-to-all | bytes 5505024 | tf_op jit(solution)/shard_map/all_to_all | solution.py:91
  524.9 4.0 reshape.56
  528.8 2.4 fusion.4
  531.2 12.9 %reduce-scatter.2.cloned.1.call-done = bf16[2,256,3584]{2,1,0:T(8,128)(2,1)} async-done(((bf16[2,512,3584]{2,1,0:T(8,128)(2,1)}), bf16[2,256,3584]{2,1,0:T(8,128)(2,1)}) %reduce-scatter.2.cloned.1.call-update) | async-done | bytes 3670032 | tf_op jit(solution)/shard_map/reduce_scatter | solution.py:87
  544.1 3.5 fusion.61
  547.6 2.2 copy.14
  (7 shorter events, 0.1 us)
Async XLA Ops:
  7.2 8.8 %copy-start.4 = (s32[256,1]{0,1:T(1,128)S(1)}, s32[256,1]{0,1:T(1,128)}, u32[]{:S(2)}) copy-start(s32[256,1]{0,1:T(1,128)} %param.9) | copy-start | bytes 3076
  7.2 8.8 %copy-start.5 = (s32[64]{0:T(128)S(1)}, s32[64]{0:T(128)}, u32[]{:S(2)}) copy-start(s32[64]{0:T(128)} %param.11) | copy-start | bytes 772
  7.2 11.9 %copy-start.3 = (f32[256,1]{0,1:T(1,128)S(1)}, f32[256,1]{0,1:T(1,128)}, u32[]{:S(2)}) copy-start(f32[256,1]{0,1:T(1,128)} %param.10) | copy-start | bytes 3076
  10.0 118.4 %collective-permute-start = (bf16[256,3584]{1,0:T(8,128)(2,1)S(1)}, bf16[256,3584]{1,0:T(8,128)(2,1)}, u32[]{:S(2)}, u32[]{:S(2)}) collective-permute-start(bf16[256,3584]{1,0:T(8,128)(2,1)S(1)} %bitcast.68), channel_id=1, source_target_pairs={{0,32},{32,0},{1,33},{33,1},{2,34},{34,2},{3,35},{35,3},{4,36},{36... | collective-permute-start | bytes 5505032 | tf_op jit(solution)/shard_map/ppermute | solution.py:14
  10.6 162.6 %collective-permute-start.1 = (bf16[256,3584]{1,0:T(8,128)(2,1)}, bf16[256,3584]{1,0:T(8,128)(2,1)}, u32[]{:S(2)}, u32[]{:S(2)}) collective-permute-start(bf16[256,3584]{1,0:T(8,128)(2,1)} %bitcast.69), channel_id=1, source_target_pairs={{0,32},{32,0},{1,33},{33,1},{2,34},{34,2},{3,35},{35,3},{4,36},{36... | collective-permute-start | bytes 5505032 | tf_op jit(solution)/shard_map/ppermute | solution.py:14
  29.3 143.9 %copy-start.2 = (bf16[1,256,3584]{2,1,0:T(8,128)(2,1)S(1)}, bf16[1,256,3584]{2,1,0:T(8,128)(2,1)}, u32[]{:S(2)}) copy-start(bf16[1,256,3584]{2,1,0:T(8,128)(2,1)} %param.13) | copy-start | bytes 5505028
  183.8 177.3 %all-to-all-start = ((bf16[64,6,7168]{2,1,0:T(8,128)(2,1)}), bf16[64,6,7168]{2,1,0:T(8,128)(2,1)}, u32[]{:S(2)}, u32[]{:S(2)}) async-start(bf16[64,6,7168]{2,1,0:T(8,128)(2,1)} %reshape.53), calls=%async_computation | async-start | bytes 14680064 | tf_op jit(solution)/shard_map/all_to_all | solution.py:59
  198.9 170.7 %all-gather.2.cloned.1.call-start = ((), (), s32[]{:S(2)}) async-start(), calls=%async_computation.3 | async-start | bytes 11010048 | tf_op jit(solution)/shard_map/all_gather | solution.py:56
  199.6 344.5 %reduce-scatter.2.cloned.1.call-start = ((), (), s32[]{:S(2)}) async-start(), calls=%async_computation.4 | async-start | bytes 11010048 | tf_op jit(solution)/shard_map/reduce_scatter | solution.py:87
  369.6 20.1 %collective-permute-start.2 = (bf16[384,7168]{1,0:T(8,128)(2,1)}, bf16[384,7168]{1,0:T(8,128)(2,1)}, u32[]{:S(2)}, u32[]{:S(2)}) collective-permute-start(bf16[384,7168]{1,0:T(8,128)(2,1)} %reshape.54), channel_id=1, source_target_pairs={{0,64},{64,0},{1,65},{65,1},{2,66},{66,2},{3,67},{67,3},{4,68},{68... | collective-permute-start | bytes 16515080 | tf_op jit(solution)/shard_map/ppermute | solution.py:18
  369.6 4.6 copy-start
  405.7 6.2 %copy-start.1 = (bf16[1,512,3584]{2,1,0:T(8,128)(2,1)S(1)}, bf16[1,512,3584]{2,1,0:T(8,128)(2,1)}, u32[]{:S(2)}) copy-start(bf16[1,512,3584]{2,1,0:T(8,128)(2,1)} %fusion) | copy-start | bytes 11010052
  419.4 5.3 collective-permute-start.3
Sparse Core Ops, SparseCore 0:
  201.5 156.8 all-gather.1
  415.9 128.1 reduce-scatter.1

commit v9 on v8

--- a/solution.py
+++ b/solution.py
@@ -34,7 +34,9 @@
 
     quarter_in = w_in[0].T
     quarter_out = w_out[0]
-    their_in, their_out = partner_2((quarter_in, quarter_out), "expert", pair_bit)
+    their_in = partner_2(quarter_in, "expert", pair_bit)
+    their_in, quarter_out = lax.optimization_barrier((their_in, quarter_out))
+    their_out = partner_2(quarter_out, "expert", pair_bit)
     quarter_in = jnp.where(flagged, their_in, quarter_in)
     quarter_out = jnp.where(flagged, their_out, quarter_out)
 

time: 561 us -> 563 us (level)
  waiting for transfers between devices: 323 us -> 330 us
  starting transfers between devices: 21.7 us -> 14.8 us
  transfers between devices with their start and end apart: 7 -> 7, of which waited for: 5 -> 5; matrix products, arithmetic and copies ran while one was open for 10% -> 11% of each run, Pallas kernels for 0% -> 0%
where the time goes in v9:
time: 563 us; the launch traced here: 559 us
  waiting for transfers between devices  330 us (59%)
  blocking collectives  94.1 us (17%)
  matrix products  58 us (10%)
  local copies, waits for them, and re-layouts  34.6 us (6%)
  between operations  14.9 us (3%)
  starting transfers between devices  14.8 us (3%)
  other arithmetic  13.3 us (2%)
    all_to_all x1, waiting for transfers between devices, body(): lax.all_to_all(send.reshape(expert_count, capacity, 2 * width), 'expert',...  164 us
    ppermute x2, waiting for transfers between devices, partner_2(): return lax.ppermute(block, axis, route)  148 us
    all_to_all x1, blocking collectives, body(): lax.all_to_all(expert_out.reshape(expert_count, capacity, width), 'expert...  94.1 us
    dot_general x2, matrix products, expert_pass(): lax.dot_general(dpre, rows, contract_first, preferred_element_type=jnp.fl...  21.7 us
    reduce_scatter x1, waiting for transfers between devices, body(): lax.psum_scatter(terms, 'dx', scatter_dimension=1, tiled=True)  12.9 us
    all_to_all x1, starting transfers between devices, body(): lax.all_to_all(send.reshape(expert_count, capacity, 2 * width), 'expert',...  12.4 us
    dot_general x2, matrix products, expert_pass(): lax.dot_general(hidden, grads, contract_first, preferred_element_type=jnp...  11.3 us
  transfers between devices with their start and end apart: 7, of which 5 were waited for; matrix products, arithmetic and copies ran while one was open for 11% of the time, Pallas kernels for 0%

profile of v9, /device:TPU:192, one launch (start us, length us, event | category | flops | bytes accessed | tf_op | source)
XLA Modules:
  0.0 559.3 jit_solution(101479850922568996)
XLA Ops:
  7.2 0.0 copy-start.4
  7.2 0.0 copy-start.3
  7.2 0.0 copy-start.2
  7.2 2.8 copy.13
  10.0 0.6 collective-permute-start
  10.6 0.0 copy-done.4
  10.6 0.6 dynamic_slice.3
  11.2 0.0 copy-done.3
  11.2 1.9 gather_fusion
  13.1 0.6 reduce-window.6
  13.7 0.0 copy-done.2
  13.7 3.2 multiply_convert_fusion
  16.9 79.1 %collective-permute-done = bf16[256,3584]{1,0:T(8,128)(2,1)} collective-permute-done((bf16[256,3584]{1,0:T(8,128)(2,1)S(1)}, bf16[256,3584]{1,0:T(8,128)(2,1)}, u32[]{:S(2)}, u32[]{:S(2)}) %collective-permute-start) | collective-permute-done | bytes 1835040 | tf_op jit(solution)/shard_map/ppermute | solution.py:14
  96.0 1.2 collective-permute-start.1
  97.2 0.2 slice_reduce_fusion
  98.0 0.1 fusion.56
  98.1 6.0 %convolution_convert_fusion = bf16[384,7168]{1,0:T(8,128)(2,1)} fusion(bf16[256,3584]{1,0:T(8,128)(2,1)} %multiply_convert_fusion, bf16[256,3584]{1,0:T(8,128)(2,1)} %param.7, s32[256]{0:T(256)S(1)} %add_add_fusion), kind=kOutput, calls=%fused_computation.1 | convolution fusion | flops 1419476992 | bytes 9176064 | tf_op jit(solution)/shard_map/dot_general | solution.py:56
  104.2 1.7 select_bitcast_fusion.1
  105.9 68.5 %collective-permute-done.1 = bf16[256,3584]{1,0:T(8,128)(2,1)} collective-permute-done((bf16[256,3584]{1,0:T(8,128)(2,1)}, bf16[256,3584]{1,0:T(8,128)(2,1)}, u32[]{:S(2)}, u32[]{:S(2)}) %collective-permute-start.1) | collective-permute-done | bytes 1835040 | tf_op jit(solution)/shard_map/ppermute | solution.py:14
  174.4 1.7 select_bitcast_fusion
  176.1 2.1 pad_maximum_fusion.1
  178.2 8.3 %reshape.53 = bf16[64,6,7168]{2,1,0:T(8,128)(2,1)} reshape(bf16[384,7168]{1,0:T(8,128)(2,1)} %convolution_convert_fusion) | data formatting | bytes 11010048 | tf_op jit(solution)/shard_map/reshape | solution.py:62
  186.5 12.4 %all-to-all-start = ((bf16[64,6,7168]{2,1,0:T(8,128)(2,1)}), bf16[64,6,7168]{2,1,0:T(8,128)(2,1)}, u32[]{:S(2)}, u32[]{:S(2)}) async-start(bf16[64,6,7168]{2,1,0:T(8,128)(2,1)} %reshape.53), calls=%async_computation | async-start | bytes 14680064 | tf_op jit(solution)/shard_map/all_to_all | solution.py:61
  198.9 0.0 all-gather.2.cloned.1.call-start
  198.9 0.7 all-gather.2.cloned.1.call-update
  199.6 0.0 reduce-scatter.2.cloned.1.call-start
  199.6 163.6 %all-to-all-done = bf16[64,6,7168]{2,1,0:T(8,128)(2,1)} async-done(((bf16[64,6,7168]{2,1,0:T(8,128)(2,1)}), bf16[64,6,7168]{2,1,0:T(8,128)(2,1)}, u32[]{:S(2)}, u32[]{:S(2)}) %all-to-all-start) | async-done | bytes 5505056 | tf_op jit(solution)/shard_map/all_to_all | solution.py:61
  363.3 8.5 %reshape.54 = bf16[384,7168]{1,0:T(8,128)(2,1)} reshape(bf16[64,6,7168]{2,1,0:T(8,128)(2,1)} %all-to-all-done) | data formatting | bytes 11010048 | tf_op jit(solution)/shard_map/reshape | solution.py:64
  371.8 0.0 collective-permute-start.2
  371.8 0.0 all-gather.2.cloned.1.call-done
  371.8 0.0 copy-start
  371.8 4.6 fusion.9
  376.4 0.0 copy-done
  376.4 5.2 fusion.13
  381.6 10.3 %fusion.19 = f32[512,3584]{1,0:T(8,128)} fusion(bf16[384,7168]{1,0:T(8,128)(2,1)} %reshape.54, bf16[2,512,3584]{2,1,0:T(8,128)(2,1)} %all-gather.2.cloned.1.call-done, f32[384,512]{1,0:T(8,128)S(1)} %fusion.9), kind=kOutput, calls=%fused_computation.31 | convolution fusion | flops 2820341760 | bytes 17301504 | tf_op jit(solution)/shard_map/dot_general | solution.py:79
  391.9 0.0 collective-permute-done.2
  391.9 4.5 fusion.8
  396.4 11.4 %fusion = bf16[1,512,3584]{2,1,0:T(8,128)(2,1)} fusion(f32[512,3584]{1,0:T(8,128)} %fusion.19, bf16[384,7168]{1,0:T(8,128)(2,1)} %collective-permute-done.2, bf16[2,512,3584]{2,1,0:T(8,128)(2,1)} %all-gather.2.cloned.1.call-done, f32[384,512]{1,0:T(8,128)S(1)} %fusion.8), kind=kOutput, calls=%fused_computation.7 | convolution fusion | flops 2824011776 | bytes 20971520 | tf_op jit(solution)/shard_map/dot_general | solution.py:79
  407.8 0.0 copy-start.1
  407.8 6.2 %fusion.1 = bf16[1,512,3584]{2,1,0:T(8,128)(2,1)S(1)} fusion(f32[512,3584]{1,0:T(8,128)} %fusion.13, bf16[384,7168]{1,0:T(8,128)(2,1)} %collective-permute-done.2, f32[384,512]{1,0:T(8,128)S(1)} %fusion.8), kind=kOutput, calls=%fused_computation.8 | convolution fusion | flops 1413939200 | bytes 14548992 | tf_op jit(solution)/shard_map/dot_general | solution.py:80
  414.0 0.0 copy-done.1
  414.0 3.9 pad_maximum_fusion
  417.9 0.0 reduce-scatter.2.cloned.1.call-update
  417.9 3.6 convolution_convert_fusion.1
  421.6 0.6 collective-permute-start.3
  422.1 4.7 collective-permute-done.3
  426.9 3.7 add_convert_fusion.2
  430.6 2.7 reshape.55
  433.2 94.1 %all_to_all.10 = bf16[64,6,3584]{2,1,0:T(8,128)(2,1)} all-to-all(bf16[64,6,3584]{2,1,0:T(8,128)(2,1)} %reshape.55), channel_id=1, replica_groups=mesh['dx'=2,'dc'=2,'expert'=64] {'expert'}, dimensions={0} | all-to-all | bytes 5505024 | tf_op jit(solution)/shard_map/all_to_all | solution.py:93
  527.4 4.0 reshape.56
  531.4 2.4 fusion.4
  533.8 12.9 %reduce-scatter.2.cloned.1.call-done = bf16[2,256,3584]{2,1,0:T(8,128)(2,1)} async-done(((bf16[2,512,3584]{2,1,0:T(8,128)(2,1)}), bf16[2,256,3584]{2,1,0:T(8,128)(2,1)}) %reduce-scatter.2.cloned.1.call-update) | async-done | bytes 3670032 | tf_op jit(solution)/shard_map/reduce_scatter | solution.py:89
  546.7 3.5 fusion.61
  550.2 2.2 copy.14
  (7 shorter events, 0.1 us)
Async XLA Ops:
  7.2 3.4 copy-start.4
  7.2 4.0 copy-start.3
  7.2 6.5 %copy-start.2 = (f32[256,1]{0,1:T(1,128)S(1)}, f32[256,1]{0,1:T(1,128)}, u32[]{:S(2)}) copy-start(f32[256,1]{0,1:T(1,128)} %param.10) | copy-start | bytes 3076
  10.0 86.0 %collective-permute-start = (bf16[256,3584]{1,0:T(8,128)(2,1)S(1)}, bf16[256,3584]{1,0:T(8,128)(2,1)}, u32[]{:S(2)}, u32[]{:S(2)}) collective-permute-start(bf16[256,3584]{1,0:T(8,128)(2,1)S(1)} %bitcast.67), channel_id=1, source_target_pairs={{0,32},{32,0},{1,33},{33,1},{2,34},{34,2},{3,35},{35,3},{4,36},{36... | collective-permute-start | bytes 5505032 | tf_op jit(solution)/shard_map/ppermute | solution.py:14
  96.0 78.4 %collective-permute-start.1 = (bf16[256,3584]{1,0:T(8,128)(2,1)}, bf16[256,3584]{1,0:T(8,128)(2,1)}, u32[]{:S(2)}, u32[]{:S(2)}) collective-permute-start(bf16[256,3584]{1,0:T(8,128)(2,1)} %bitcast.7), channel_id=1, source_target_pairs={{0,32},{32,0},{1,33},{33,1},{2,34},{34,2},{3,35},{35,3},{4,36},{36... | collective-permute-start | bytes 5505032 | tf_op jit(solution)/shard_map/ppermute | solution.py:14
  186.5 176.8 %all-to-all-start = ((bf16[64,6,7168]{2,1,0:T(8,128)(2,1)}), bf16[64,6,7168]{2,1,0:T(8,128)(2,1)}, u32[]{:S(2)}, u32[]{:S(2)}) async-start(bf16[64,6,7168]{2,1,0:T(8,128)(2,1)} %reshape.53), calls=%async_computation | async-start | bytes 14680064 | tf_op jit(solution)/shard_map/all_to_all | solution.py:61
  198.9 172.9 %all-gather.2.cloned.1.call-start = ((), (), s32[]{:S(2)}) async-start(), calls=%async_computation.3 | async-start | bytes 11010048 | tf_op jit(solution)/shard_map/all_gather | solution.py:58
  199.6 347.1 %reduce-scatter.2.cloned.1.call-start = ((), (), s32[]{:S(2)}) async-start(), calls=%async_computation.4 | async-start | bytes 11010048 | tf_op jit(solution)/shard_map/reduce_scatter | solution.py:89
  371.8 20.1 %collective-permute-start.2 = (bf16[384,7168]{1,0:T(8,128)(2,1)}, bf16[384,7168]{1,0:T(8,128)(2,1)}, u32[]{:S(2)}, u32[]{:S(2)}) collective-permute-start(bf16[384,7168]{1,0:T(8,128)(2,1)} %reshape.54), channel_id=1, source_target_pairs={{0,64},{64,0},{1,65},{65,1},{2,66},{66,2},{3,67},{67,3},{4,68},{68... | collective-permute-start | bytes 16515080 | tf_op jit(solution)/shard_map/ppermute | solution.py:18
  371.8 4.6 copy-start
  407.8 6.2 %copy-start.1 = (bf16[1,512,3584]{2,1,0:T(8,128)(2,1)S(1)}, bf16[1,512,3584]{2,1,0:T(8,128)(2,1)}, u32[]{:S(2)}) copy-start(bf16[1,512,3584]{2,1,0:T(8,128)(2,1)} %fusion) | copy-start | bytes 11010052
  421.6 5.3 collective-permute-start.3
Sparse Core Ops, SparseCore 0:
  201.5 158.6 all-gather.1
  418.0 128.5 reduce-scatter.1

commit v10 on v8

--- a/solution.py
+++ b/solution.py
@@ -83,10 +83,10 @@
     out_own, in_own, outg_own = expert_pass(recv)
     expert_out = (out_own + back.astype(jnp.float32)).astype(jnp.bfloat16)
 
-    terms = jnp.stack([in_own + in_other, outg_own + outg_other]).astype(jnp.bfloat16)
-    grad_quarters = lax.psum_scatter(terms, "dx", scatter_dimension=1, tiled=True)
-    grad_quarter_in = grad_quarters[0].T
-    grad_quarter_out = grad_quarters[1]
+    term_out = (outg_own + outg_other).astype(jnp.bfloat16)
+    grad_quarter_out = lax.psum_scatter(term_out, "dx", scatter_dimension=0, tiled=True)
+    term_in = (in_own + in_other).astype(jnp.bfloat16)
+    grad_quarter_in = lax.psum_scatter(term_in, "dx", scatter_dimension=0, tiled=True).T
 
     returned = lax.all_to_all(
         expert_out.reshape(expert_count, capacity, width), "expert",

time: 561 us -> 550 us (0.980)
  blocking collectives: 93.8 us -> 0 us
  waiting for transfers between devices: 323 us -> 406 us
    all_to_all x1 -> x0, blocking collectives: 93.8 us -> none  [body(): lax.all_to_all(expert_out.reshape(expert_count, capacity, width), 'expert...]
    reduce_scatter x1 -> x2, waiting for transfers between devices: 12.9 us -> 60.7 us  [the longest x1 43.6 us: body(): lax.psum_scatter(term_in, 'dx', scatter_dimension=0, tiled=True)]
    all_to_all x0 -> x1, waiting for transfers between devices: none -> 38.6 us  [body(): lax.all_to_all(expert_out.reshape(expert_count, capacity, width), 'expert...]
    all_to_all x0 -> x1, starting transfers between devices: none -> 6.96 us  [body(): lax.all_to_all(expert_out.reshape(expert_count, capacity, width), 'expert...]
  transfers between devices with their start and end apart: 7 -> 9, of which waited for: 5 -> 6; matrix products, arithmetic and copies ran while one was open for 10% -> 13% of each run, Pallas kernels for 0% -> 0%
where the time goes in v10:
time: 550 us; the launch traced here: 546 us
  waiting for transfers between devices  406 us (74%)
  matrix products  59.1 us (11%)
  local copies, waits for them, and re-layouts  32.6 us (6%)
  starting transfers between devices  27.2 us (5%)
  between operations  14.6 us (3%)
  other arithmetic  6.54 us (1%)
    all_to_all x1, waiting for transfers between devices, body(): lax.all_to_all(send.reshape(expert_count, capacity, 2 * width), 'expert',...  162 us
    ppermute x2, waiting for transfers between devices, partner_2(): return lax.ppermute(block, axis, route)  144 us
    reduce_scatter x1, waiting for transfers between devices, body(): lax.psum_scatter(term_in, 'dx', scatter_dimension=0, tiled=True)  43.6 us
    all_to_all x1, waiting for transfers between devices, body(): lax.all_to_all(expert_out.reshape(expert_count, capacity, width), 'expert...  38.6 us
    dot_general x2, matrix products, expert_pass(): lax.dot_general(dpre, rows, contract_first, preferred_element_type=jnp.fl...  21.8 us
    reduce_scatter x1, waiting for transfers between devices, body(): lax.psum_scatter(term_out, 'dx', scatter_dimension=0, tiled=True)  17.1 us
    all_to_all x1, starting transfers between devices, body(): lax.all_to_all(send.reshape(expert_count, capacity, 2 * width), 'expert',...  13.6 us
  transfers between devices with their start and end apart: 9, of which 6 were waited for; matrix products, arithmetic and copies ran while one was open for 13% of the time, Pallas kernels for 0%

profile of v10, /device:TPU:192, one launch (start us, length us, event | category | flops | bytes accessed | tf_op | source)
XLA Modules:
  0.0 545.8 jit_solution(1498264646794146193)
XLA Ops:
  7.2 0.0 copy-start.2
  7.2 0.0 copy-start.3
  7.2 0.0 copy-start.1
  7.2 2.8 copy.13
  10.0 0.6 collective-permute-start
  10.6 5.4 collective-permute-start.1
  16.0 0.0 copy-done.2
  16.0 0.0 copy-done.3
  16.0 1.9 gather_fusion
  17.9 0.6 dynamic_slice.3
  18.5 0.6 reduce-window.6
  19.1 0.0 copy-done.1
  19.1 3.2 multiply_convert_fusion
  22.3 0.2 slice_reduce_fusion
  23.2 0.1 fusion.54
  23.3 6.0 %convolution_convert_fusion = bf16[384,7168]{1,0:T(8,128)(2,1)} fusion(bf16[256,3584]{1,0:T(8,128)(2,1)} %multiply_convert_fusion, bf16[256,3584]{1,0:T(8,128)(2,1)} %param.7, s32[256]{0:T(256)S(1)} %add_add_fusion), kind=kOutput, calls=%fused_computation.1 | convolution fusion | flops 1419476992 | bytes 9176064 | tf_op jit(solution)/shard_map/dot_general | solution.py:54
  29.3 0.0 copy-start
  29.3 99.1 %collective-permute-done = bf16[256,3584]{1,0:T(8,128)(2,1)} collective-permute-done((bf16[256,3584]{1,0:T(8,128)(2,1)S(1)}, bf16[256,3584]{1,0:T(8,128)(2,1)}, u32[]{:S(2)}, u32[]{:S(2)}) %collective-permute-start) | collective-permute-done | bytes 1835040 | tf_op jit(solution)/shard_map/ppermute | solution.py:14
  128.4 0.2 select_bitcast_fusion.1
  128.6 44.6 %collective-permute-done.1 = bf16[256,3584]{1,0:T(8,128)(2,1)} collective-permute-done((bf16[256,3584]{1,0:T(8,128)(2,1)}, bf16[256,3584]{1,0:T(8,128)(2,1)}, u32[]{:S(2)}, u32[]{:S(2)}) %collective-permute-start.1) | collective-permute-done | bytes 1835040 | tf_op jit(solution)/shard_map/ppermute | solution.py:14
  173.2 0.0 copy-done
  173.2 0.2 select_bitcast_fusion
  173.4 2.2 pad_maximum_fusion
  175.6 8.3 %reshape.53 = bf16[64,6,7168]{2,1,0:T(8,128)(2,1)} reshape(bf16[384,7168]{1,0:T(8,128)(2,1)} %convolution_convert_fusion) | data formatting | bytes 11010048 | tf_op jit(solution)/shard_map/reshape | solution.py:60
  184.0 13.6 %all-to-all-start = ((bf16[64,6,7168]{2,1,0:T(8,128)(2,1)}), bf16[64,6,7168]{2,1,0:T(8,128)(2,1)}, u32[]{:S(2)}, u32[]{:S(2)}) async-start(bf16[64,6,7168]{2,1,0:T(8,128)(2,1)} %reshape.53), calls=%async_computation | async-start | bytes 14680064 | tf_op jit(solution)/shard_map/all_to_all | solution.py:59
  197.5 0.0 all-gather.2.cloned.1.call-start
  197.6 0.7 all-gather.2.cloned.1.call-update
  198.3 0.0 reduce-scatter.3.cloned.1.call-start
  198.3 162.2 %all-to-all-done = bf16[64,6,7168]{2,1,0:T(8,128)(2,1)} async-done(((bf16[64,6,7168]{2,1,0:T(8,128)(2,1)}), bf16[64,6,7168]{2,1,0:T(8,128)(2,1)}, u32[]{:S(2)}, u32[]{:S(2)}) %all-to-all-start) | async-done | bytes 5505056 | tf_op jit(solution)/shard_map/all_to_all | solution.py:59
  360.5 8.4 %reshape.54 = bf16[384,7168]{1,0:T(8,128)(2,1)} reshape(bf16[64,6,7168]{2,1,0:T(8,128)(2,1)} %all-to-all-done) | data formatting | bytes 11010048 | tf_op jit(solution)/shard_map/reshape | solution.py:62
  368.9 0.0 collective-permute-start.2
  368.9 0.0 all-gather.2.cloned.1.call-done
  368.9 4.5 fusion.7
  373.4 10.4 %fusion.17 = f32[512,3584]{1,0:T(8,128)} fusion(bf16[384,7168]{1,0:T(8,128)(2,1)} %reshape.54, bf16[2,512,3584]{2,1,0:T(8,128)(2,1)} %all-gather.2.cloned.1.call-done, f32[384,512]{1,0:T(8,128)S(1)} %fusion.7), kind=kOutput, calls=%fused_computation.28 | convolution fusion | flops 2820341760 | bytes 17301504 | tf_op jit(solution)/shard_map/dot_general | solution.py:77
  383.8 0.0 collective-permute-done.2
  383.8 4.5 fusion.6
  388.3 11.4 %add_convert_fusion.1 = bf16[512,3584]{1,0:T(8,128)(2,1)} fusion(f32[512,3584]{1,0:T(8,128)} %fusion.17, bf16[384,7168]{1,0:T(8,128)(2,1)} %collective-permute-done.2, bf16[2,512,3584]{2,1,0:T(8,128)(2,1)} %all-gather.2.cloned.1.call-done, f32[384,512]{1,0:T(8,128)S(1)} %fusion.6), kind=kOutput, calls=%fused_computation.3 | convolution fusion | flops 2824011776 | bytes 20971520 | tf_op jit(solution)/shard_map/dot_general | solution.py:77
  399.7 0.0 reduce-scatter.3.cloned.1.call-update
  399.7 0.0 reduce-scatter.5.cloned.1.call-start
  399.8 5.2 convolution_convert_fusion.1
  404.9 0.5 collective-permute-start.3
  405.4 4.4 fusion.11
  409.8 5.8 %add_convert_fusion = bf16[512,3584]{1,0:T(8,128)(2,1)} fusion(f32[512,3584]{1,0:T(8,128)S(1)} %fusion.11, bf16[384,7168]{1,0:T(8,128)(2,1)} %collective-permute-done.2, f32[384,512]{1,0:T(8,128)S(1)} %fusion.6), kind=kOutput, calls=%fused_computation.2 | convolution fusion | flops 1413939200 | bytes 14548992 | tf_op jit(solution)/shard_map/dot_general | solution.py:78
  415.6 0.0 reduce-scatter.5.cloned.1.call-update
  415.7 0.0 collective-permute-done.3
  415.7 4.5 add_convert_fusion.2
  420.2 2.7 reshape.55
  422.9 7.0 %all-to-all-start.1 = ((bf16[64,6,3584]{2,1,0:T(8,128)(2,1)}), bf16[64,6,3584]{2,1,0:T(8,128)(2,1)}, u32[]{:S(2)}, u32[]{:S(2)}) async-start(bf16[64,6,3584]{2,1,0:T(8,128)(2,1)} %reshape.55), calls=%async_computation.1 | async-start | bytes 7340032 | tf_op jit(solution)/shard_map/all_to_all | solution.py:91
  429.8 43.6 %reduce-scatter.3.cloned.1.call-done = bf16[256,3584]{1,0:T(8,128)(2,1)} async-done(((bf16[512,3584]{1,0:T(8,128)(2,1)}), bf16[256,3584]{1,0:T(8,128)(2,1)}) %reduce-scatter.3.cloned.1.call-update) | async-done | bytes 1835024 | tf_op jit(solution)/shard_map/reduce_scatter | solution.py:89
  473.4 3.8 copy.14
  477.2 38.6 %all-to-all-done.1 = bf16[64,6,3584]{2,1,0:T(8,128)(2,1)} async-done(((bf16[64,6,3584]{2,1,0:T(8,128)(2,1)}), bf16[64,6,3584]{2,1,0:T(8,128)(2,1)}, u32[]{:S(2)}, u32[]{:S(2)}) %all-to-all-start.1) | async-done | bytes 2752544 | tf_op jit(solution)/shard_map/all_to_all | solution.py:91
  515.8 4.0 reshape.56
  519.7 2.4 fusion.2
  522.1 17.1 %reduce-scatter.5.cloned.1.call-done = bf16[256,3584]{1,0:T(8,128)(2,1)} async-done(((bf16[512,3584]{1,0:T(8,128)(2,1)}), bf16[256,3584]{1,0:T(8,128)(2,1)}) %reduce-scatter.5.cloned.1.call-update) | async-done | bytes 1835024 | tf_op jit(solution)/shard_map/reduce_scatter | solution.py:87
  (7 shorter events, 0.1 us)
Async XLA Ops:
  7.2 8.8 %copy-start.2 = (s32[256,1]{0,1:T(1,128)S(1)}, s32[256,1]{0,1:T(1,128)}, u32[]{:S(2)}) copy-start(s32[256,1]{0,1:T(1,128)} %param.9) | copy-start | bytes 3076
  7.2 8.8 %copy-start.3 = (s32[64]{0:T(128)S(1)}, s32[64]{0:T(128)}, u32[]{:S(2)}) copy-start(s32[64]{0:T(128)} %param.11) | copy-start | bytes 772
  7.2 11.9 %copy-start.1 = (f32[256,1]{0,1:T(1,128)S(1)}, f32[256,1]{0,1:T(1,128)}, u32[]{:S(2)}) copy-start(f32[256,1]{0,1:T(1,128)} %param.10) | copy-start | bytes 3076
  10.0 118.4 %collective-permute-start = (bf16[256,3584]{1,0:T(8,128)(2,1)S(1)}, bf16[256,3584]{1,0:T(8,128)(2,1)}, u32[]{:S(2)}, u32[]{:S(2)}) collective-permute-start(bf16[256,3584]{1,0:T(8,128)(2,1)S(1)} %bitcast.62), channel_id=1, source_target_pairs={{0,32},{32,0},{1,33},{33,1},{2,34},{34,2},{3,35},{35,3},{4,36},{36... | collective-permute-start | bytes 5505032 | tf_op jit(solution)/shard_map/ppermute | solution.py:14
  10.6 162.6 %collective-permute-start.1 = (bf16[256,3584]{1,0:T(8,128)(2,1)}, bf16[256,3584]{1,0:T(8,128)(2,1)}, u32[]{:S(2)}, u32[]{:S(2)}) collective-permute-start(bf16[256,3584]{1,0:T(8,128)(2,1)} %bitcast.64), channel_id=1, source_target_pairs={{0,32},{32,0},{1,33},{33,1},{2,34},{34,2},{3,35},{35,3},{4,36},{36... | collective-permute-start | bytes 5505032 | tf_op jit(solution)/shard_map/ppermute | solution.py:14
  29.3 143.9 %copy-start = (bf16[1,256,3584]{2,1,0:T(8,128)(2,1)S(1)}, bf16[1,256,3584]{2,1,0:T(8,128)(2,1)}, u32[]{:S(2)}) copy-start(bf16[1,256,3584]{2,1,0:T(8,128)(2,1)} %param.13) | copy-start | bytes 5505028
  184.0 176.5 %all-to-all-start = ((bf16[64,6,7168]{2,1,0:T(8,128)(2,1)}), bf16[64,6,7168]{2,1,0:T(8,128)(2,1)}, u32[]{:S(2)}, u32[]{:S(2)}) async-start(bf16[64,6,7168]{2,1,0:T(8,128)(2,1)} %reshape.53), calls=%async_computation | async-start | bytes 14680064 | tf_op jit(solution)/shard_map/all_to_all | solution.py:59
  197.5 171.3 %all-gather.2.cloned.1.call-start = ((), (), s32[]{:S(2)}) async-start(), calls=%async_computation.4 | async-start | bytes 11010048 | tf_op jit(solution)/shard_map/all_gather | solution.py:56
  198.3 275.1 %reduce-scatter.3.cloned.1.call-start = ((), (), s32[]{:S(2)}) async-start(), calls=%async_computation.5 | async-start | bytes 5505024 | tf_op jit(solution)/shard_map/reduce_scatter | solution.py:89
  368.9 14.9 %collective-permute-start.2 = (bf16[384,7168]{1,0:T(8,128)(2,1)}, bf16[384,7168]{1,0:T(8,128)(2,1)}, u32[]{:S(2)}, u32[]{:S(2)}) collective-permute-start(bf16[384,7168]{1,0:T(8,128)(2,1)} %reshape.54), channel_id=1, source_target_pairs={{0,64},{64,0},{1,65},{65,1},{2,66},{66,2},{3,67},{67,3},{4,68},{68... | collective-permute-start | bytes 16515080 | tf_op jit(solution)/shard_map/ppermute | solution.py:18
  399.7 139.6 %reduce-scatter.5.cloned.1.call-start = ((), (), s32[]{:S(2)}) async-start(), calls=%async_computation.6 | async-start | bytes 5505024 | tf_op jit(solution)/shard_map/reduce_scatter | solution.py:87
  404.9 10.7 %collective-permute-start.3 = (bf16[384,3584]{1,0:T(8,128)(2,1)}, bf16[384,3584]{1,0:T(8,128)(2,1)}, u32[]{:S(2)}, u32[]{:S(2)}) collective-permute-start(bf16[384,3584]{1,0:T(8,128)(2,1)} %convolution_convert_fusion.1), channel_id=1, source_target_pairs={{0,64},{64,0},{1,65},{65,1},{2,66},{66,2},{3,67},{67,3},{4,68},{68... | collective-permute-start | bytes 8257544 | tf_op jit(solution)/shard_map/ppermute | solution.py:18
  422.9 92.9 %all-to-all-start.1 = ((bf16[64,6,3584]{2,1,0:T(8,128)(2,1)}), bf16[64,6,3584]{2,1,0:T(8,128)(2,1)}, u32[]{:S(2)}, u32[]{:S(2)}) async-start(bf16[64,6,3584]{2,1,0:T(8,128)(2,1)} %reshape.55), calls=%async_computation.1 | async-start | bytes 7340032 | tf_op jit(solution)/shard_map/all_to_all | solution.py:91
Sparse Core Ops, SparseCore 0:
  200.2 156.9 all-gather.1
  399.8 73.5 reduce-scatter.2
  476.6 62.5 reduce-scatter.4

commit v11 on v10

--- a/solution.py
+++ b/solution.py
@@ -85,8 +85,13 @@
 
     term_out = (outg_own + outg_other).astype(jnp.bfloat16)
     grad_quarter_out = lax.psum_scatter(term_out, "dx", scatter_dimension=0, tiled=True)
-    term_in = (in_own + in_other).astype(jnp.bfloat16)
-    grad_quarter_in = lax.psum_scatter(term_in, "dx", scatter_dimension=0, tiled=True).T
+    term_in = in_own + in_other
+    quarter = term_in.shape[0] // 2
+    first = lax.axis_index("dx") == 0
+    kept = jnp.where(first, term_in[:quarter], term_in[quarter:])
+    sent = jnp.where(first, term_in[quarter:], term_in[:quarter]).astype(jnp.bfloat16)
+    got = lax.ppermute(sent, "dx", [(0, 1), (1, 0)])
+    grad_quarter_in = (kept + got.astype(jnp.float32)).astype(jnp.bfloat16).T
 
     returned = lax.all_to_all(
         expert_out.reshape(expert_count, capacity, width), "expert",

time: 550 us -> 543 us (0.987)
  waiting for transfers between devices: 406 us -> 397 us
  other arithmetic: 6.54 us -> 14 us
  matrix products: 59.1 us -> 52.2 us
    ppermute x0 -> x1, waiting for transfers between devices: none -> 84.9 us  [body(): got = lax.ppermute(sent, 'dx', [(0, 1), (1, 0)])]
    reduce_scatter x1 -> x0, waiting for transfers between devices: 43.6 us -> none  [body(): lax.psum_scatter(term_in, 'dx', scatter_dimension=0, tiled=True)]
    all_to_all x1, waiting for transfers between devices: 38.6 us -> 0.01 us  [body(): lax.all_to_all(expert_out.reshape(expert_count, capacity, width), 'expert...]
    reduce_scatter x1, waiting for transfers between devices: 17.1 us -> 0.01 us  [body(): lax.psum_scatter(term_out, 'dx', scatter_dimension=0, tiled=True)]
    ppermute x2, waiting for transfers between devices: 0.01 us -> 9.37 us  [swap_core(): return lax.ppermute(block, 'dc', [(0, 1), (1, 0)])]
  transfers between devices with their start and end apart: 9 -> 9, of which waited for: 6 -> 5; matrix products, arithmetic and copies ran while one was open for 13% -> 15% of each run, Pallas kernels for 0% -> 0%
where the time goes in v11:
time: 543 us; the launch traced here: 539 us
  waiting for transfers between devices  397 us (73%)
  matrix products  52.2 us (10%)
  local copies, waits for them, and re-layouts  31.7 us (6%)
  starting transfers between devices  29.2 us (5%)
  between operations  14.9 us (3%)
  other arithmetic  14 us (3%)
    all_to_all x1, waiting for transfers between devices, body(): lax.all_to_all(send.reshape(expert_count, capacity, 2 * width), 'expert',...  161 us
    ppermute x2, waiting for transfers between devices, partner_2(): return lax.ppermute(block, axis, route)  141 us
    ppermute x1, waiting for transfers between devices, body(): got = lax.ppermute(sent, 'dx', [(0, 1), (1, 0)])  84.9 us
    dot_general x2, matrix products, expert_pass(): lax.dot_general(dpre, rows, contract_first, preferred_element_type=jnp.fl...  23.1 us
    all_to_all x1, starting transfers between devices, body(): lax.all_to_all(send.reshape(expert_count, capacity, 2 * width), 'expert',...  15.1 us
  transfers between devices with their start and end apart: 9, of which 5 were waited for; matrix products, arithmetic and copies ran while one was open for 15% of the time, Pallas kernels for 0%

profile of v11, /device:TPU:192, one launch (start us, length us, event | category | flops | bytes accessed | tf_op | source)
XLA Modules:
  0.0 539.1 jit_solution(1449336282911776781)
XLA Ops:
  7.2 0.0 copy-start.7
  7.2 0.0 copy-start.6
  7.2 0.0 copy-start.5
  7.2 0.6 collective-permute-start.1
  7.8 2.8 copy.13
  10.6 5.5 %collective-permute-start = (bf16[256,3584]{1,0:T(8,128)(2,1)S(1)}, bf16[256,3584]{1,0:T(8,128)(2,1)}, u32[]{:S(2)}, u32[]{:S(2)}) collective-permute-start(bf16[256,3584]{1,0:T(8,128)(2,1)S(1)} %bitcast.63), channel_id=1, source_target_pairs={{0,32},{32,0},{1,33},{33,1},{2,34},{34,2},{3,35},{35,3},{4,36},{36... | collective-permute-start | bytes 5505032 | tf_op jit(solution)/shard_map/ppermute | solution.py:14
  16.1 0.0 copy-done.7
  16.1 0.0 copy-done.6
  16.1 1.9 gather_fusion
  18.0 0.6 reduce-window.6
  18.6 0.0 copy-done.5
  18.6 3.2 multiply_convert_fusion
  21.8 0.2 slice_reduce_fusion
  22.0 0.6 dynamic_slice.3
  23.3 0.1 fusion.55
  23.4 0.0 copy-start.1
  23.4 6.2 %convolution_convert_fusion = bf16[384,7168]{1,0:T(8,128)(2,1)} fusion(bf16[256,3584]{1,0:T(8,128)(2,1)} %multiply_convert_fusion, bf16[256,3584]{1,0:T(8,128)(2,1)} %param.7, s32[256]{0:T(256)S(1)} %add_add_fusion), kind=kOutput, calls=%fused_computation.1 | convolution fusion | flops 1419476992 | bytes 9176064 | tf_op jit(solution)/shard_map/dot_general | solution.py:54
  29.6 96.2 %collective-permute-done.1 = bf16[256,3584]{1,0:T(8,128)(2,1)} collective-permute-done((bf16[256,3584]{1,0:T(8,128)(2,1)}, bf16[256,3584]{1,0:T(8,128)(2,1)}, u32[]{:S(2)}, u32[]{:S(2)}) %collective-permute-start.1) | collective-permute-done | bytes 1835040 | tf_op jit(solution)/shard_map/ppermute | solution.py:14
  125.8 0.0 copy-done.1
  125.8 0.2 select_bitcast_fusion
  126.0 44.6 %collective-permute-done = bf16[256,3584]{1,0:T(8,128)(2,1)} collective-permute-done((bf16[256,3584]{1,0:T(8,128)(2,1)S(1)}, bf16[256,3584]{1,0:T(8,128)(2,1)}, u32[]{:S(2)}, u32[]{:S(2)}) %collective-permute-start) | collective-permute-done | bytes 1835040 | tf_op jit(solution)/shard_map/ppermute | solution.py:14
  170.6 0.2 select_bitcast_fusion.1
  170.8 2.1 pad_maximum_fusion
  173.0 8.2 %reshape.53 = bf16[64,6,7168]{2,1,0:T(8,128)(2,1)} reshape(bf16[384,7168]{1,0:T(8,128)(2,1)} %convolution_convert_fusion) | data formatting | bytes 11010048 | tf_op jit(solution)/shard_map/reshape | solution.py:60
  181.2 15.1 %all-to-all-start = ((bf16[64,6,7168]{2,1,0:T(8,128)(2,1)}), bf16[64,6,7168]{2,1,0:T(8,128)(2,1)}, u32[]{:S(2)}, u32[]{:S(2)}) async-start(bf16[64,6,7168]{2,1,0:T(8,128)(2,1)} %reshape.53), calls=%async_computation | async-start | bytes 14680064 | tf_op jit(solution)/shard_map/all_to_all | solution.py:59
  196.3 0.0 all-gather.2.cloned.1.call-start
  196.3 0.7 all-gather.2.cloned.1.call-update
  197.0 0.0 reduce-scatter.2.cloned.1.call-start
  197.1 161.3 %all-to-all-done = bf16[64,6,7168]{2,1,0:T(8,128)(2,1)} async-done(((bf16[64,6,7168]{2,1,0:T(8,128)(2,1)}), bf16[64,6,7168]{2,1,0:T(8,128)(2,1)}, u32[]{:S(2)}, u32[]{:S(2)}) %all-to-all-start) | async-done | bytes 5505056 | tf_op jit(solution)/shard_map/all_to_all | solution.py:59
  358.4 8.6 %reshape.54 = bf16[384,7168]{1,0:T(8,128)(2,1)} reshape(bf16[64,6,7168]{2,1,0:T(8,128)(2,1)} %all-to-all-done) | data formatting | bytes 11010048 | tf_op jit(solution)/shard_map/reshape | solution.py:62
  367.0 0.0 collective-permute-start.2
  367.0 0.0 all-gather.2.cloned.1.call-done
  367.0 0.0 copy-start.2
  367.0 9.4 %collective-permute-done.2 = bf16[384,7168]{1,0:T(8,128)(2,1)} collective-permute-done((bf16[384,7168]{1,0:T(8,128)(2,1)}, bf16[384,7168]{1,0:T(8,128)(2,1)}, u32[]{:S(2)}, u32[]{:S(2)}) %collective-permute-start.2) | collective-permute-done | bytes 5505056 | tf_op jit(solution)/shard_map/ppermute | solution.py:18
  376.4 4.5 fusion.6
  380.8 0.0 copy-done.2
  380.9 0.0 copy-start
  380.9 1.6 convolution_convert_fusion.1
  382.5 0.4 collective-permute-start.3
  382.9 0.5 copy-done
  383.4 1.6 fusion.7
  385.0 0.0 copy-start.3
  385.0 2.2 fusion.11
  387.2 0.0 copy-done.3
  387.2 5.8 %add_convert_fusion = bf16[512,3584]{1,0:T(8,128)(2,1)} fusion(f32[512,3584]{1,0:T(8,128)S(1)} %fusion.11, bf16[384,7168]{1,0:T(8,128)(2,1)} %collective-permute-done.2, f32[384,512]{1,0:T(8,128)S(1)} %fusion.6), kind=kOutput, calls=%fused_computation.2 | convolution fusion | flops 1413939200 | bytes 14548992 | tf_op jit(solution)/shard_map/dot_general | solution.py:78
  393.1 0.0 reduce-scatter.2.cloned.1.call-update
  393.1 0.0 collective-permute-done.3
  393.1 4.8 add_convert_fusion.1
  397.9 2.7 reshape.55
  400.5 0.0 copy-start.4
  400.5 7.0 %all-to-all-start.1 = ((bf16[64,6,3584]{2,1,0:T(8,128)(2,1)}), bf16[64,6,3584]{2,1,0:T(8,128)(2,1)}, u32[]{:S(2)}, u32[]{:S(2)}) async-start(bf16[64,6,3584]{2,1,0:T(8,128)(2,1)} %reshape.55), calls=%async_computation.1 | async-start | bytes 7340032 | tf_op jit(solution)/shard_map/all_to_all | solution.py:96
  407.5 0.0 copy-done.4
  407.5 10.4 %fusion.17 = f32[512,3584]{1,0:T(8,128)} fusion(bf16[384,7168]{1,0:T(8,128)(2,1)} %reshape.54, bf16[2,512,3584]{2,1,0:T(8,128)(2,1)} %all-gather.2.cloned.1.call-done, f32[384,512]{1,0:T(8,128)S(1)} %copy-done.4), kind=kOutput, calls=%fused_computation.30 | convolution fusion | flops 2820341760 | bytes 17301504 | tf_op jit(solution)/shard_map/dot_general | solution.py:77
  417.9 12.7 %convolution_add_fusion = f32[512,3584]{1,0:T(8,128)} fusion(f32[512,3584]{1,0:T(8,128)} %fusion.17, bf16[384,7168]{1,0:T(8,128)(2,1)} %collective-permute-done.2, bf16[2,512,3584]{2,1,0:T(8,128)(2,1)} %all-gather.2.cloned.1.call-done, f32[384,512]{1,0:T(8,128)S(1)} %fusion.6), kind=kOutput, calls=%fused_computation.3 | convolution fusion | flops 2822176768 | bytes 24641536 | tf_op jit(solution)/shard_map/dot_general | solution.py:77
  430.6 3.5 select_convert_fusion
  434.1 0.6 collective-permute-start.4
  434.6 84.9 %collective-permute-done.4 = bf16[256,3584]{1,0:T(8,128)(2,1)S(1)} collective-permute-done((bf16[256,3584]{1,0:T(8,128)(2,1)S(1)}, bf16[256,3584]{1,0:T(8,128)(2,1)S(1)}, u32[]{:S(2)}, u32[]{:S(2)}) %collective-permute-start.4) | collective-permute-done | bytes 1835040 | tf_op jit(solution)/shard_map/ppermute | solution.py:93
  519.6 4.1 fusion.21
  523.6 2.3 copy.14
  525.9 0.0 all-to-all-done.1
  525.9 4.0 reshape.56
  529.9 2.4 fusion.2
  532.3 0.0 reduce-scatter.2.cloned.1.call-done
  (7 shorter events, 0.1 us)
Async XLA Ops:
  7.2 8.9 %copy-start.7 = (s32[64]{0:T(128)S(1)}, s32[64]{0:T(128)}, u32[]{:S(2)}) copy-start(s32[64]{0:T(128)} %param.11) | copy-start | bytes 772
  7.2 8.9 %copy-start.6 = (s32[256,1]{0,1:T(1,128)S(1)}, s32[256,1]{0,1:T(1,128)}, u32[]{:S(2)}) copy-start(s32[256,1]{0,1:T(1,128)} %param.9) | copy-start | bytes 3076
  7.2 11.4 %copy-start.5 = (f32[256,1]{0,1:T(1,128)S(1)}, f32[256,1]{0,1:T(1,128)}, u32[]{:S(2)}) copy-start(f32[256,1]{0,1:T(1,128)} %param.10) | copy-start | bytes 3076
  7.2 118.6 %collective-permute-start.1 = (bf16[256,3584]{1,0:T(8,128)(2,1)}, bf16[256,3584]{1,0:T(8,128)(2,1)}, u32[]{:S(2)}, u32[]{:S(2)}) collective-permute-start(bf16[256,3584]{1,0:T(8,128)(2,1)} %bitcast.64), channel_id=1, source_target_pairs={{0,32},{32,0},{1,33},{33,1},{2,34},{34,2},{3,35},{35,3},{4,36},{36... | collective-permute-start | bytes 5505032 | tf_op jit(solution)/shard_map/ppermute | solution.py:14
  10.6 160.1 %collective-permute-start = (bf16[256,3584]{1,0:T(8,128)(2,1)S(1)}, bf16[256,3584]{1,0:T(8,128)(2,1)}, u32[]{:S(2)}, u32[]{:S(2)}) collective-permute-start(bf16[256,3584]{1,0:T(8,128)(2,1)S(1)} %bitcast.63), channel_id=1, source_target_pairs={{0,32},{32,0},{1,33},{33,1},{2,34},{34,2},{3,35},{35,3},{4,36},{36... | collective-permute-start | bytes 5505032 | tf_op jit(solution)/shard_map/ppermute | solution.py:14
  23.4 102.4 %copy-start.1 = (bf16[1,256,3584]{2,1,0:T(8,128)(2,1)S(1)}, bf16[1,256,3584]{2,1,0:T(8,128)(2,1)}, u32[]{:S(2)}) copy-start(bf16[1,256,3584]{2,1,0:T(8,128)(2,1)} %param.13) | copy-start | bytes 5505028
  181.2 177.2 %all-to-all-start = ((bf16[64,6,7168]{2,1,0:T(8,128)(2,1)}), bf16[64,6,7168]{2,1,0:T(8,128)(2,1)}, u32[]{:S(2)}, u32[]{:S(2)}) async-start(bf16[64,6,7168]{2,1,0:T(8,128)(2,1)} %reshape.53), calls=%async_computation | async-start | bytes 14680064 | tf_op jit(solution)/shard_map/all_to_all | solution.py:59
  196.3 170.7 %all-gather.2.cloned.1.call-start = ((), (), s32[]{:S(2)}) async-start(), calls=%async_computation.3 | async-start | bytes 11010048 | tf_op jit(solution)/shard_map/all_gather | solution.py:56
  197.0 335.3 %reduce-scatter.2.cloned.1.call-start = ((), (), s32[]{:S(2)}) async-start(), calls=%async_computation.4 | async-start | bytes 5505024 | tf_op jit(solution)/shard_map/reduce_scatter | solution.py:87
  367.0 9.4 %collective-permute-start.2 = (bf16[384,7168]{1,0:T(8,128)(2,1)}, bf16[384,7168]{1,0:T(8,128)(2,1)}, u32[]{:S(2)}, u32[]{:S(2)}) collective-permute-start(bf16[384,7168]{1,0:T(8,128)(2,1)} %reshape.54), channel_id=1, source_target_pairs={{0,64},{64,0},{1,65},{65,1},{2,66},{66,2},{3,67},{67,3},{4,68},{68... | collective-permute-start | bytes 16515080 | tf_op jit(solution)/shard_map/ppermute | solution.py:18
  367.0 13.9 %copy-start.2 = (bf16[2,512,3584]{2,1,0:T(8,128)(2,1)S(1)}, bf16[2,512,3584]{2,1,0:T(8,128)(2,1)}, u32[]{:S(2)}) copy-start(bf16[2,512,3584]{2,1,0:T(8,128)(2,1)} %all-gather.2.cloned.1.call-done) | copy-start | bytes 22020100
  380.9 2.6 copy-start
  382.5 10.6 %collective-permute-start.3 = (bf16[384,3584]{1,0:T(8,128)(2,1)S(1)}, bf16[384,3584]{1,0:T(8,128)(2,1)}, u32[]{:S(2)}, u32[]{:S(2)}) collective-permute-start(bf16[384,3584]{1,0:T(8,128)(2,1)S(1)} %convolution_convert_fusion.1), channel_id=1, source_target_pairs={{0,64},{64,0},{1,65},{65,1},{2,66},{66,2},{3,67},{67,3},{4,68},{68... | collective-permute-start | bytes 8257544 | tf_op jit(solution)/shard_map/ppermute | solution.py:18
  385.0 2.2 copy-start.3
  400.5 7.0 %copy-start.4 = (f32[384,512]{1,0:T(8,128)S(1)}, f32[384,512]{1,0:T(8,128)}, u32[]{:S(2)}) copy-start(f32[384,512]{1,0:T(8,128)} %copy-done.3) | copy-start | bytes 2359300
  400.5 125.4 %all-to-all-start.1 = ((bf16[64,6,3584]{2,1,0:T(8,128)(2,1)}), bf16[64,6,3584]{2,1,0:T(8,128)(2,1)}, u32[]{:S(2)}, u32[]{:S(2)}) async-start(bf16[64,6,3584]{2,1,0:T(8,128)(2,1)} %reshape.55), calls=%async_computation.1 | async-start | bytes 7340032 | tf_op jit(solution)/shard_map/all_to_all | solution.py:96
  434.1 85.5 %collective-permute-start.4 = (bf16[256,3584]{1,0:T(8,128)(2,1)S(1)}, bf16[256,3584]{1,0:T(8,128)(2,1)S(1)}, u32[]{:S(2)}, u32[]{:S(2)}) collective-permute-start(bf16[256,3584]{1,0:T(8,128)(2,1)S(1)} %select_convert_fusion), channel_id=1, source_target_pairs={{0,128},{128,0},{1,129},{129,1},{2,130},{130,2},{3,131},{131,3},{4... | collective-permute-start | bytes 5505032 | tf_op jit(solution)/shard_map/ppermute | solution.py:93
Sparse Core Ops, SparseCore 0:
  198.9 156.9 all-gather.1
  393.2 111.2 reduce-scatter.1

commit v12 on v11

--- a/solution.py
+++ b/solution.py
@@ -78,9 +78,10 @@
         term_out = lax.dot_general(hidden, grads, contract_first, preferred_element_type=jnp.float32)
         return out, term_in, term_out
 
+    out_own, in_own, outg_own = expert_pass(recv)
+    other, out_own = lax.optimization_barrier((other, out_own))
     out_other, in_other, outg_other = expert_pass(other)
     back = swap_core(out_other.astype(jnp.bfloat16))
-    out_own, in_own, outg_own = expert_pass(recv)
     expert_out = (out_own + back.astype(jnp.float32)).astype(jnp.bfloat16)
 
     term_out = (outg_own + outg_other).astype(jnp.bfloat16)

time: 543 us -> 543 us (level)
  waiting for transfers between devices: 397 us -> 389 us
    ppermute x2, waiting for transfers between devices: 9.37 us -> 0.41 us  [swap_core(): return lax.ppermute(block, 'dc', [(0, 1), (1, 0)])]
  transfers between devices with their start and end apart: 9 -> 9, of which waited for: 5 -> 5; matrix products, arithmetic and copies ran while one was open for 15% -> 16% of each run, Pallas kernels for 0% -> 0%
where the time goes in v12:
time: 543 us; the launch traced here: 539 us
  waiting for transfers between devices  389 us (72%)
  matrix products  56.5 us (10%)
  local copies, waits for them, and re-layouts  31.5 us (6%)
  starting transfers between devices  29.1 us (5%)
  other arithmetic  18.2 us (3%)
  between operations  14.9 us (3%)
    all_to_all x1, waiting for transfers between devices, body(): lax.all_to_all(send.reshape(expert_count, capacity, 2 * width), 'expert',...  161 us
    ppermute x2, waiting for transfers between devices, partner_2(): return lax.ppermute(block, axis, route)  141 us
    ppermute x1, waiting for transfers between devices, body(): got = lax.ppermute(sent, 'dx', [(0, 1), (1, 0)])  85.5 us
    dot_general x2, matrix products, expert_pass(): lax.dot_general(dpre, rows, contract_first, preferred_element_type=jnp.fl...  23 us
    all_to_all x1, starting transfers between devices, body(): lax.all_to_all(send.reshape(expert_count, capacity, 2 * width), 'expert',...  15.1 us
  transfers between devices with their start and end apart: 9, of which 5 were waited for; matrix products, arithmetic and copies ran while one was open for 16% of the time, Pallas kernels for 0%

profile of v12, /device:TPU:192, one launch (start us, length us, event | category | flops | bytes accessed | tf_op | source)
XLA Modules:
  0.0 538.9 jit_solution(1710655088337456339)
XLA Ops:
  7.2 0.0 copy-start.6
  7.2 0.0 copy-start.5
  7.2 0.0 copy-start.4
  7.2 0.6 collective-permute-start.1
  7.8 2.8 copy.13
  10.6 5.5 %collective-permute-start = (bf16[256,3584]{1,0:T(8,128)(2,1)S(1)}, bf16[256,3584]{1,0:T(8,128)(2,1)}, u32[]{:S(2)}, u32[]{:S(2)}) collective-permute-start(bf16[256,3584]{1,0:T(8,128)(2,1)S(1)} %bitcast.61), channel_id=1, source_target_pairs={{0,32},{32,0},{1,33},{33,1},{2,34},{34,2},{3,35},{35,3},{4,36},{36... | collective-permute-start | bytes 5505032 | tf_op jit(solution)/shard_map/ppermute | solution.py:14
  16.1 0.0 copy-done.6
  16.1 0.0 copy-done.5
  16.1 1.9 gather_fusion
  18.0 0.6 reduce-window.6
  18.6 0.0 copy-done.4
  18.6 3.2 multiply_convert_fusion
  21.8 0.2 slice_reduce_fusion
  22.0 0.6 dynamic_slice.3
  23.3 0.1 fusion.55
  23.4 0.0 copy-start
  23.4 6.2 %convolution_convert_fusion = bf16[384,7168]{1,0:T(8,128)(2,1)} fusion(bf16[256,3584]{1,0:T(8,128)(2,1)} %multiply_convert_fusion, bf16[256,3584]{1,0:T(8,128)(2,1)} %param.7, s32[256]{0:T(256)S(1)} %add_add_fusion), kind=kOutput, calls=%fused_computation.1 | convolution fusion | flops 1419476992 | bytes 9176064 | tf_op jit(solution)/shard_map/dot_general | solution.py:54
  29.6 96.2 %collective-permute-done.1 = bf16[256,3584]{1,0:T(8,128)(2,1)} collective-permute-done((bf16[256,3584]{1,0:T(8,128)(2,1)}, bf16[256,3584]{1,0:T(8,128)(2,1)}, u32[]{:S(2)}, u32[]{:S(2)}) %collective-permute-start.1) | collective-permute-done | bytes 1835040 | tf_op jit(solution)/shard_map/ppermute | solution.py:14
  125.8 0.0 copy-done
  125.8 0.2 select_bitcast_fusion
  126.0 44.6 %collective-permute-done = bf16[256,3584]{1,0:T(8,128)(2,1)} collective-permute-done((bf16[256,3584]{1,0:T(8,128)(2,1)S(1)}, bf16[256,3584]{1,0:T(8,128)(2,1)}, u32[]{:S(2)}, u32[]{:S(2)}) %collective-permute-start) | collective-permute-done | bytes 1835040 | tf_op jit(solution)/shard_map/ppermute | solution.py:14
  170.6 0.2 select_bitcast_fusion.1
  170.8 2.1 pad_maximum_fusion
  173.0 8.3 %reshape.53 = bf16[64,6,7168]{2,1,0:T(8,128)(2,1)} reshape(bf16[384,7168]{1,0:T(8,128)(2,1)} %convolution_convert_fusion) | data formatting | bytes 11010048 | tf_op jit(solution)/shard_map/reshape | solution.py:60
  181.3 15.1 %all-to-all-start = ((bf16[64,6,7168]{2,1,0:T(8,128)(2,1)}), bf16[64,6,7168]{2,1,0:T(8,128)(2,1)}, u32[]{:S(2)}, u32[]{:S(2)}) async-start(bf16[64,6,7168]{2,1,0:T(8,128)(2,1)} %reshape.53), calls=%async_computation | async-start | bytes 14680064 | tf_op jit(solution)/shard_map/all_to_all | solution.py:59
  196.3 0.0 all-gather.2.cloned.1.call-start
  196.4 0.7 all-gather.2.cloned.1.call-update
  197.1 0.0 reduce-scatter.2.cloned.1.call-start
  197.1 161.3 %all-to-all-done = bf16[64,6,7168]{2,1,0:T(8,128)(2,1)} async-done(((bf16[64,6,7168]{2,1,0:T(8,128)(2,1)}), bf16[64,6,7168]{2,1,0:T(8,128)(2,1)}, u32[]{:S(2)}, u32[]{:S(2)}) %all-to-all-start) | async-done | bytes 5505056 | tf_op jit(solution)/shard_map/all_to_all | solution.py:59
  358.4 8.6 %reshape.54 = bf16[384,7168]{1,0:T(8,128)(2,1)} reshape(bf16[64,6,7168]{2,1,0:T(8,128)(2,1)} %all-to-all-done) | data formatting | bytes 11010048 | tf_op jit(solution)/shard_map/reshape | solution.py:62
  367.0 0.0 collective-permute-start.2
  367.0 0.0 all-gather.2.cloned.1.call-done
  367.0 0.0 copy-start.1
  367.0 4.6 fusion.7
  371.7 0.3 copy-done.1
  372.0 0.0 copy-start.2
  372.0 4.0 fusion.20
  376.0 0.4 collective-permute-done.2
  376.4 3.4 fusion.6
  379.8 3.2 convolution_convert_fusion.1
  383.0 0.1 collective-permute-start.3
  383.1 0.0 copy-done.2
  383.1 3.9 fusion.8
  387.0 5.8 %add_convert_fusion = bf16[512,3584]{1,0:T(8,128)(2,1)} fusion(f32[512,3584]{1,0:T(8,128)S(1)} %fusion.8, bf16[384,7168]{1,0:T(8,128)(2,1)} %collective-permute-done.2, f32[384,512]{1,0:T(8,128)S(1)} %fusion.6), kind=kOutput, calls=%fused_computation.2 | convolution fusion | flops 1413939200 | bytes 14548992 | tf_op jit(solution)/shard_map/dot_general | solution.py:78
  392.8 0.0 reduce-scatter.2.cloned.1.call-update
  392.9 0.0 collective-permute-done.3
  392.9 4.2 add_convert_fusion.1
  397.0 2.7 reshape.55
  399.7 0.0 copy-start.3
  399.7 6.9 %all-to-all-start.1 = ((bf16[64,6,3584]{2,1,0:T(8,128)(2,1)}), bf16[64,6,3584]{2,1,0:T(8,128)(2,1)}, u32[]{:S(2)}, u32[]{:S(2)}) async-start(bf16[64,6,3584]{2,1,0:T(8,128)(2,1)} %reshape.55), calls=%async_computation.1 | async-start | bytes 7340032 | tf_op jit(solution)/shard_map/all_to_all | solution.py:97
  406.6 0.0 copy-done.3
  406.7 10.4 %fusion.12 = f32[512,3584]{1,0:T(8,128)} fusion(bf16[384,7168]{1,0:T(8,128)(2,1)} %reshape.54, bf16[2,512,3584]{2,1,0:T(8,128)(2,1)} %all-gather.2.cloned.1.call-done, f32[384,512]{1,0:T(8,128)S(1)} %copy-done.3), kind=kOutput, calls=%fused_computation.25 | convolution fusion | flops 2820341760 | bytes 17301504 | tf_op jit(solution)/shard_map/dot_general | solution.py:77
  417.1 12.6 %convolution_add_fusion = f32[512,3584]{1,0:T(8,128)} fusion(f32[512,3584]{1,0:T(8,128)} %fusion.12, bf16[384,7168]{1,0:T(8,128)(2,1)} %collective-permute-done.2, bf16[2,512,3584]{2,1,0:T(8,128)(2,1)} %all-gather.2.cloned.1.call-done, f32[384,512]{1,0:T(8,128)S(1)} %fusion.6), kind=kOutput, calls=%fused_computation.3 | convolution fusion | flops 2822176768 | bytes 24641536 | tf_op jit(solution)/shard_map/dot_general | solution.py:77
  429.6 3.5 select_convert_fusion
  433.1 0.8 collective-permute-start.4
  433.9 85.5 %collective-permute-done.4 = bf16[256,3584]{1,0:T(8,128)(2,1)S(1)} collective-permute-done((bf16[256,3584]{1,0:T(8,128)(2,1)S(1)}, bf16[256,3584]{1,0:T(8,128)(2,1)S(1)}, u32[]{:S(2)}, u32[]{:S(2)}) %collective-permute-start.4) | collective-permute-done | bytes 1835040 | tf_op jit(solution)/shard_map/ppermute | solution.py:94
  519.4 4.1 fusion.21
  523.4 2.3 copy.14
  525.7 0.0 all-to-all-done.1
  525.7 4.0 reshape.56
  529.7 2.4 fusion.2
  532.1 0.0 reduce-scatter.2.cloned.1.call-done
  (7 shorter events, 0.1 us)
Async XLA Ops:
  7.2 8.9 %copy-start.6 = (s32[64]{0:T(128)S(1)}, s32[64]{0:T(128)}, u32[]{:S(2)}) copy-start(s32[64]{0:T(128)} %param.11) | copy-start | bytes 772
  7.2 8.9 %copy-start.5 = (s32[256,1]{0,1:T(1,128)S(1)}, s32[256,1]{0,1:T(1,128)}, u32[]{:S(2)}) copy-start(s32[256,1]{0,1:T(1,128)} %param.9) | copy-start | bytes 3076
  7.2 11.4 %copy-start.4 = (f32[256,1]{0,1:T(1,128)S(1)}, f32[256,1]{0,1:T(1,128)}, u32[]{:S(2)}) copy-start(f32[256,1]{0,1:T(1,128)} %param.10) | copy-start | bytes 3076
  7.2 118.6 %collective-permute-start.1 = (bf16[256,3584]{1,0:T(8,128)(2,1)}, bf16[256,3584]{1,0:T(8,128)(2,1)}, u32[]{:S(2)}, u32[]{:S(2)}) collective-permute-start(bf16[256,3584]{1,0:T(8,128)(2,1)} %bitcast.62), channel_id=1, source_target_pairs={{0,32},{32,0},{1,33},{33,1},{2,34},{34,2},{3,35},{35,3},{4,36},{36... | collective-permute-start | bytes 5505032 | tf_op jit(solution)/shard_map/ppermute | solution.py:14
  10.6 160.1 %collective-permute-start = (bf16[256,3584]{1,0:T(8,128)(2,1)S(1)}, bf16[256,3584]{1,0:T(8,128)(2,1)}, u32[]{:S(2)}, u32[]{:S(2)}) collective-permute-start(bf16[256,3584]{1,0:T(8,128)(2,1)S(1)} %bitcast.61), channel_id=1, source_target_pairs={{0,32},{32,0},{1,33},{33,1},{2,34},{34,2},{3,35},{35,3},{4,36},{36... | collective-permute-start | bytes 5505032 | tf_op jit(solution)/shard_map/ppermute | solution.py:14
  23.4 102.4 %copy-start = (bf16[1,256,3584]{2,1,0:T(8,128)(2,1)S(1)}, bf16[1,256,3584]{2,1,0:T(8,128)(2,1)}, u32[]{:S(2)}) copy-start(bf16[1,256,3584]{2,1,0:T(8,128)(2,1)} %param.13) | copy-start | bytes 5505028
  181.3 177.2 %all-to-all-start = ((bf16[64,6,7168]{2,1,0:T(8,128)(2,1)}), bf16[64,6,7168]{2,1,0:T(8,128)(2,1)}, u32[]{:S(2)}, u32[]{:S(2)}) async-start(bf16[64,6,7168]{2,1,0:T(8,128)(2,1)} %reshape.53), calls=%async_computation | async-start | bytes 14680064 | tf_op jit(solution)/shard_map/all_to_all | solution.py:59
  196.3 170.7 %all-gather.2.cloned.1.call-start = ((), (), s32[]{:S(2)}) async-start(), calls=%async_computation.3 | async-start | bytes 11010048 | tf_op jit(solution)/shard_map/all_gather | solution.py:56
  197.1 335.0 %reduce-scatter.2.cloned.1.call-start = ((), (), s32[]{:S(2)}) async-start(), calls=%async_computation.4 | async-start | bytes 5505024 | tf_op jit(solution)/shard_map/reduce_scatter | solution.py:88
  367.0 9.4 %collective-permute-start.2 = (bf16[384,7168]{1,0:T(8,128)(2,1)}, bf16[384,7168]{1,0:T(8,128)(2,1)}, u32[]{:S(2)}, u32[]{:S(2)}) collective-permute-start(bf16[384,7168]{1,0:T(8,128)(2,1)} %reshape.54), channel_id=1, source_target_pairs={{0,64},{64,0},{1,65},{65,1},{2,66},{66,2},{3,67},{67,3},{4,68},{68... | collective-permute-start | bytes 16515080 | tf_op jit(solution)/shard_map/ppermute | solution.py:18
  367.0 5.0 copy-start.1
  372.0 11.1 %copy-start.2 = (f32[384,512]{1,0:T(8,128)}, f32[384,512]{1,0:T(8,128)S(1)}, u32[]{:S(2)}) copy-start(f32[384,512]{1,0:T(8,128)S(1)} %fusion.7) | copy-start | bytes 2359300
  383.0 9.9 %collective-permute-start.3 = (bf16[384,3584]{1,0:T(8,128)(2,1)}, bf16[384,3584]{1,0:T(8,128)(2,1)}, u32[]{:S(2)}, u32[]{:S(2)}) collective-permute-start(bf16[384,3584]{1,0:T(8,128)(2,1)} %convolution_convert_fusion.1), channel_id=1, source_target_pairs={{0,64},{64,0},{1,65},{65,1},{2,66},{66,2},{3,67},{67,3},{4,68},{68... | collective-permute-start | bytes 8257544 | tf_op jit(solution)/shard_map/ppermute | solution.py:18
  399.7 6.9 %copy-start.3 = (f32[384,512]{1,0:T(8,128)S(1)}, f32[384,512]{1,0:T(8,128)}, u32[]{:S(2)}) copy-start(f32[384,512]{1,0:T(8,128)} %copy-done.2) | copy-start | bytes 2359300
  399.7 126.0 %all-to-all-start.1 = ((bf16[64,6,3584]{2,1,0:T(8,128)(2,1)}), bf16[64,6,3584]{2,1,0:T(8,128)(2,1)}, u32[]{:S(2)}, u32[]{:S(2)}) async-start(bf16[64,6,3584]{2,1,0:T(8,128)(2,1)} %reshape.55), calls=%async_computation.1 | async-start | bytes 7340032 | tf_op jit(solution)/shard_map/all_to_all | solution.py:97
  433.1 86.3 %collective-permute-start.4 = (bf16[256,3584]{1,0:T(8,128)(2,1)S(1)}, bf16[256,3584]{1,0:T(8,128)(2,1)S(1)}, u32[]{:S(2)}, u32[]{:S(2)}) collective-permute-start(bf16[256,3584]{1,0:T(8,128)(2,1)S(1)} %select_convert_fusion), channel_id=1, source_target_pairs={{0,128},{128,0},{1,129},{129,1},{2,130},{130,2},{3,131},{131,3},{4... | collective-permute-start | bytes 5505032 | tf_op jit(solution)/shard_map/ppermute | solution.py:94
Sparse Core Ops, SparseCore 0:
  198.9 156.9 all-gather.1
  393.0 111.9 reduce-scatter.1

commit v13 on v12

--- a/solution.py
+++ b/solution.py
@@ -97,9 +97,10 @@
     returned = lax.all_to_all(
         expert_out.reshape(expert_count, capacity, width), "expert",
         split_axis=0, concat_axis=0, tiled=True,
-    ).reshape(slots, width)
+    )
     route_out = lax.dot_general(
-        select, returned, contract_first, preferred_element_type=jnp.float32
+        select.reshape(expert_count, capacity, route_count), returned,
+        (((0, 1), (0, 1)), ((), ())), preferred_element_type=jnp.float32,
     )
     weighted = gates.reshape(local_tokens, top_count, 1) * route_out.astype(
         jnp.bfloat16

time: 543 us -> 541 us (level)
  no operation moved by 1% of the time
where the time goes in v13:
time: 541 us; the launch traced here: 537 us
  waiting for transfers between devices  389 us (72%)
  matrix products  58.8 us (11%)
  local copies, waits for them, and re-layouts  27.6 us (5%)
  starting transfers between devices  26.5 us (5%)
  other arithmetic  21.2 us (4%)
  between operations  14.9 us (3%)
    all_to_all x1, waiting for transfers between devices, body(): lax.all_to_all(send.reshape(expert_count, capacity, 2 * width), 'expert',...  163 us
    ppermute x2, waiting for transfers between devices, partner_2(): return lax.ppermute(block, axis, route)  139 us
    ppermute x1, waiting for transfers between devices, body(): got = lax.ppermute(sent, 'dx', [(0, 1), (1, 0)])  85.5 us
    dot_general x2, matrix products, expert_pass(): lax.dot_general(dpre, rows, contract_first, preferred_element_type=jnp.fl...  23 us
    all_to_all x1, starting transfers between devices, body(): lax.all_to_all(send.reshape(expert_count, capacity, 2 * width), 'expert',...  12.3 us
  transfers between devices with their start and end apart: 9, of which 5 were waited for; matrix products, arithmetic and copies ran while one was open for 16% of the time, Pallas kernels for 0%

profile of v13, /device:TPU:192, one launch (start us, length us, event | category | flops | bytes accessed | tf_op | source)
XLA Modules:
  0.0 537.5 jit_solution(11489156743793209640)
XLA Ops:
  7.2 0.0 copy-start.6
  7.2 0.0 copy-start.4
  7.2 0.0 copy-start.5
  7.2 0.6 collective-permute-start.1
  7.8 2.8 copy.18
  10.6 5.5 %collective-permute-start = (bf16[256,3584]{1,0:T(8,128)(2,1)S(1)}, bf16[256,3584]{1,0:T(8,128)(2,1)}, u32[]{:S(2)}, u32[]{:S(2)}) collective-permute-start(bf16[256,3584]{1,0:T(8,128)(2,1)S(1)} %bitcast.70), channel_id=1, source_target_pairs={{0,32},{32,0},{1,33},{33,1},{2,34},{34,2},{3,35},{35,3},{4,36},{36... | collective-permute-start | bytes 5505032 | tf_op jit(solution)/shard_map/ppermute | solution.py:14
  16.1 0.0 copy-done.6
  16.1 0.0 copy-done.4
  16.1 1.9 gather_fusion
  18.0 0.6 reduce-window.6
  18.6 0.0 copy-done.5
  18.6 3.2 multiply_convert_fusion
  21.8 0.2 slice_reduce_fusion
  22.0 0.6 dynamic_slice.3
  23.3 0.1 fusion.59
  23.4 0.0 copy-start
  23.4 6.2 %convolution_convert_fusion = bf16[384,7168]{1,0:T(8,128)(2,1)} fusion(bf16[256,3584]{1,0:T(8,128)(2,1)} %multiply_convert_fusion, bf16[256,3584]{1,0:T(8,128)(2,1)} %param.7, s32[256]{0:T(256)S(1)} %add_add_fusion), kind=kOutput, calls=%fused_computation.1 | convolution fusion | flops 1419476992 | bytes 9176064 | tf_op jit(solution)/shard_map/dot_general | solution.py:54
  29.6 96.2 %collective-permute-done.1 = bf16[256,3584]{1,0:T(8,128)(2,1)} collective-permute-done((bf16[256,3584]{1,0:T(8,128)(2,1)}, bf16[256,3584]{1,0:T(8,128)(2,1)}, u32[]{:S(2)}, u32[]{:S(2)}) %collective-permute-start.1) | collective-permute-done | bytes 1835040 | tf_op jit(solution)/shard_map/ppermute | solution.py:14
  125.8 0.0 copy-done
  125.8 1.7 select_bitcast_fusion
  127.5 43.1 %collective-permute-done = bf16[256,3584]{1,0:T(8,128)(2,1)} collective-permute-done((bf16[256,3584]{1,0:T(8,128)(2,1)S(1)}, bf16[256,3584]{1,0:T(8,128)(2,1)}, u32[]{:S(2)}, u32[]{:S(2)}) %collective-permute-start) | collective-permute-done | bytes 1835040 | tf_op jit(solution)/shard_map/ppermute | solution.py:14
  170.6 1.7 select_bitcast_fusion.1
  172.3 2.1 pad_maximum_fusion
  174.5 8.3 %reshape.65 = bf16[64,6,7168]{2,1,0:T(8,128)(2,1)} reshape(bf16[384,7168]{1,0:T(8,128)(2,1)} %convolution_convert_fusion) | data formatting | bytes 11010048 | tf_op jit(solution)/shard_map/reshape | solution.py:60
  182.8 12.3 %all-to-all-start = ((bf16[64,6,7168]{2,1,0:T(8,128)(2,1)}), bf16[64,6,7168]{2,1,0:T(8,128)(2,1)}, u32[]{:S(2)}, u32[]{:S(2)}) async-start(bf16[64,6,7168]{2,1,0:T(8,128)(2,1)} %reshape.65), calls=%async_computation | async-start | bytes 14680064 | tf_op jit(solution)/shard_map/all_to_all | solution.py:59
  195.1 0.0 all-gather.2.cloned.1.call-start
  195.1 0.7 all-gather.2.cloned.1.call-update
  195.8 0.0 reduce-scatter.2.cloned.1.call-start
  195.9 162.6 %all-to-all-done = bf16[64,6,7168]{2,1,0:T(8,128)(2,1)} async-done(((bf16[64,6,7168]{2,1,0:T(8,128)(2,1)}), bf16[64,6,7168]{2,1,0:T(8,128)(2,1)}, u32[]{:S(2)}, u32[]{:S(2)}) %all-to-all-start) | async-done | bytes 5505056 | tf_op jit(solution)/shard_map/all_to_all | solution.py:59
  358.5 8.6 %reshape.66 = bf16[384,7168]{1,0:T(8,128)(2,1)} reshape(bf16[64,6,7168]{2,1,0:T(8,128)(2,1)} %all-to-all-done) | data formatting | bytes 11010048 | tf_op jit(solution)/shard_map/reshape | solution.py:62
  367.1 0.0 collective-permute-start.2
  367.1 0.0 all-gather.2.cloned.1.call-done
  367.1 0.0 copy-start.1
  367.1 4.6 fusion.8
  371.8 0.3 copy-done.1
  372.1 0.0 copy-start.2
  372.1 4.0 fusion.22
  376.1 0.4 collective-permute-done.2
  376.5 3.4 fusion.7
  379.9 3.2 convolution_convert_fusion.1
  383.0 0.1 collective-permute-start.3
  383.2 0.0 copy-done.2
  383.2 3.9 fusion.10
  387.1 5.8 %add_convert_fusion = bf16[512,3584]{1,0:T(8,128)(2,1)} fusion(f32[512,3584]{1,0:T(8,128)S(1)} %fusion.10, bf16[384,7168]{1,0:T(8,128)(2,1)} %collective-permute-done.2, f32[384,512]{1,0:T(8,128)S(1)} %fusion.7), kind=kOutput, calls=%fused_computation.2 | convolution fusion | flops 1413939200 | bytes 14548992 | tf_op jit(solution)/shard_map/dot_general | solution.py:78
  392.9 0.0 reduce-scatter.2.cloned.1.call-update
  392.9 0.0 collective-permute-done.3
  393.0 4.2 add_convert_fusion.1
  397.1 2.7 reshape.67
  399.8 0.0 copy-start.3
  399.8 7.1 %all-to-all-start.1 = ((bf16[64,6,3584]{2,1,0:T(8,128)(2,1)}), bf16[64,6,3584]{2,1,0:T(8,128)(2,1)}, u32[]{:S(2)}, u32[]{:S(2)}) async-start(bf16[64,6,3584]{2,1,0:T(8,128)(2,1)} %reshape.67), calls=%async_computation.1 | async-start | bytes 7340032 | tf_op jit(solution)/shard_map/all_to_all | solution.py:97
  406.9 0.0 copy-done.3
  406.9 10.4 %fusion.14 = f32[512,3584]{1,0:T(8,128)} fusion(bf16[384,7168]{1,0:T(8,128)(2,1)} %reshape.66, bf16[2,512,3584]{2,1,0:T(8,128)(2,1)} %all-gather.2.cloned.1.call-done, f32[384,512]{1,0:T(8,128)S(1)} %copy-done.3), kind=kOutput, calls=%fused_computation.27 | convolution fusion | flops 2820341760 | bytes 17301504 | tf_op jit(solution)/shard_map/dot_general | solution.py:77
  417.3 12.6 %convolution_add_fusion = f32[512,3584]{1,0:T(8,128)} fusion(f32[512,3584]{1,0:T(8,128)} %fusion.14, bf16[384,7168]{1,0:T(8,128)(2,1)} %collective-permute-done.2, bf16[2,512,3584]{2,1,0:T(8,128)(2,1)} %all-gather.2.cloned.1.call-done, f32[384,512]{1,0:T(8,128)S(1)} %fusion.7), kind=kOutput, calls=%fused_computation.3 | convolution fusion | flops 2822176768 | bytes 24641536 | tf_op jit(solution)/shard_map/dot_general | solution.py:77
  429.9 3.5 select_convert_fusion
  433.3 0.8 collective-permute-start.4
  434.1 85.5 %collective-permute-done.4 = bf16[256,3584]{1,0:T(8,128)(2,1)S(1)} collective-permute-done((bf16[256,3584]{1,0:T(8,128)(2,1)S(1)}, bf16[256,3584]{1,0:T(8,128)(2,1)S(1)}, u32[]{:S(2)}, u32[]{:S(2)}) %collective-permute-start.4) | collective-permute-done | bytes 1835040 | tf_op jit(solution)/shard_map/ppermute | solution.py:94
  519.6 4.1 fusion.23
  523.6 2.3 copy.20
  525.9 0.0 all-to-all-done.1
  525.9 4.7 fusion.3
  530.6 0.0 reduce-scatter.2.cloned.1.call-done
  (8 shorter events, 0.1 us)
Async XLA Ops:
  7.2 8.9 %copy-start.6 = (s32[64]{0:T(128)S(1)}, s32[64]{0:T(128)}, u32[]{:S(2)}) copy-start(s32[64]{0:T(128)} %param.11) | copy-start | bytes 772
  7.2 8.9 %copy-start.4 = (s32[256,1]{0,1:T(1,128)S(1)}, s32[256,1]{0,1:T(1,128)}, u32[]{:S(2)}) copy-start(s32[256,1]{0,1:T(1,128)} %param.9) | copy-start | bytes 3076
  7.2 11.4 %copy-start.5 = (f32[256,1]{0,1:T(1,128)S(1)}, f32[256,1]{0,1:T(1,128)}, u32[]{:S(2)}) copy-start(f32[256,1]{0,1:T(1,128)} %param.10) | copy-start | bytes 3076
  7.2 118.6 %collective-permute-start.1 = (bf16[256,3584]{1,0:T(8,128)(2,1)}, bf16[256,3584]{1,0:T(8,128)(2,1)}, u32[]{:S(2)}, u32[]{:S(2)}) collective-permute-start(bf16[256,3584]{1,0:T(8,128)(2,1)} %bitcast.71), channel_id=1, source_target_pairs={{0,32},{32,0},{1,33},{33,1},{2,34},{34,2},{3,35},{35,3},{4,36},{36... | collective-permute-start | bytes 5505032 | tf_op jit(solution)/shard_map/ppermute | solution.py:14
  10.6 160.1 %collective-permute-start = (bf16[256,3584]{1,0:T(8,128)(2,1)S(1)}, bf16[256,3584]{1,0:T(8,128)(2,1)}, u32[]{:S(2)}, u32[]{:S(2)}) collective-permute-start(bf16[256,3584]{1,0:T(8,128)(2,1)S(1)} %bitcast.70), channel_id=1, source_target_pairs={{0,32},{32,0},{1,33},{33,1},{2,34},{34,2},{3,35},{35,3},{4,36},{36... | collective-permute-start | bytes 5505032 | tf_op jit(solution)/shard_map/ppermute | solution.py:14
  23.4 102.4 %copy-start = (bf16[1,256,3584]{2,1,0:T(8,128)(2,1)S(1)}, bf16[1,256,3584]{2,1,0:T(8,128)(2,1)}, u32[]{:S(2)}) copy-start(bf16[1,256,3584]{2,1,0:T(8,128)(2,1)} %param.13) | copy-start | bytes 5505028
  182.8 175.8 %all-to-all-start = ((bf16[64,6,7168]{2,1,0:T(8,128)(2,1)}), bf16[64,6,7168]{2,1,0:T(8,128)(2,1)}, u32[]{:S(2)}, u32[]{:S(2)}) async-start(bf16[64,6,7168]{2,1,0:T(8,128)(2,1)} %reshape.65), calls=%async_computation | async-start | bytes 14680064 | tf_op jit(solution)/shard_map/all_to_all | solution.py:59
  195.1 172.0 %all-gather.2.cloned.1.call-start = ((), (), s32[]{:S(2)}) async-start(), calls=%async_computation.3 | async-start | bytes 11010048 | tf_op jit(solution)/shard_map/all_gather | solution.py:56
  195.8 334.8 %reduce-scatter.2.cloned.1.call-start = ((), (), s32[]{:S(2)}) async-start(), calls=%async_computation.4 | async-start | bytes 5505024 | tf_op jit(solution)/shard_map/reduce_scatter | solution.py:88
  367.1 9.4 %collective-permute-start.2 = (bf16[384,7168]{1,0:T(8,128)(2,1)}, bf16[384,7168]{1,0:T(8,128)(2,1)}, u32[]{:S(2)}, u32[]{:S(2)}) collective-permute-start(bf16[384,7168]{1,0:T(8,128)(2,1)} %reshape.66), channel_id=1, source_target_pairs={{0,64},{64,0},{1,65},{65,1},{2,66},{66,2},{3,67},{67,3},{4,68},{68... | collective-permute-start | bytes 16515080 | tf_op jit(solution)/shard_map/ppermute | solution.py:18
  367.1 5.0 copy-start.1
  372.1 11.1 %copy-start.2 = (f32[384,512]{1,0:T(8,128)}, f32[384,512]{1,0:T(8,128)S(1)}, u32[]{:S(2)}) copy-start(f32[384,512]{1,0:T(8,128)S(1)} %fusion.8) | copy-start | bytes 2359300
  383.0 9.9 %collective-permute-start.3 = (bf16[384,3584]{1,0:T(8,128)(2,1)}, bf16[384,3584]{1,0:T(8,128)(2,1)}, u32[]{:S(2)}, u32[]{:S(2)}) collective-permute-start(bf16[384,3584]{1,0:T(8,128)(2,1)} %convolution_convert_fusion.1), channel_id=1, source_target_pairs={{0,64},{64,0},{1,65},{65,1},{2,66},{66,2},{3,67},{67,3},{4,68},{68... | collective-permute-start | bytes 8257544 | tf_op jit(solution)/shard_map/ppermute | solution.py:18
  399.8 7.1 %copy-start.3 = (f32[384,512]{1,0:T(8,128)S(1)}, f32[384,512]{1,0:T(8,128)}, u32[]{:S(2)}) copy-start(f32[384,512]{1,0:T(8,128)} %copy-done.2) | copy-start | bytes 2359300
  399.8 126.1 %all-to-all-start.1 = ((bf16[64,6,3584]{2,1,0:T(8,128)(2,1)}), bf16[64,6,3584]{2,1,0:T(8,128)(2,1)}, u32[]{:S(2)}, u32[]{:S(2)}) async-start(bf16[64,6,3584]{2,1,0:T(8,128)(2,1)} %reshape.67), calls=%async_computation.1 | async-start | bytes 7340032 | tf_op jit(solution)/shard_map/all_to_all | solution.py:97
  433.3 86.2 %collective-permute-start.4 = (bf16[256,3584]{1,0:T(8,128)(2,1)S(1)}, bf16[256,3584]{1,0:T(8,128)(2,1)S(1)}, u32[]{:S(2)}, u32[]{:S(2)}) collective-permute-start(bf16[256,3584]{1,0:T(8,128)(2,1)S(1)} %select_convert_fusion), channel_id=1, source_target_pairs={{0,128},{128,0},{1,129},{129,1},{2,130},{130,2},{3,131},{131,3},{4... | collective-permute-start | bytes 5505032 | tf_op jit(solution)/shard_map/ppermute | solution.py:94
Sparse Core Ops, SparseCore 0:
  197.7 157.4 all-gather.1
  393.1 112.0 reduce-scatter.1
